TPU v7x, 256 devices: a whole 4x4x8 slice. The times are simulated.
256 devices in a mesh: dp: 8 (over z), section: 2 (over core), round: 16 (over x, y).
Axes of the slice: x: 4, y: 4, z: 8, core: 2. Of those that a mesh axis runs over, the one named last changes fastest.
Arguments:
- syndromes: int32 [16, 840, 2048], P('dp', None, 'round'), may hold values 0 or 1
- lengths: int32 [16], P('dp'), may hold values from 512 to 2048, as said below
- flips: int32 [16, 2048], P('dp', 'round'), may hold values 0 or 1
- embed: bfloat16 [840, 512], replicated, may hold values from -0.4375 to 0.4375
- w_in: bfloat16 [2, 512, 1024], P('section'), may hold values from -0.25 to 0.25
- w_out: bfloat16 [2, 1024, 512], P('section'), may hold values from -0.1875 to 0.1875
- leak: float32 [2, 2048, 512], P('section', 'round'), may hold values from 0 to 1, as said below
- angle: float32 [2, 512], P('section'), may hold values from -3.140625 to 3.140625
- readout: bfloat16 [512], replicated, may hold values from -0.25 to 0.25
Outputs:
- grad_in: float32 [2, 512, 1024], P('section', None, ('dp', 'round'))
- grad_out: float32 [2, 1024, 512], P('section', ('dp', 'round'))
Inputs may be any that keep to these rules, and one draw needn't show every extreme that they name: A shot's measured rounds are its first lengths rounds; some shot has all 2048. `leak`: Positive.
All inputs are finite; a program needn't handle non-finite values. No bound on the sum of `syndromes` or of `flips` on one device may be relied on, other than what follows from the above.
Results may differ from a plain program's by a relative error of at most 0.013.
Values may be sent and summed in bfloat16 or wider, within the bound.
No kernel may reach another device: no remote copies, remote signals or barrier semaphores. Data moves between devices by JAX's collectives and lax.ppermute only.
A program may use at most 64 MiB of HBM per device.

v0:
```python
import functools

import jax
import jax.numpy as jnp
from jax import lax
from jax.experimental import pallas as pl
from jax.experimental.pallas import tpu as pltpu
from jax.sharding import PartitionSpec as P

MICRO = 1


def _recurrence_kernel(a_re_ref, a_im_ref, d_re_ref, d_im_ref, p_re_ref, p_im_ref, h_re_ref, h_im_ref, *, reverse):
    rounds, width = a_re_ref.shape
    shots = d_re_ref.shape[0]

    def step(i, carry):
        p_re, p_im, states = carry
        t = rounds - 1 - i if reverse else i
        row = pl.ds(t, 1)
        a_re = a_re_ref[row, :]
        a_im = a_im_ref[row, :]
        next_p_re = p_re * a_re - p_im * a_im
        next_p_im = p_re * a_im + p_im * a_re
        p_re_ref[row, :] = next_p_re
        p_im_ref[row, :] = next_p_im
        moved = []
        for b in range(shots):
            h_re, h_im = states[b]
            new_re = a_re * h_re - a_im * h_im + d_re_ref[b, row, :]
            new_im = a_im * h_re + a_re * h_im + d_im_ref[b, row, :]
            h_re_ref[b, row, :] = new_re
            h_im_ref[b, row, :] = new_im
            moved.append((new_re, new_im))
        return (next_p_re, next_p_im, tuple(moved))

    zero = jnp.zeros((1, width), jnp.float32)
    start = (jnp.ones((1, width), jnp.float32), zero, tuple((zero, zero) for _ in range(shots)))
    lax.fori_loop(0, rounds, step, start, unroll=8)


def recurrence(a_re, a_im, d_re, d_im, reverse=False):
    rounds, width = a_re.shape
    shots = d_re.shape[0]
    vmem = pl.BlockSpec(memory_space=pltpu.VMEM)
    coeff = jax.ShapeDtypeStruct((rounds, width), jnp.float32)
    state = jax.ShapeDtypeStruct((shots, rounds, width), jnp.float32)
    return pl.pallas_call(
        functools.partial(_recurrence_kernel, reverse=reverse),
        out_shape=(coeff, coeff, state, state),
        in_specs=[vmem] * 4,
        out_specs=(vmem,) * 4,
        cost_estimate=pl.CostEstimate(
            flops=8 * rounds * width * (shots + 1),
            transcendentals=0,
            bytes_accessed=4 * 4 * rounds * width * (shots + 1),
        ),
    )(a_re, a_im, d_re, d_im)


def entering(shard, axis, combine, identity, reverse):
    peers, position = (lax.axis_size(axis), lax.axis_index(axis))
    common = jnp.broadcast_shapes(*(part.shape for part in shard))
    stacked = jnp.stack([jnp.broadcast_to(part, common) for part in shard])
    everything = lax.all_gather(stacked, axis)
    state = tuple(
        jnp.broadcast_to(jnp.asarray(zero, part.dtype), common) for part, zero in zip(shard, identity)
    )
    for k in range(peers):
        at = peers - 1 - k if reverse else k
        reached = at > position if reverse else at < position
        new = combine(state, tuple(everything[at, i] for i in range(len(shard))))
        state = tuple(jnp.where(reached, a, b) for a, b in zip(new, state))
    return state


def ring_stage(x, axis, n, stride, dim):
    index = lax.axis_index(axis)
    size = lax.axis_size(axis)
    pos = (index // stride) % n

    def moved(j, step):
        at = (j // stride) % n
        return j - at * stride + ((at + step) % n) * stride

    ahead = [(j, moved(j, 1)) for j in range(size)]
    behind = [(j, moved(j, -1)) for j in range(size)]
    chunk = x.shape[dim] // n

    def take(part, c):
        return lax.dynamic_slice_in_dim(part, c * chunk, chunk, dim)

    first, second = x[0:1], x[1:2]
    acc_first = take(first, (pos - 1) % n)
    acc_second = take(second, (pos + 1) % n)
    for step in range(n - 1):
        acc_first = lax.ppermute(acc_first, axis, ahead) + take(first, (pos - step - 2) % n)
        acc_second = lax.ppermute(acc_second, axis, behind) + take(second, (pos + step + 2) % n)
    return jnp.concatenate([acc_first, acc_second], 0)


def reduce_scatter_rows(x):
    rows_round = lax.axis_size("round")
    side = int(round(rows_round ** 0.5))
    x = ring_stage(x, "dp", lax.axis_size("dp"), 1, 1)
    x = ring_stage(x, "round", rows_round // side, side, 1)
    return ring_stage(x, "round", side, 1, 1)


def passed_along(value, axis, steps):
    count = lax.axis_size(axis)
    leading, last = (max(0, -steps), min(count, count - steps))
    return lax.ppermute(value, axis, [(source, source + steps) for source in range(leading, last)])


def combine_pairs(preceding, following):
    first_real, first_imag, first_state_real, first_state_imag = preceding
    second_real, second_imag, second_state_real, second_state_imag = following
    return (
        first_real * second_real - first_imag * second_imag,
        first_real * second_imag + first_imag * second_real,
        second_real * first_state_real - second_imag * first_state_imag + second_state_real,
        second_imag * first_state_real + second_real * first_state_imag + second_state_imag,
    )


def incoming_state(summary, neutral):
    return entering(summary, "round", combine_pairs, neutral, False)


def incoming_adjoint(summary, neutral):
    return entering(summary, "round", combine_pairs, neutral, True)


def neutral_of(summary):
    return (
        jnp.ones_like(summary[0]),
        jnp.zeros_like(summary[1]),
        jnp.zeros_like(summary[2]),
        jnp.zeros_like(summary[3]),
    )


def inverse_rms(values):
    return lax.rsqrt(jnp.mean(values * values, axis=-1, keepdims=True) + 1e-06)


def forward_block(inputs, weight_in, weight_out, trans_real, trans_imag, input_gain, valid_rounds):
    feature_count = inputs.shape[-1]
    widened = inputs.astype(jnp.float32)
    normed = (widened * inverse_rms(widened)).astype(jnp.bfloat16)
    driven = jnp.einsum("brw,wk->brk", normed, weight_in, preferred_element_type=jnp.float32)
    driven = driven * valid_rounds[:, :, None]
    drive_real = driven[:, :, :feature_count] * input_gain
    drive_imag = driven[:, :, feature_count:] * input_gain
    prod_real, prod_imag, local_real, local_imag = recurrence(
        trans_real, trans_imag, drive_real, drive_imag
    )
    prod_real, prod_imag = (prod_real[None], prod_imag[None])
    summary = (prod_real[:, -1], prod_imag[:, -1], local_real[:, -1], local_imag[:, -1])
    carried = incoming_state(summary, neutral_of(summary))
    carry_real = carried[2][:, None]
    carry_imag = carried[3][:, None]
    state_real = local_real + prod_real * carry_real - prod_imag * carry_imag
    state_imag = local_imag + prod_real * carry_imag + prod_imag * carry_real
    hidden = jnp.concatenate([state_real, state_imag], axis=-1).astype(jnp.bfloat16)
    mixed = jnp.einsum("brk,kw->brw", hidden, weight_out, preferred_element_type=jnp.float32)
    outputs = (widened + mixed).astype(jnp.bfloat16)
    return (outputs, normed, hidden)


def backward_block(
    inputs,
    normed,
    hidden,
    upstream,
    weight_in,
    weight_out,
    trans_real,
    trans_imag,
    input_gain,
    valid_rounds,
):
    feature_count = inputs.shape[-1]
    upstream_low = upstream.astype(jnp.bfloat16)
    grad_out = jnp.einsum("brk,brw->kw", hidden, upstream_low, preferred_element_type=jnp.float32)
    state_grad = jnp.einsum(
        "brw,kw->brk", upstream_low, weight_out, preferred_element_type=jnp.float32
    )
    error_real = state_grad[:, :, :feature_count]
    error_imag = state_grad[:, :, feature_count:]
    back_real = trans_real[None]
    back_imag = -trans_imag[None]
    pushed_real = back_real * error_real - back_imag * error_imag
    pushed_imag = back_real * error_imag + back_imag * error_real
    suffix_real, suffix_imag, local_real, local_imag = recurrence(
        back_real[0], back_imag[0], pushed_real, pushed_imag, reverse=True
    )
    suffix_real, suffix_imag = (suffix_real[None], suffix_imag[None])
    summary = (suffix_real[:, 0], suffix_imag[:, 0], local_real[:, 0], local_imag[:, 0])
    carried = incoming_adjoint(summary, neutral_of(summary))
    carry_real = carried[2][:, None]
    carry_imag = carried[3][:, None]
    passed_real = local_real + suffix_real * carry_real - suffix_imag * carry_imag
    passed_imag = local_imag + suffix_real * carry_imag + suffix_imag * carry_real
    next_real = jnp.concatenate([passed_real[:, 1:], carry_real], axis=1)
    next_imag = jnp.concatenate([passed_imag[:, 1:], carry_imag], axis=1)
    adjoint_real = error_real + next_real
    adjoint_imag = error_imag + next_imag
    drive_grad = (
        jnp.concatenate([adjoint_real * input_gain, adjoint_imag * input_gain], axis=-1)
        * valid_rounds[:, :, None]
    ).astype(jnp.bfloat16)
    grad_in = jnp.einsum("brk,brw->kw", drive_grad, normed, preferred_element_type=jnp.float32)
    normed_grad = jnp.einsum(
        "brk,wk->brw", drive_grad, weight_in, preferred_element_type=jnp.float32
    )
    widened = inputs.astype(jnp.float32)
    inv_scale = inverse_rms(widened)
    input_grad = upstream + inv_scale * (
        normed_grad
        - widened * inv_scale * inv_scale * jnp.mean(normed_grad * widened, axis=-1, keepdims=True)
    )
    return (grad_in, grad_out, input_grad)


def body(syndromes, lengths, flips, embed, w_in, w_out, leak, angle, readout):
    shots_here = syndromes.shape[0]
    rounds_here = syndromes.shape[2]
    feature_count = embed.shape[1]
    micro_shots = shots_here // MICRO
    shot_total = shots_here * lax.axis_size("dp")
    section_index = lax.axis_index("section")
    first_section = section_index == 0
    positions = lax.axis_index("round") * rounds_here + jnp.arange(rounds_here, dtype=jnp.int32)
    valid_all = (positions[None, :] < lengths[:, None]).astype(jnp.float32)
    weight_in = w_in[0]
    weight_out = w_out[0]
    forget = leak[0]
    decay_factor = jnp.exp(-forget)
    trans_real = decay_factor * jnp.cos(angle[0])[None, :]
    trans_imag = decay_factor * jnp.sin(angle[0])[None, :]
    input_gain = jnp.sqrt(-jnp.expm1(-2.0 * forget))
    readout_wide = readout.astype(jnp.float32)
    received = jnp.zeros((micro_shots, rounds_here, feature_count), jnp.bfloat16)
    saved_ticks = []
    loss_grads = []
    for tick_index in range(MICRO + 1):
        own_index = min(tick_index, MICRO - 1)
        syndrome_bits = syndromes[own_index * micro_shots : (own_index + 1) * micro_shots].astype(
            jnp.bfloat16
        )
        embedded = jnp.einsum(
            "bsr,sw->brw", syndrome_bits, embed, preferred_element_type=jnp.float32
        ).astype(jnp.bfloat16)
        inputs = jnp.where(first_section, embedded, received)
        micro_index = jnp.clip(tick_index - section_index, 0, MICRO - 1)
        valid_rounds = lax.dynamic_slice_in_dim(
            valid_all, micro_index * micro_shots, micro_shots, 0
        )
        outputs, normed, hidden = forward_block(
            inputs, weight_in, weight_out, trans_real, trans_imag, input_gain, valid_rounds
        )
        saved_ticks.append((inputs, normed, hidden, valid_rounds))
        if tick_index >= 1:
            logits = jnp.einsum("brw,w->br", outputs, readout, preferred_element_type=jnp.float32)
            targets = flips[(tick_index - 1) * micro_shots : tick_index * micro_shots].astype(
                jnp.float32
            )
            scaled = (jax.nn.sigmoid(logits) - targets) * valid_rounds / shot_total
            loss_grads.append(scaled[:, :, None] * readout_wide)
        if tick_index < MICRO:
            received = passed_along(outputs, "section", 1)
    grad_in_sum = jnp.zeros((2 * feature_count, feature_count), jnp.float32)
    grad_out_sum = jnp.zeros((2 * feature_count, feature_count), jnp.float32)
    arriving = jnp.zeros((micro_shots, rounds_here, feature_count), jnp.bfloat16)
    for tick_index in range(MICRO + 1):
        later_saved = saved_ticks[min(tick_index + 1, MICRO)]
        earlier = saved_ticks[max(tick_index - 1, 0)]
        picked = tuple(
            (jnp.where(first_section, lower, higher) for higher, lower in zip(later_saved, earlier))
        )
        own_grad = (
            loss_grads[tick_index]
            if tick_index < MICRO
            else jnp.zeros((micro_shots, rounds_here, feature_count), jnp.float32)
        )
        upstream = jnp.where(first_section, arriving.astype(jnp.float32), own_grad)
        grad_in_part, grad_out_part, input_grad = backward_block(
            picked[0],
            picked[1],
            picked[2],
            upstream,
            weight_in,
            weight_out,
            trans_real,
            trans_imag,
            input_gain,
            picked[3],
        )
        grad_in_sum = grad_in_sum + grad_in_part
        grad_out_sum = grad_out_sum + grad_out_part
        if tick_index < MICRO:
            arriving = passed_along(input_grad.astype(jnp.bfloat16), "section", -1)
    reduced = reduce_scatter_rows(jnp.stack([grad_in_sum, grad_out_sum]))
    return (jnp.swapaxes(reduced[0:1], 1, 2), reduced[1:2])


def solution(mesh):
    return jax.shard_map(
        body,
        mesh=mesh,
        in_specs=(
            P("dp", None, "round"),
            P("dp"),
            P("dp", "round"),
            P(),
            P("section", None, None),
            P("section", None, None),
            P("section", "round", None),
            P("section", None),
            P(),
        ),
        out_specs=(P("section", None, ("dp", "round")), P("section", ("dp", "round"), None)),
        check_vma=False,
    )
```

profile of v0, /device:TPU:8, one launch (start us, length us, event | category | flops | bytes accessed | tf_op | source)
XLA Modules:
  0.0 262.7 jit_solution(13818605666924622161)
XLA Ops:
  8.1 3.3 %shard_map.104 = (f32[128,512]{1,0:T(8,128)}, f32[128,512]{1,0:T(8,128)}, f32[2,128,512]{2,1,0:T(8,128)}, f32[2,128,512]{2,1,0:T(8,128)}) custom-call(f32[128,512]{1,0:T(8,128)} %get-tuple-element.207.a_re_ref, f32[128,512]{1,0:T(8,128)} %get-tuple-element.206.a_im_ref, f32[2,128,512]{2,1,0:T(8,128)} %get-tuple-element.190.d_re_ref, ...), custom_call_target="tpu_custom_call" | custom-call | flops 1572864 | bytes 3145728 | tf_op jit(solution)/shard_map/pallas_call | solution.py:48
  13.7 23.7 %all-gather = f32[64,2,512]{2,1,0:T(2,128)S(1)} all-gather(f32[4,2,512]{2,1,0:T(2,128)S(1)} %copy.30), channel_id=2, replica_groups=mesh['dp'=8,'section'=2,'round'=16] {'round'}, dimensions={0}, use_global_device_ids=true | all-gather | bytes 278528 | tf_op jit(solution)/shard_map/all_gather | solution.py:65
  45.6 3.2 %shard_map.105 = (f32[128,512]{1,0:T(8,128)}, f32[128,512]{1,0:T(8,128)}, f32[2,128,512]{2,1,0:T(8,128)}, f32[2,128,512]{2,1,0:T(8,128)}) custom-call(f32[128,512]{1,0:T(8,128)} %get-tuple-element.207.a_re_ref, f32[128,512]{1,0:T(8,128)} %get-tuple-element.206.a_im_ref, f32[2,128,512]{2,1,0:T(8,128)} %get-tuple-element.188.d_re_ref, ...), custom_call_target="tpu_custom_call" | custom-call | flops 1572864 | bytes 3145728 | tf_op jit(solution)/shard_map/pallas_call | solution.py:48
  51.8 22.2 %all-gather.1 = f32[64,2,512]{2,1,0:T(2,128)S(1)} all-gather(f32[4,2,512]{2,1,0:T(2,128)S(1)} %copy.31), channel_id=3, replica_groups=mesh['dp'=8,'section'=2,'round'=16] {'round'}, dimensions={0}, use_global_device_ids=true | all-gather | bytes 278528 | tf_op jit(solution)/shard_map/all_gather | solution.py:65
  81.2 3.2 %shard_map.106 = (f32[128,512]{1,0:T(8,128)}, f32[128,512]{1,0:T(8,128)}, f32[2,128,512]{2,1,0:T(8,128)}, f32[2,128,512]{2,1,0:T(8,128)}) custom-call(f32[128,512]{1,0:T(8,128)} %get-tuple-element.207.a_re_ref, f32[128,512]{1,0:T(8,128)} %copy-done.3, f32[2,128,512]{2,1,0:T(8,128)} %get-tuple-element.182.d_re_ref, f32[2,128,512]{2,1,0:T(8,128)} %get-tuple-element.181.d_im_ref), custom_call_target="tpu_custom_call" | custom-call | flops 1572864 | bytes 3145728 | tf_op jit(solution)/shard_map/pallas_call | solution.py:48
  89.5 22.5 %all-gather.2 = f32[64,2,512]{2,1,0:T(2,128)S(1)} all-gather(f32[4,2,512]{2,1,0:T(2,128)S(1)} %copy.32), channel_id=4, replica_groups=mesh['dp'=8,'section'=2,'round'=16] {'round'}, dimensions={0}, use_global_device_ids=true | all-gather | bytes 278528 | tf_op jit(solution)/shard_map/all_gather | solution.py:65
  121.2 3.2 %shard_map.107 = (f32[128,512]{1,0:T(8,128)}, f32[128,512]{1,0:T(8,128)}, f32[2,128,512]{2,1,0:T(8,128)}, f32[2,128,512]{2,1,0:T(8,128)}) custom-call(f32[128,512]{1,0:T(8,128)} %get-tuple-element.207.a_re_ref, f32[128,512]{1,0:T(8,128)} %copy-done.3, f32[2,128,512]{2,1,0:T(8,128)} %get-tuple-element.180.d_re_ref, f32[2,128,512]{2,1,0:T(8,128)} %get-tuple-element.179.d_im_ref), custom_call_target="tpu_custom_call" | custom-call | flops 1572864 | bytes 3145728 | tf_op jit(solution)/shard_map/pallas_call | solution.py:48
  127.5 22.2 %all-gather.3 = f32[64,2,512]{2,1,0:T(2,128)S(1)} all-gather(f32[4,2,512]{2,1,0:T(2,128)S(1)} %copy.36), channel_id=5, replica_groups=mesh['dp'=8,'section'=2,'round'=16] {'round'}, dimensions={0}, use_global_device_ids=true | all-gather | bytes 278528 | tf_op jit(solution)/shard_map/all_gather | solution.py:65
  158.8 4.9 %collective-permute-start.15 = (f32[1,128,512]{2,1,0:T(8,128)S(1)}, f32[1,128,512]{2,1,0:T(8,128)}, u32[]{:S(2)}, u32[]{:S(2)}) collective-permute-start(f32[1,128,512]{2,1,0:T(8,128)S(1)} %dynamic-slice_bitcast_fusion), channel_id=1, source_target_pairs={{0,224},{32,0},{64,32},{96,64},{128,96},{160,128},{192,160},{224,1... | collective-permute-start | bytes 786440 | tf_op jit(solution)/shard_map/ppermute | solution.py:98
  169.0 3.9 %collective-permute-start.16 = (f32[1,128,512]{2,1,0:T(8,128)S(1)}, f32[1,128,512]{2,1,0:T(8,128)}, u32[]{:S(2)}, u32[]{:S(2)}) collective-permute-start(f32[1,128,512]{2,1,0:T(8,128)S(1)} %bitcast_add_fusion.8), channel_id=1, source_target_pairs={{0,224},{32,0},{64,32},{96,64},{128,96},{160,128},{192,160},{224,1... | collective-permute-start | bytes 786440 | tf_op jit(solution)/shard_map/ppermute | solution.py:98
  179.2 3.9 %collective-permute-start.17 = (f32[1,128,512]{2,1,0:T(8,128)S(1)}, f32[1,128,512]{2,1,0:T(8,128)}, u32[]{:S(2)}, u32[]{:S(2)}) collective-permute-start(f32[1,128,512]{2,1,0:T(8,128)S(1)} %bitcast_add_fusion.7), channel_id=1, source_target_pairs={{0,224},{32,0},{64,32},{96,64},{128,96},{160,128},{192,160},{224,1... | collective-permute-start | bytes 786440 | tf_op jit(solution)/shard_map/ppermute | solution.py:98
  183.1 3.5 %collective-permute-done.4 = f32[1,128,512]{2,1,0:T(8,128)} collective-permute-done((f32[1,128,512]{2,1,0:T(8,128)}, f32[1,128,512]{2,1,0:T(8,128)}, u32[]{:S(2)}, u32[]{:S(2)}) %collective-permute-start.4) | collective-permute-done | bytes 262176 | tf_op jit(solution)/shard_map/ppermute | solution.py:97
  190.6 3.9 %collective-permute-start.18 = (f32[1,128,512]{2,1,0:T(8,128)S(1)}, f32[1,128,512]{2,1,0:T(8,128)}, u32[]{:S(2)}, u32[]{:S(2)}) collective-permute-start(f32[1,128,512]{2,1,0:T(8,128)S(1)} %bitcast_add_fusion.6), channel_id=1, source_target_pairs={{0,224},{32,0},{64,32},{96,64},{128,96},{160,128},{192,160},{224,1... | collective-permute-start | bytes 786440 | tf_op jit(solution)/shard_map/ppermute | solution.py:98
  194.5 4.3 %collective-permute-done.5 = f32[1,128,512]{2,1,0:T(8,128)} collective-permute-done((f32[1,128,512]{2,1,0:T(8,128)}, f32[1,128,512]{2,1,0:T(8,128)}, u32[]{:S(2)}, u32[]{:S(2)}) %collective-permute-start.5) | collective-permute-done | bytes 262176 | tf_op jit(solution)/shard_map/ppermute | solution.py:97
  201.6 3.7 %collective-permute-start.19 = (f32[1,128,512]{2,1,0:T(8,128)S(1)}, f32[1,128,512]{2,1,0:T(8,128)}, u32[]{:S(2)}, u32[]{:S(2)}) collective-permute-start(f32[1,128,512]{2,1,0:T(8,128)S(1)} %bitcast_add_fusion.5), channel_id=1, source_target_pairs={{0,224},{32,0},{64,32},{96,64},{128,96},{160,128},{192,160},{224,1... | collective-permute-start | bytes 786440 | tf_op jit(solution)/shard_map/ppermute | solution.py:98
  205.3 4.9 %collective-permute-done.6 = f32[1,128,512]{2,1,0:T(8,128)} collective-permute-done((f32[1,128,512]{2,1,0:T(8,128)}, f32[1,128,512]{2,1,0:T(8,128)}, u32[]{:S(2)}, u32[]{:S(2)}) %collective-permute-start.6) | collective-permute-done | bytes 262176 | tf_op jit(solution)/shard_map/ppermute | solution.py:97
  212.9 3.3 %collective-permute-start.20 = (f32[1,128,512]{2,1,0:T(8,128)S(1)}, f32[1,128,512]{2,1,0:T(8,128)}, u32[]{:S(2)}, u32[]{:S(2)}) collective-permute-start(f32[1,128,512]{2,1,0:T(8,128)S(1)} %bitcast_add_fusion.4), channel_id=1, source_target_pairs={{0,224},{32,0},{64,32},{96,64},{128,96},{160,128},{192,160},{224,1... | collective-permute-start | bytes 786440 | tf_op jit(solution)/shard_map/ppermute | solution.py:98
  216.2 4.4 %collective-permute-done.7 = f32[1,128,512]{2,1,0:T(8,128)} collective-permute-done((f32[1,128,512]{2,1,0:T(8,128)}, f32[1,128,512]{2,1,0:T(8,128)}, u32[]{:S(2)}, u32[]{:S(2)}) %collective-permute-start.7) | collective-permute-done | bytes 262176 | tf_op jit(solution)/shard_map/ppermute | solution.py:97
  223.4 3.3 %collective-permute-start.21 = (f32[1,128,512]{2,1,0:T(8,128)S(1)}, f32[1,128,512]{2,1,0:T(8,128)S(1)}, u32[]{:S(2)}, u32[]{:S(2)}) collective-permute-start(f32[1,128,512]{2,1,0:T(8,128)S(1)} %bitcast_add_fusion.3), channel_id=1, source_target_pairs={{0,224},{32,0},{64,32},{96,64},{128,96},{160,128},{192,160},{224,1... | collective-permute-start | bytes 786440 | tf_op jit(solution)/shard_map/ppermute | solution.py:98
  226.7 3.5 %collective-permute-done.8 = f32[1,128,512]{2,1,0:T(8,128)} collective-permute-done((f32[1,128,512]{2,1,0:T(8,128)}, f32[1,128,512]{2,1,0:T(8,128)}, u32[]{:S(2)}, u32[]{:S(2)}) %collective-permute-start.8) | collective-permute-done | bytes 262176 | tf_op jit(solution)/shard_map/ppermute | solution.py:97
  232.9 3.0 %collective-permute-start.22 = (f32[1,32,512]{2,1,0:T(8,128)S(1)}, f32[1,32,512]{2,1,0:T(8,128)S(1)}, u32[]{:S(2)}, u32[]{:S(2)}) collective-permute-start(f32[1,32,512]{2,1,0:T(8,128)S(1)} %constant_dynamic-slice_fusion.1), channel_id=1, source_target_pairs={{0,12},{1,13},{2,14},{3,15},{4,0},{5,1},{6,2},{7,3},{8,4},{9,5},{1... | collective-permute-start | bytes 196616 | tf_op jit(solution)/shard_map/ppermute | solution.py:98
  237.8 3.6 %collective-permute-start.23 = (f32[1,32,512]{2,1,0:T(8,128)S(1)}, f32[1,32,512]{2,1,0:T(8,128)S(1)}, u32[]{:S(2)}, u32[]{:S(2)}) collective-permute-start(f32[1,32,512]{2,1,0:T(8,128)S(1)} %dynamic-slice_add_fusion.2), channel_id=1, source_target_pairs={{0,12},{1,13},{2,14},{3,15},{4,0},{5,1},{6,2},{7,3},{8,4},{9,5},{1... | collective-permute-start | bytes 196616 | tf_op jit(solution)/shard_map/ppermute | solution.py:98
  243.4 3.6 %collective-permute-start.24 = (f32[1,32,512]{2,1,0:T(8,128)S(1)}, f32[1,32,512]{2,1,0:T(8,128)S(1)}, u32[]{:S(2)}, u32[]{:S(2)}) collective-permute-start(f32[1,32,512]{2,1,0:T(8,128)S(1)} %dynamic-slice_add_fusion.1), channel_id=1, source_target_pairs={{0,12},{1,13},{2,14},{3,15},{4,0},{5,1},{6,2},{7,3},{8,4},{9,5},{1... | collective-permute-start | bytes 196616 | tf_op jit(solution)/shard_map/ppermute | solution.py:98
  257.0 2.9 %collective-permute-start.27 = (f32[1,8,512]{2,1,0:T(8,128)S(1)}, f32[1,8,512]{2,1,0:T(8,128)S(1)}, u32[]{:S(2)}, u32[]{:S(2)}) collective-permute-start(f32[1,8,512]{2,1,0:T(8,128)S(1)} %dynamic-slice_add_fusion.7), channel_id=1, source_target_pairs={{0,3},{1,0},{2,1},{3,2},{4,7},{5,4},{6,5},{7,6},{8,11},{9,8},{10,9... | collective-permute-start | bytes 49160 | tf_op jit(solution)/shard_map/ppermute | solution.py:98
  (263 shorter events, 96.8 us)
Async XLA Ops:
  154.8 10.8 %collective-permute-start.2 = (f32[1,128,512]{2,1,0:T(8,128)S(1)}, f32[1,128,512]{2,1,0:T(8,128)S(1)}, u32[]{:S(2)}, u32[]{:S(2)}) collective-permute-start(f32[1,128,512]{2,1,0:T(8,128)S(1)} %dynamic-slice_bitcast_fusion.1), channel_id=1, source_target_pairs={{0,32},{32,64},{64,96},{96,128},{128,160},{160,192},{192,224},{224... | collective-permute-start | bytes 786440 | tf_op jit(solution)/shard_map/ppermute | solution.py:97
  158.8 9.1 %collective-permute-start.15 = (f32[1,128,512]{2,1,0:T(8,128)S(1)}, f32[1,128,512]{2,1,0:T(8,128)}, u32[]{:S(2)}, u32[]{:S(2)}) collective-permute-start(f32[1,128,512]{2,1,0:T(8,128)S(1)} %dynamic-slice_bitcast_fusion), channel_id=1, source_target_pairs={{0,224},{32,0},{64,32},{96,64},{128,96},{160,128},{192,160},{224,1... | collective-permute-start | bytes 786440 | tf_op jit(solution)/shard_map/ppermute | solution.py:98
  166.3 8.9 %collective-permute-start.3 = (f32[1,128,512]{2,1,0:T(8,128)}, f32[1,128,512]{2,1,0:T(8,128)}, u32[]{:S(2)}, u32[]{:S(2)}) collective-permute-start(f32[1,128,512]{2,1,0:T(8,128)} %bitcast_add_fusion.15), channel_id=1, source_target_pairs={{0,32},{32,64},{64,96},{96,128},{128,160},{160,192},{192,224},{224... | collective-permute-start | bytes 786440 | tf_op jit(solution)/shard_map/ppermute | solution.py:97
  169.0 9.2 %collective-permute-start.16 = (f32[1,128,512]{2,1,0:T(8,128)S(1)}, f32[1,128,512]{2,1,0:T(8,128)}, u32[]{:S(2)}, u32[]{:S(2)}) collective-permute-start(f32[1,128,512]{2,1,0:T(8,128)S(1)} %bitcast_add_fusion.8), channel_id=1, source_target_pairs={{0,224},{32,0},{64,32},{96,64},{128,96},{160,128},{192,160},{224,1... | collective-permute-start | bytes 786440 | tf_op jit(solution)/shard_map/ppermute | solution.py:98
  176.9 9.7 %collective-permute-start.4 = (f32[1,128,512]{2,1,0:T(8,128)}, f32[1,128,512]{2,1,0:T(8,128)}, u32[]{:S(2)}, u32[]{:S(2)}) collective-permute-start(f32[1,128,512]{2,1,0:T(8,128)} %bitcast_add_fusion.14), channel_id=1, source_target_pairs={{0,32},{32,64},{64,96},{96,128},{128,160},{160,192},{192,224},{224... | collective-permute-start | bytes 786440 | tf_op jit(solution)/shard_map/ppermute | solution.py:97
  179.2 10.3 %collective-permute-start.17 = (f32[1,128,512]{2,1,0:T(8,128)S(1)}, f32[1,128,512]{2,1,0:T(8,128)}, u32[]{:S(2)}, u32[]{:S(2)}) collective-permute-start(f32[1,128,512]{2,1,0:T(8,128)S(1)} %bitcast_add_fusion.7), channel_id=1, source_target_pairs={{0,224},{32,0},{64,32},{96,64},{128,96},{160,128},{192,160},{224,1... | collective-permute-start | bytes 786440 | tf_op jit(solution)/shard_map/ppermute | solution.py:98
  188.3 10.5 %collective-permute-start.5 = (f32[1,128,512]{2,1,0:T(8,128)}, f32[1,128,512]{2,1,0:T(8,128)}, u32[]{:S(2)}, u32[]{:S(2)}) collective-permute-start(f32[1,128,512]{2,1,0:T(8,128)} %bitcast_add_fusion.13), channel_id=1, source_target_pairs={{0,32},{32,64},{64,96},{96,128},{128,160},{160,192},{192,224},{224... | collective-permute-start | bytes 786440 | tf_op jit(solution)/shard_map/ppermute | solution.py:97
  190.6 9.9 %collective-permute-start.18 = (f32[1,128,512]{2,1,0:T(8,128)S(1)}, f32[1,128,512]{2,1,0:T(8,128)}, u32[]{:S(2)}, u32[]{:S(2)}) collective-permute-start(f32[1,128,512]{2,1,0:T(8,128)S(1)} %bitcast_add_fusion.6), channel_id=1, source_target_pairs={{0,224},{32,0},{64,32},{96,64},{128,96},{160,128},{192,160},{224,1... | collective-permute-start | bytes 786440 | tf_op jit(solution)/shard_map/ppermute | solution.py:98
  200.5 9.7 %collective-permute-start.6 = (f32[1,128,512]{2,1,0:T(8,128)}, f32[1,128,512]{2,1,0:T(8,128)}, u32[]{:S(2)}, u32[]{:S(2)}) collective-permute-start(f32[1,128,512]{2,1,0:T(8,128)} %bitcast_add_fusion.12), channel_id=1, source_target_pairs={{0,32},{32,64},{64,96},{96,128},{128,160},{160,192},{192,224},{224... | collective-permute-start | bytes 786440 | tf_op jit(solution)/shard_map/ppermute | solution.py:97
  201.6 10.3 %collective-permute-start.19 = (f32[1,128,512]{2,1,0:T(8,128)S(1)}, f32[1,128,512]{2,1,0:T(8,128)}, u32[]{:S(2)}, u32[]{:S(2)}) collective-permute-start(f32[1,128,512]{2,1,0:T(8,128)S(1)} %bitcast_add_fusion.5), channel_id=1, source_target_pairs={{0,224},{32,0},{64,32},{96,64},{128,96},{160,128},{192,160},{224,1... | collective-permute-start | bytes 786440 | tf_op jit(solution)/shard_map/ppermute | solution.py:98
  211.8 8.8 %collective-permute-start.7 = (f32[1,128,512]{2,1,0:T(8,128)}, f32[1,128,512]{2,1,0:T(8,128)}, u32[]{:S(2)}, u32[]{:S(2)}) collective-permute-start(f32[1,128,512]{2,1,0:T(8,128)} %bitcast_add_fusion.11), channel_id=1, source_target_pairs={{0,32},{32,64},{64,96},{96,128},{128,160},{160,192},{192,224},{224... | collective-permute-start | bytes 786440 | tf_op jit(solution)/shard_map/ppermute | solution.py:97
  212.9 9.4 %collective-permute-start.20 = (f32[1,128,512]{2,1,0:T(8,128)S(1)}, f32[1,128,512]{2,1,0:T(8,128)}, u32[]{:S(2)}, u32[]{:S(2)}) collective-permute-start(f32[1,128,512]{2,1,0:T(8,128)S(1)} %bitcast_add_fusion.4), channel_id=1, source_target_pairs={{0,224},{32,0},{64,32},{96,64},{128,96},{160,128},{192,160},{224,1... | collective-permute-start | bytes 786440 | tf_op jit(solution)/shard_map/ppermute | solution.py:98
  222.3 7.9 %collective-permute-start.8 = (f32[1,128,512]{2,1,0:T(8,128)}, f32[1,128,512]{2,1,0:T(8,128)}, u32[]{:S(2)}, u32[]{:S(2)}) collective-permute-start(f32[1,128,512]{2,1,0:T(8,128)} %bitcast_add_fusion.10), channel_id=1, source_target_pairs={{0,32},{32,64},{64,96},{96,128},{128,160},{160,192},{192,224},{224... | collective-permute-start | bytes 786440 | tf_op jit(solution)/shard_map/ppermute | solution.py:97
  223.4 8.4 %collective-permute-start.21 = (f32[1,128,512]{2,1,0:T(8,128)S(1)}, f32[1,128,512]{2,1,0:T(8,128)S(1)}, u32[]{:S(2)}, u32[]{:S(2)}) collective-permute-start(f32[1,128,512]{2,1,0:T(8,128)S(1)} %bitcast_add_fusion.3), channel_id=1, source_target_pairs={{0,224},{32,0},{64,32},{96,64},{128,96},{160,128},{192,160},{224,1... | collective-permute-start | bytes 786440 | tf_op jit(solution)/shard_map/ppermute | solution.py:98
  231.3 5.8 %collective-permute-start.9 = (f32[1,32,512]{2,1,0:T(8,128)S(1)}, f32[1,32,512]{2,1,0:T(8,128)S(1)}, u32[]{:S(2)}, u32[]{:S(2)}) collective-permute-start(f32[1,32,512]{2,1,0:T(8,128)S(1)} %constant_dynamic-slice_fusion.3), channel_id=1, source_target_pairs={{0,4},{1,5},{2,6},{3,7},{4,8},{5,9},{6,10},{7,11},{8,12},{9,13},{1... | collective-permute-start | bytes 196616 | tf_op jit(solution)/shard_map/ppermute | solution.py:97
  232.9 4.9 %collective-permute-start.22 = (f32[1,32,512]{2,1,0:T(8,128)S(1)}, f32[1,32,512]{2,1,0:T(8,128)S(1)}, u32[]{:S(2)}, u32[]{:S(2)}) collective-permute-start(f32[1,32,512]{2,1,0:T(8,128)S(1)} %constant_dynamic-slice_fusion.1), channel_id=1, source_target_pairs={{0,12},{1,13},{2,14},{3,15},{4,0},{5,1},{6,2},{7,3},{8,4},{9,5},{1... | collective-permute-start | bytes 196616 | tf_op jit(solution)/shard_map/ppermute | solution.py:98
  237.0 5.6 %collective-permute-start.10 = (f32[1,32,512]{2,1,0:T(8,128)S(1)}, f32[1,32,512]{2,1,0:T(8,128)S(1)}, u32[]{:S(2)}, u32[]{:S(2)}) collective-permute-start(f32[1,32,512]{2,1,0:T(8,128)S(1)} %dynamic-slice_add_fusion.5), channel_id=1, source_target_pairs={{0,4},{1,5},{2,6},{3,7},{4,8},{5,9},{6,10},{7,11},{8,12},{9,13},{1... | collective-permute-start | bytes 196616 | tf_op jit(solution)/shard_map/ppermute | solution.py:97
  237.8 5.6 %collective-permute-start.23 = (f32[1,32,512]{2,1,0:T(8,128)S(1)}, f32[1,32,512]{2,1,0:T(8,128)S(1)}, u32[]{:S(2)}, u32[]{:S(2)}) collective-permute-start(f32[1,32,512]{2,1,0:T(8,128)S(1)} %dynamic-slice_add_fusion.2), channel_id=1, source_target_pairs={{0,12},{1,13},{2,14},{3,15},{4,0},{5,1},{6,2},{7,3},{8,4},{9,5},{1... | collective-permute-start | bytes 196616 | tf_op jit(solution)/shard_map/ppermute | solution.py:98
  242.6 5.6 %collective-permute-start.11 = (f32[1,32,512]{2,1,0:T(8,128)S(1)}, f32[1,32,512]{2,1,0:T(8,128)S(1)}, u32[]{:S(2)}, u32[]{:S(2)}) collective-permute-start(f32[1,32,512]{2,1,0:T(8,128)S(1)} %dynamic-slice_add_fusion.4), channel_id=1, source_target_pairs={{0,4},{1,5},{2,6},{3,7},{4,8},{5,9},{6,10},{7,11},{8,12},{9,13},{1... | collective-permute-start | bytes 196616 | tf_op jit(solution)/shard_map/ppermute | solution.py:97
  243.4 6.0 %collective-permute-start.24 = (f32[1,32,512]{2,1,0:T(8,128)S(1)}, f32[1,32,512]{2,1,0:T(8,128)S(1)}, u32[]{:S(2)}, u32[]{:S(2)}) collective-permute-start(f32[1,32,512]{2,1,0:T(8,128)S(1)} %dynamic-slice_add_fusion.1), channel_id=1, source_target_pairs={{0,12},{1,13},{2,14},{3,15},{4,0},{5,1},{6,2},{7,3},{8,4},{9,5},{1... | collective-permute-start | bytes 196616 | tf_op jit(solution)/shard_map/ppermute | solution.py:98
  249.4 3.8 %collective-permute-start.25 = (f32[1,8,512]{2,1,0:T(8,128)S(1)}, f32[1,8,512]{2,1,0:T(8,128)S(1)}, u32[]{:S(2)}, u32[]{:S(2)}) collective-permute-start(f32[1,8,512]{2,1,0:T(8,128)S(1)} %constant_dynamic-slice_fusion), channel_id=1, source_target_pairs={{0,3},{1,0},{2,1},{3,2},{4,7},{5,4},{6,5},{7,6},{8,11},{9,8},{10,9... | collective-permute-start | bytes 49160 | tf_op jit(solution)/shard_map/ppermute | solution.py:98
  252.0 4.5 %collective-permute-start.13 = (f32[1,8,512]{2,1,0:T(8,128)S(1)}, f32[1,8,512]{2,1,0:T(8,128)S(1)}, u32[]{:S(2)}, u32[]{:S(2)}) collective-permute-start(f32[1,8,512]{2,1,0:T(8,128)S(1)} %dynamic-slice_add_fusion.10), channel_id=1, source_target_pairs={{0,1},{1,2},{2,3},{3,0},{4,5},{5,6},{6,7},{7,4},{8,9},{9,10},{10,1... | collective-permute-start | bytes 49160 | tf_op jit(solution)/shard_map/ppermute | solution.py:97
  256.6 4.9 %collective-permute-start.14 = (f32[1,8,512]{2,1,0:T(8,128)S(1)}, f32[1,8,512]{2,1,0:T(8,128)S(1)}, u32[]{:S(2)}, u32[]{:S(2)}) collective-permute-start(f32[1,8,512]{2,1,0:T(8,128)S(1)} %dynamic-slice_add_fusion.9), channel_id=1, source_target_pairs={{0,1},{1,2},{2,3},{3,0},{4,5},{5,6},{6,7},{7,4},{8,9},{9,10},{10,1... | collective-permute-start | bytes 49160 | tf_op jit(solution)/shard_map/ppermute | solution.py:97
  257.0 5.2 %collective-permute-start.27 = (f32[1,8,512]{2,1,0:T(8,128)S(1)}, f32[1,8,512]{2,1,0:T(8,128)S(1)}, u32[]{:S(2)}, u32[]{:S(2)}) collective-permute-start(f32[1,8,512]{2,1,0:T(8,128)S(1)} %dynamic-slice_add_fusion.7), channel_id=1, source_target_pairs={{0,3},{1,0},{2,1},{3,2},{4,7},{5,4},{6,5},{7,6},{8,11},{9,8},{10,9... | collective-permute-start | bytes 49160 | tf_op jit(solution)/shard_map/ppermute | solution.py:98
  (34 other events, 378.5 us)
where the time goes:
time: 267 us; the launch traced here: 263 us
  blocking collectives  90.6 us (34%)
  starting transfers between devices  52.1 us (20%)
  waiting for transfers between devices  39.5 us (15%)
  other arithmetic  33.2 us (12%)
  local copies, waits for them, and re-layouts  19.6 us (7%)
  matrix products  13.1 us (5%)
  Pallas kernels  12.9 us (5%)
    all_gather x4, blocking collectives, entering(): everything = lax.all_gather(stacked, axis)  90.6 us
    ppermute x13, starting transfers between devices, ring_stage(): lax.ppermute(acc_second, axis, behind) + take(second, (pos + step + 2) % n)  43.1 us
    ppermute x13, waiting for transfers between devices, ring_stage(): lax.ppermute(acc_first, axis, ahead) + take(first, (pos - step - 2) % n)  32.8 us
    pallas_call x4, Pallas kernels, recurrence(): pl.pallas_call(functools.partial(_recurrence_kernel, reverse=reverse), ou...  12.9 us
    add x12, other arithmetic, ring_stage(): lax.ppermute(acc_first, axis, ahead) + take(first, (pos - step - 2) % n)  10.2 us
    add x13, other arithmetic, ring_stage(): lax.ppermute(acc_second, axis, behind) + take(second, (pos + step + 2) % n)  8.03 us
    ppermute x13, waiting for transfers between devices, ring_stage(): lax.ppermute(acc_second, axis, behind) + take(second, (pos + step + 2) % n)  5.74 us
    ppermute x13, starting transfers between devices, ring_stage(): lax.ppermute(acc_first, axis, ahead) + take(first, (pos - step - 2) % n)  5.51 us
  transfers between devices with their start and end apart: 28, of which 22 were waited for; matrix products, arithmetic and copies ran while one was open for 8% of the time, Pallas kernels for 0%

commit v1 on v0

--- a/solution.py
+++ b/solution.py
@@ -61,16 +61,30 @@
 def entering(shard, axis, combine, identity, reverse):
     peers, position = (lax.axis_size(axis), lax.axis_index(axis))
     common = jnp.broadcast_shapes(*(part.shape for part in shard))
-    stacked = jnp.stack([jnp.broadcast_to(part, common) for part in shard])
-    everything = lax.all_gather(stacked, axis)
-    state = tuple(
+    own = tuple(jnp.broadcast_to(part, common) for part in shard)
+    neutral = tuple(
         jnp.broadcast_to(jnp.asarray(zero, part.dtype), common) for part, zero in zip(shard, identity)
     )
-    for k in range(peers):
-        at = peers - 1 - k if reverse else k
-        reached = at > position if reverse else at < position
-        new = combine(state, tuple(everything[at, i] for i in range(len(shard))))
-        state = tuple(jnp.where(reached, a, b) for a, b in zip(new, state))
+
+    def fetch(value, distance):
+        if reverse:
+            pairs = [(j, j - distance) for j in range(distance, peers)]
+            present = position + distance < peers
+        else:
+            pairs = [(j, j + distance) for j in range(peers - distance)]
+            present = position >= distance
+        got = lax.ppermute(jnp.stack(value), axis, pairs)
+        return tuple(jnp.where(present, got[i], neutral[i]) for i in range(len(value)))
+
+    if peers == 1:
+        return neutral
+    state = fetch(own, 1)
+    if peers > 2:
+        state = combine(fetch(own, 2), state)
+    window = 2
+    while window < peers:
+        state = combine(fetch(state, window), state)
+        window *= 2
     return state
 
 

time: 267 us -> 291 us (1.090)
  blocking collectives: 90.6 us -> 0 us
  starting transfers between devices: 52.1 us -> 124 us
  waiting for transfers between devices: 39.5 us -> 85.7 us
  local copies, waits for them, and re-layouts: 19.6 us -> 14.5 us
    all_gather x4 -> x0, blocking collectives: 90.6 us -> none  [entering(): everything = lax.all_gather(stacked, axis)]
    ppermute x0 -> x20, starting transfers between devices: none -> 67.2 us  [fetch(): got = lax.ppermute(jnp.stack(value), axis, pairs)]
    ppermute x0 -> x20, waiting for transfers between devices: none -> 44 us  [fetch(): got = lax.ppermute(jnp.stack(value), axis, pairs)]
    ppermute x13, starting transfers between devices: 5.51 us -> 11 us  [ring_stage(): lax.ppermute(acc_first, axis, ahead) + take(first, (pos - step - 2) % n)]
    unnamed x61 -> x59, local copies, waits for them, and re-layouts: 3.4 us -> 0.27 us
    add x13, other arithmetic: 8.03 us -> 10.9 us  [ring_stage(): lax.ppermute(acc_second, axis, behind) + take(second, (pos + step + 2) % n)]
  transfers between devices with their start and end apart: 28 -> 48, of which waited for: 22 -> 40; matrix products, arithmetic and copies ran while one was open for 8% -> 9% of each run, Pallas kernels for 0% -> 0%
where the time goes in v1:
time: 291 us; the launch traced here: 286 us
  starting transfers between devices  124 us (43%)
  waiting for transfers between devices  85.7 us (29%)
  other arithmetic  34.1 us (12%)
  local copies, waits for them, and re-layouts  14.5 us (5%)
  matrix products  13.2 us (5%)
  Pallas kernels  12.9 us (4%)
    ppermute x20, starting transfers between devices, fetch(): got = lax.ppermute(jnp.stack(value), axis, pairs)  67.2 us
    ppermute x20, waiting for transfers between devices, fetch(): got = lax.ppermute(jnp.stack(value), axis, pairs)  44 us
    ppermute x13, starting transfers between devices, ring_stage(): lax.ppermute(acc_second, axis, behind) + take(second, (pos + step + 2) % n)  43.2 us
    ppermute x13, waiting for transfers between devices, ring_stage(): lax.ppermute(acc_first, axis, ahead) + take(first, (pos - step - 2) % n)  30.1 us
    pallas_call x4, Pallas kernels, recurrence(): pl.pallas_call(functools.partial(_recurrence_kernel, reverse=reverse), ou...  12.9 us
    ppermute x13, starting transfers between devices, ring_stage(): lax.ppermute(acc_first, axis, ahead) + take(first, (pos - step - 2) % n)  11 us
    add x13, other arithmetic, ring_stage(): lax.ppermute(acc_second, axis, behind) + take(second, (pos + step + 2) % n)  10.9 us
    ppermute x13, waiting for transfers between devices, ring_stage(): lax.ppermute(acc_second, axis, behind) + take(second, (pos + step + 2) % n)  8.37 us
  transfers between devices with their start and end apart: 48, of which 40 were waited for; matrix products, arithmetic and copies ran while one was open for 9% of the time, Pallas kernels for 0%

profile of v1, /device:TPU:8, one launch (start us, length us, event | category | flops | bytes accessed | tf_op | source)
XLA Modules:
  0.0 286.4 jit_solution(16302450112029178742)
XLA Ops:
  17.1 3.8 %collective-permute-start = (f32[4,2,512]{2,0,1:T(4,128)S(1)}, f32[4,2,512]{2,0,1:T(4,128)S(1)}, u32[]{:S(2)}, u32[]{:S(2)}) collective-permute-start(f32[4,2,512]{2,0,1:T(4,128)S(1)} %pad_maximum_fusion.5), channel_id=1, source_target_pairs={{0,2},{1,3},{2,4},{3,5},{4,6},{5,7},{6,8},{7,9},{8,10},{9,11},{10,... | collective-permute-start | bytes 49160 | tf_op jit(solution)/shard_map/ppermute | solution.py:76
  22.4 5.7 %collective-permute-start.2 = (f32[4,2,512]{2,0,1:T(4,128)S(1)}, f32[4,2,512]{2,0,1:T(4,128)S(1)}, u32[]{:S(2)}, u32[]{:S(2)}) collective-permute-start(f32[4,2,512]{2,0,1:T(4,128)S(1)} %pad_maximum_fusion.6), channel_id=1, source_target_pairs={{0,2},{1,3},{2,4},{3,5},{4,6},{5,7},{6,8},{7,9},{8,10},{9,11},{10,... | collective-permute-start | bytes 49160 | tf_op jit(solution)/shard_map/ppermute | solution.py:76
  29.6 7.1 %collective-permute-start.3 = (f32[4,2,512]{2,0,1:T(4,128)S(1)}, f32[4,2,512]{2,0,1:T(4,128)S(1)}, u32[]{:S(2)}, u32[]{:S(2)}) collective-permute-start(f32[4,2,512]{2,0,1:T(4,128)S(1)} %pad_maximum_fusion.7), channel_id=1, source_target_pairs={{0,4},{1,5},{2,6},{3,7},{4,8},{5,9},{6,10},{7,11},{8,12},{9,13},{1... | collective-permute-start | bytes 49160 | tf_op jit(solution)/shard_map/ppermute | solution.py:76
  38.2 5.7 %collective-permute-start.4 = (f32[4,2,512]{2,0,1:T(4,128)S(1)}, f32[4,2,512]{2,0,1:T(4,128)S(1)}, u32[]{:S(2)}, u32[]{:S(2)}) collective-permute-start(f32[4,2,512]{2,0,1:T(4,128)S(1)} %pad_maximum_fusion.8), channel_id=1, source_target_pairs={{0,8},{1,9},{2,10},{3,11},{4,12},{5,13},{6,14},{7,15},{16,24},{17,... | collective-permute-start | bytes 49160 | tf_op jit(solution)/shard_map/ppermute | solution.py:76
  59.9 4.4 %collective-permute-start.6 = (f32[4,2,512]{2,0,1:T(4,128)S(1)}, f32[4,2,512]{2,0,1:T(4,128)S(1)}, u32[]{:S(2)}, u32[]{:S(2)}) collective-permute-start(f32[4,2,512]{2,0,1:T(4,128)S(1)} %pad_maximum_fusion.9), channel_id=1, source_target_pairs={{0,2},{1,3},{2,4},{3,5},{4,6},{5,7},{6,8},{7,9},{8,10},{9,11},{10,... | collective-permute-start | bytes 49160 | tf_op jit(solution)/shard_map/ppermute | solution.py:76
  65.9 5.7 %collective-permute-start.8 = (f32[4,2,512]{2,0,1:T(4,128)S(1)}, f32[4,2,512]{2,0,1:T(4,128)S(1)}, u32[]{:S(2)}, u32[]{:S(2)}) collective-permute-start(f32[4,2,512]{2,0,1:T(4,128)S(1)} %pad_maximum_fusion.10), channel_id=1, source_target_pairs={{0,2},{1,3},{2,4},{3,5},{4,6},{5,7},{6,8},{7,9},{8,10},{9,11},{10,... | collective-permute-start | bytes 49160 | tf_op jit(solution)/shard_map/ppermute | solution.py:76
  73.1 6.0 %collective-permute-start.9 = (f32[4,2,512]{2,0,1:T(4,128)S(1)}, f32[4,2,512]{2,0,1:T(4,128)S(1)}, u32[]{:S(2)}, u32[]{:S(2)}) collective-permute-start(f32[4,2,512]{2,0,1:T(4,128)S(1)} %pad_maximum_fusion.11), channel_id=1, source_target_pairs={{0,4},{1,5},{2,6},{3,7},{4,8},{5,9},{6,10},{7,11},{8,12},{9,13},{1... | collective-permute-start | bytes 49160 | tf_op jit(solution)/shard_map/ppermute | solution.py:76
  80.5 7.0 %collective-permute-start.10 = (f32[4,2,512]{2,0,1:T(4,128)S(1)}, f32[4,2,512]{2,0,1:T(4,128)S(1)}, u32[]{:S(2)}, u32[]{:S(2)}) collective-permute-start(f32[4,2,512]{2,0,1:T(4,128)S(1)} %pad_maximum_fusion.12), channel_id=1, source_target_pairs={{0,8},{1,9},{2,10},{3,11},{4,12},{5,13},{6,14},{7,15},{16,24},{17,... | collective-permute-start | bytes 49160 | tf_op jit(solution)/shard_map/ppermute | solution.py:76
  102.1 3.9 %collective-permute-start.12 = (f32[4,2,512]{2,0,1:T(4,128)S(1)}, f32[4,2,512]{2,0,1:T(4,128)S(1)}, u32[]{:S(2)}, u32[]{:S(2)}) collective-permute-start(f32[4,2,512]{2,0,1:T(4,128)S(1)} %pad_maximum_fusion.13), channel_id=1, source_target_pairs={{1,0},{2,1},{3,2},{4,3},{5,4},{6,5},{7,6},{8,7},{9,8},{10,9},{11,1... | collective-permute-start | bytes 49160 | tf_op jit(solution)/shard_map/ppermute | solution.py:76
  107.9 5.3 %collective-permute-done.11 = f32[4,2,512]{2,0,1:T(4,128)S(1)} collective-permute-done((f32[4,2,512]{2,0,1:T(4,128)S(1)}, f32[4,2,512]{2,0,1:T(4,128)S(1)}, u32[]{:S(2)}, u32[]{:S(2)}) %collective-permute-start.11) | collective-permute-done | bytes 16416 | tf_op jit(solution)/shard_map/ppermute | solution.py:76
  114.6 5.8 %collective-permute-done.13 = f32[4,2,512]{2,0,1:T(4,128)S(1)} collective-permute-done((f32[4,2,512]{2,0,1:T(4,128)S(1)}, f32[4,2,512]{2,0,1:T(4,128)S(1)}, u32[]{:S(2)}, u32[]{:S(2)}) %collective-permute-start.13) | collective-permute-done | bytes 16416 | tf_op jit(solution)/shard_map/ppermute | solution.py:76
  121.8 4.3 %collective-permute-done.14 = f32[4,2,512]{2,0,1:T(4,128)S(1)} collective-permute-done((f32[4,2,512]{2,0,1:T(4,128)S(1)}, f32[4,2,512]{2,0,1:T(4,128)S(1)}, u32[]{:S(2)}, u32[]{:S(2)}) %collective-permute-start.14) | collective-permute-done | bytes 16416 | tf_op jit(solution)/shard_map/ppermute | solution.py:76
  129.5 3.9 %collective-permute-done.15 = f32[4,2,512]{2,0,1:T(4,128)S(1)} collective-permute-done((f32[4,2,512]{2,0,1:T(4,128)S(1)}, f32[4,2,512]{2,0,1:T(4,128)S(1)}, u32[]{:S(2)}, u32[]{:S(2)}) %collective-permute-start.15) | collective-permute-done | bytes 16416 | tf_op jit(solution)/shard_map/ppermute | solution.py:76
  160.0 5.8 %collective-permute-done.19 = f32[4,2,512]{2,0,1:T(4,128)S(1)} collective-permute-done((f32[4,2,512]{2,0,1:T(4,128)S(1)}, f32[4,2,512]{2,0,1:T(4,128)S(1)}, u32[]{:S(2)}, u32[]{:S(2)}) %collective-permute-start.19) | collective-permute-done | bytes 16416 | tf_op jit(solution)/shard_map/ppermute | solution.py:76
  173.2 5.9 %collective-permute-start.35 = (f32[1,128,512]{2,1,0:T(8,128)S(1)}, f32[1,128,512]{2,1,0:T(8,128)S(1)}, u32[]{:S(2)}, u32[]{:S(2)}) collective-permute-start(f32[1,128,512]{2,1,0:T(8,128)S(1)} %dynamic-slice_bitcast_fusion), channel_id=1, source_target_pairs={{0,224},{32,0},{64,32},{96,64},{128,96},{160,128},{192,160},{224,1... | collective-permute-start | bytes 786440 | tf_op jit(solution)/shard_map/ppermute | solution.py:112
  183.8 4.3 %collective-permute-start.36 = (f32[1,128,512]{2,1,0:T(8,128)}, f32[1,128,512]{2,1,0:T(8,128)}, u32[]{:S(2)}, u32[]{:S(2)}) collective-permute-start(f32[1,128,512]{2,1,0:T(8,128)} %bitcast_add_fusion.8), channel_id=1, source_target_pairs={{0,224},{32,0},{64,32},{96,64},{128,96},{160,128},{192,160},{224,1... | collective-permute-start | bytes 786440 | tf_op jit(solution)/shard_map/ppermute | solution.py:112
  194.0 3.7 %collective-permute-start.37 = (f32[1,128,512]{2,1,0:T(8,128)}, f32[1,128,512]{2,1,0:T(8,128)}, u32[]{:S(2)}, u32[]{:S(2)}) collective-permute-start(f32[1,128,512]{2,1,0:T(8,128)} %bitcast_add_fusion.7), channel_id=1, source_target_pairs={{0,224},{32,0},{64,32},{96,64},{128,96},{160,128},{192,160},{224,1... | collective-permute-start | bytes 786440 | tf_op jit(solution)/shard_map/ppermute | solution.py:112
  197.7 4.1 %collective-permute-done.23 = f32[1,128,512]{2,1,0:T(8,128)} collective-permute-done((f32[1,128,512]{2,1,0:T(8,128)S(1)}, f32[1,128,512]{2,1,0:T(8,128)}, u32[]{:S(2)}, u32[]{:S(2)}) %collective-permute-start.23) | collective-permute-done | bytes 262176 | tf_op jit(solution)/shard_map/ppermute | solution.py:111
  208.2 5.2 %collective-permute-done.24 = f32[1,128,512]{2,1,0:T(8,128)} collective-permute-done((f32[1,128,512]{2,1,0:T(8,128)S(1)}, f32[1,128,512]{2,1,0:T(8,128)}, u32[]{:S(2)}, u32[]{:S(2)}) %collective-permute-start.24) | collective-permute-done | bytes 262176 | tf_op jit(solution)/shard_map/ppermute | solution.py:111
  219.9 4.3 %collective-permute-done.25 = f32[1,128,512]{2,1,0:T(8,128)} collective-permute-done((f32[1,128,512]{2,1,0:T(8,128)S(1)}, f32[1,128,512]{2,1,0:T(8,128)}, u32[]{:S(2)}, u32[]{:S(2)}) %collective-permute-start.25) | collective-permute-done | bytes 262176 | tf_op jit(solution)/shard_map/ppermute | solution.py:111
  228.2 3.7 %collective-permute-start.40 = (f32[1,128,512]{2,1,0:T(8,128)}, f32[1,128,512]{2,1,0:T(8,128)}, u32[]{:S(2)}, u32[]{:S(2)}) collective-permute-start(f32[1,128,512]{2,1,0:T(8,128)} %bitcast_add_fusion.4), channel_id=1, source_target_pairs={{0,224},{32,0},{64,32},{96,64},{128,96},{160,128},{192,160},{224,1... | collective-permute-start | bytes 786440 | tf_op jit(solution)/shard_map/ppermute | solution.py:112
  239.3 3.7 %collective-permute-start.41 = (f32[1,128,512]{2,1,0:T(8,128)}, f32[1,128,512]{2,1,0:T(8,128)}, u32[]{:S(2)}, u32[]{:S(2)}) collective-permute-start(f32[1,128,512]{2,1,0:T(8,128)} %bitcast_add_fusion.3), channel_id=1, source_target_pairs={{0,224},{32,0},{64,32},{96,64},{128,96},{160,128},{192,160},{224,1... | collective-permute-start | bytes 786440 | tf_op jit(solution)/shard_map/ppermute | solution.py:112
  248.2 4.5 %collective-permute-start.42 = (f32[1,32,512]{2,1,0:T(8,128)S(1)}, f32[1,32,512]{2,1,0:T(8,128)S(1)}, u32[]{:S(2)}, u32[]{:S(2)}) collective-permute-start(f32[1,32,512]{2,1,0:T(8,128)S(1)} %constant_dynamic-slice_fusion.1), channel_id=1, source_target_pairs={{0,12},{1,13},{2,14},{3,15},{4,0},{5,1},{6,2},{7,3},{8,4},{9,5},{1... | collective-permute-start | bytes 196616 | tf_op jit(solution)/shard_map/ppermute | solution.py:112
  270.9 3.7 %collective-permute-start.32 = (f32[1,8,512]{2,1,0:T(8,128)S(1)}, f32[1,8,512]{2,1,0:T(8,128)S(1)}, u32[]{:S(2)}, u32[]{:S(2)}) collective-permute-start(f32[1,8,512]{2,1,0:T(8,128)S(1)} %constant_dynamic-slice_fusion.2), channel_id=1, source_target_pairs={{0,1},{1,2},{2,3},{3,0},{4,5},{5,6},{6,7},{7,4},{8,9},{9,10},{10,1... | collective-permute-start | bytes 49160 | tf_op jit(solution)/shard_map/ppermute | solution.py:111
  (265 shorter events, 166.9 us)
Async XLA Ops:
  13.6 7.3 %collective-permute-start.1 = (f32[4,2,512]{2,0,1:T(4,128)S(1)}, f32[4,2,512]{2,0,1:T(4,128)S(1)}, u32[]{:S(2)}, u32[]{:S(2)}) collective-permute-start(f32[4,2,512]{2,0,1:T(4,128)S(1)} %pad_maximum_fusion.5), channel_id=1, source_target_pairs={{0,1},{1,2},{2,3},{3,4},{4,5},{5,6},{6,7},{7,8},{8,9},{9,10},{10,1... | collective-permute-start | bytes 49160 | tf_op jit(solution)/shard_map/ppermute | solution.py:76
  22.4 7.1 %collective-permute-start.2 = (f32[4,2,512]{2,0,1:T(4,128)S(1)}, f32[4,2,512]{2,0,1:T(4,128)S(1)}, u32[]{:S(2)}, u32[]{:S(2)}) collective-permute-start(f32[4,2,512]{2,0,1:T(4,128)S(1)} %pad_maximum_fusion.6), channel_id=1, source_target_pairs={{0,2},{1,3},{2,4},{3,5},{4,6},{5,7},{6,8},{7,9},{8,10},{9,11},{10,... | collective-permute-start | bytes 49160 | tf_op jit(solution)/shard_map/ppermute | solution.py:76
  29.6 8.6 %collective-permute-start.3 = (f32[4,2,512]{2,0,1:T(4,128)S(1)}, f32[4,2,512]{2,0,1:T(4,128)S(1)}, u32[]{:S(2)}, u32[]{:S(2)}) collective-permute-start(f32[4,2,512]{2,0,1:T(4,128)S(1)} %pad_maximum_fusion.7), channel_id=1, source_target_pairs={{0,4},{1,5},{2,6},{3,7},{4,8},{5,9},{6,10},{7,11},{8,12},{9,13},{1... | collective-permute-start | bytes 49160 | tf_op jit(solution)/shard_map/ppermute | solution.py:76
  38.2 7.2 %collective-permute-start.4 = (f32[4,2,512]{2,0,1:T(4,128)S(1)}, f32[4,2,512]{2,0,1:T(4,128)S(1)}, u32[]{:S(2)}, u32[]{:S(2)}) collective-permute-start(f32[4,2,512]{2,0,1:T(4,128)S(1)} %pad_maximum_fusion.8), channel_id=1, source_target_pairs={{0,8},{1,9},{2,10},{3,11},{4,12},{5,13},{6,14},{7,15},{16,24},{17,... | collective-permute-start | bytes 49160 | tf_op jit(solution)/shard_map/ppermute | solution.py:76
  65.9 7.1 %collective-permute-start.8 = (f32[4,2,512]{2,0,1:T(4,128)S(1)}, f32[4,2,512]{2,0,1:T(4,128)S(1)}, u32[]{:S(2)}, u32[]{:S(2)}) collective-permute-start(f32[4,2,512]{2,0,1:T(4,128)S(1)} %pad_maximum_fusion.10), channel_id=1, source_target_pairs={{0,2},{1,3},{2,4},{3,5},{4,6},{5,7},{6,8},{7,9},{8,10},{9,11},{10,... | collective-permute-start | bytes 49160 | tf_op jit(solution)/shard_map/ppermute | solution.py:76
  73.1 7.4 %collective-permute-start.9 = (f32[4,2,512]{2,0,1:T(4,128)S(1)}, f32[4,2,512]{2,0,1:T(4,128)S(1)}, u32[]{:S(2)}, u32[]{:S(2)}) collective-permute-start(f32[4,2,512]{2,0,1:T(4,128)S(1)} %pad_maximum_fusion.11), channel_id=1, source_target_pairs={{0,4},{1,5},{2,6},{3,7},{4,8},{5,9},{6,10},{7,11},{8,12},{9,13},{1... | collective-permute-start | bytes 49160 | tf_op jit(solution)/shard_map/ppermute | solution.py:76
  80.5 8.4 %collective-permute-start.10 = (f32[4,2,512]{2,0,1:T(4,128)S(1)}, f32[4,2,512]{2,0,1:T(4,128)S(1)}, u32[]{:S(2)}, u32[]{:S(2)}) collective-permute-start(f32[4,2,512]{2,0,1:T(4,128)S(1)} %pad_maximum_fusion.12), channel_id=1, source_target_pairs={{0,8},{1,9},{2,10},{3,11},{4,12},{5,13},{6,14},{7,15},{16,24},{17,... | collective-permute-start | bytes 49160 | tf_op jit(solution)/shard_map/ppermute | solution.py:76
  158.1 7.8 %collective-permute-start.19 = (f32[4,2,512]{2,0,1:T(4,128)S(1)}, f32[4,2,512]{2,0,1:T(4,128)S(1)}, u32[]{:S(2)}, u32[]{:S(2)}) collective-permute-start(f32[4,2,512]{2,0,1:T(4,128)S(1)} %pad_maximum_fusion.18), channel_id=1, source_target_pairs={{2,0},{3,1},{4,2},{5,3},{6,4},{7,5},{8,6},{9,7},{10,8},{11,9},{12,... | collective-permute-start | bytes 49160 | tf_op jit(solution)/shard_map/ppermute | solution.py:76
  171.8 7.3 %collective-permute-start.21 = (f32[4,2,512]{2,0,1:T(4,128)S(1)}, f32[4,2,512]{2,0,1:T(4,128)S(1)}, u32[]{:S(2)}, u32[]{:S(2)}) collective-permute-start(f32[4,2,512]{2,0,1:T(4,128)S(1)} %pad_maximum_fusion.20), channel_id=1, source_target_pairs={{8,0},{9,1},{10,2},{11,3},{12,4},{13,5},{14,6},{15,7},{24,16},{25,... | collective-permute-start | bytes 49160 | tf_op jit(solution)/shard_map/ppermute | solution.py:76
  173.2 9.8 %collective-permute-start.35 = (f32[1,128,512]{2,1,0:T(8,128)S(1)}, f32[1,128,512]{2,1,0:T(8,128)S(1)}, u32[]{:S(2)}, u32[]{:S(2)}) collective-permute-start(f32[1,128,512]{2,1,0:T(8,128)S(1)} %dynamic-slice_bitcast_fusion), channel_id=1, source_target_pairs={{0,224},{32,0},{64,32},{96,64},{128,96},{160,128},{192,160},{224,1... | collective-permute-start | bytes 786440 | tf_op jit(solution)/shard_map/ppermute | solution.py:112
  180.4 10.6 %collective-permute-start.22 = (f32[1,128,512]{2,1,0:T(8,128)S(1)}, f32[1,128,512]{2,1,0:T(8,128)}, u32[]{:S(2)}, u32[]{:S(2)}) collective-permute-start(f32[1,128,512]{2,1,0:T(8,128)S(1)} %dynamic-slice_bitcast_fusion.1), channel_id=1, source_target_pairs={{0,32},{32,64},{64,96},{96,128},{128,160},{160,192},{192,224},{224... | collective-permute-start | bytes 786440 | tf_op jit(solution)/shard_map/ppermute | solution.py:111
  183.8 8.5 %collective-permute-start.36 = (f32[1,128,512]{2,1,0:T(8,128)}, f32[1,128,512]{2,1,0:T(8,128)}, u32[]{:S(2)}, u32[]{:S(2)}) collective-permute-start(f32[1,128,512]{2,1,0:T(8,128)} %bitcast_add_fusion.8), channel_id=1, source_target_pairs={{0,224},{32,0},{64,32},{96,64},{128,96},{160,128},{192,160},{224,1... | collective-permute-start | bytes 786440 | tf_op jit(solution)/shard_map/ppermute | solution.py:112
  192.0 9.7 %collective-permute-start.23 = (f32[1,128,512]{2,1,0:T(8,128)S(1)}, f32[1,128,512]{2,1,0:T(8,128)}, u32[]{:S(2)}, u32[]{:S(2)}) collective-permute-start(f32[1,128,512]{2,1,0:T(8,128)S(1)} %bitcast_add_fusion.15), channel_id=1, source_target_pairs={{0,32},{32,64},{64,96},{96,128},{128,160},{160,192},{192,224},{224... | collective-permute-start | bytes 786440 | tf_op jit(solution)/shard_map/ppermute | solution.py:111
  194.0 8.9 %collective-permute-start.37 = (f32[1,128,512]{2,1,0:T(8,128)}, f32[1,128,512]{2,1,0:T(8,128)}, u32[]{:S(2)}, u32[]{:S(2)}) collective-permute-start(f32[1,128,512]{2,1,0:T(8,128)} %bitcast_add_fusion.7), channel_id=1, source_target_pairs={{0,224},{32,0},{64,32},{96,64},{128,96},{160,128},{192,160},{224,1... | collective-permute-start | bytes 786440 | tf_op jit(solution)/shard_map/ppermute | solution.py:112
  202.8 10.6 %collective-permute-start.24 = (f32[1,128,512]{2,1,0:T(8,128)S(1)}, f32[1,128,512]{2,1,0:T(8,128)}, u32[]{:S(2)}, u32[]{:S(2)}) collective-permute-start(f32[1,128,512]{2,1,0:T(8,128)S(1)} %bitcast_add_fusion.14), channel_id=1, source_target_pairs={{0,32},{32,64},{64,96},{96,128},{128,160},{160,192},{192,224},{224... | collective-permute-start | bytes 786440 | tf_op jit(solution)/shard_map/ppermute | solution.py:111
  204.7 9.9 %collective-permute-start.38 = (f32[1,128,512]{2,1,0:T(8,128)}, f32[1,128,512]{2,1,0:T(8,128)}, u32[]{:S(2)}, u32[]{:S(2)}) collective-permute-start(f32[1,128,512]{2,1,0:T(8,128)} %bitcast_add_fusion.6), channel_id=1, source_target_pairs={{0,224},{32,0},{64,32},{96,64},{128,96},{160,128},{192,160},{224,1... | collective-permute-start | bytes 786440 | tf_op jit(solution)/shard_map/ppermute | solution.py:112
  214.5 9.7 %collective-permute-start.25 = (f32[1,128,512]{2,1,0:T(8,128)S(1)}, f32[1,128,512]{2,1,0:T(8,128)}, u32[]{:S(2)}, u32[]{:S(2)}) collective-permute-start(f32[1,128,512]{2,1,0:T(8,128)S(1)} %bitcast_add_fusion.13), channel_id=1, source_target_pairs={{0,32},{32,64},{64,96},{96,128},{128,160},{160,192},{192,224},{224... | collective-permute-start | bytes 786440 | tf_op jit(solution)/shard_map/ppermute | solution.py:111
  216.3 10.2 %collective-permute-start.39 = (f32[1,128,512]{2,1,0:T(8,128)}, f32[1,128,512]{2,1,0:T(8,128)}, u32[]{:S(2)}, u32[]{:S(2)}) collective-permute-start(f32[1,128,512]{2,1,0:T(8,128)} %bitcast_add_fusion.5), channel_id=1, source_target_pairs={{0,224},{32,0},{64,32},{96,64},{128,96},{160,128},{192,160},{224,1... | collective-permute-start | bytes 786440 | tf_op jit(solution)/shard_map/ppermute | solution.py:112
  225.2 8.8 %collective-permute-start.26 = (f32[1,128,512]{2,1,0:T(8,128)S(1)}, f32[1,128,512]{2,1,0:T(8,128)}, u32[]{:S(2)}, u32[]{:S(2)}) collective-permute-start(f32[1,128,512]{2,1,0:T(8,128)S(1)} %bitcast_add_fusion.12), channel_id=1, source_target_pairs={{0,32},{32,64},{64,96},{96,128},{128,160},{160,192},{192,224},{224... | collective-permute-start | bytes 786440 | tf_op jit(solution)/shard_map/ppermute | solution.py:111
  228.2 9.4 %collective-permute-start.40 = (f32[1,128,512]{2,1,0:T(8,128)}, f32[1,128,512]{2,1,0:T(8,128)}, u32[]{:S(2)}, u32[]{:S(2)}) collective-permute-start(f32[1,128,512]{2,1,0:T(8,128)} %bitcast_add_fusion.4), channel_id=1, source_target_pairs={{0,224},{32,0},{64,32},{96,64},{128,96},{160,128},{192,160},{224,1... | collective-permute-start | bytes 786440 | tf_op jit(solution)/shard_map/ppermute | solution.py:112
  235.1 8.0 %collective-permute-start.27 = (f32[1,128,512]{2,1,0:T(8,128)S(1)}, f32[1,128,512]{2,1,0:T(8,128)}, u32[]{:S(2)}, u32[]{:S(2)}) collective-permute-start(f32[1,128,512]{2,1,0:T(8,128)S(1)} %bitcast_add_fusion.11), channel_id=1, source_target_pairs={{0,32},{32,64},{64,96},{96,128},{128,160},{160,192},{192,224},{224... | collective-permute-start | bytes 786440 | tf_op jit(solution)/shard_map/ppermute | solution.py:111
  239.3 7.9 %collective-permute-start.41 = (f32[1,128,512]{2,1,0:T(8,128)}, f32[1,128,512]{2,1,0:T(8,128)}, u32[]{:S(2)}, u32[]{:S(2)}) collective-permute-start(f32[1,128,512]{2,1,0:T(8,128)} %bitcast_add_fusion.3), channel_id=1, source_target_pairs={{0,224},{32,0},{64,32},{96,64},{128,96},{160,128},{192,160},{224,1... | collective-permute-start | bytes 786440 | tf_op jit(solution)/shard_map/ppermute | solution.py:112
  244.2 8.6 %collective-permute-start.28 = (f32[1,128,512]{2,1,0:T(8,128)S(1)}, f32[1,128,512]{2,1,0:T(8,128)S(1)}, u32[]{:S(2)}, u32[]{:S(2)}) collective-permute-start(f32[1,128,512]{2,1,0:T(8,128)S(1)} %bitcast_add_fusion.10), channel_id=1, source_target_pairs={{0,32},{32,64},{64,96},{96,128},{128,160},{160,192},{192,224},{224... | collective-permute-start | bytes 786440 | tf_op jit(solution)/shard_map/ppermute | solution.py:111
  265.8 8.8 %collective-permute-start.45 = (f32[1,8,512]{2,1,0:T(8,128)S(1)}, f32[1,8,512]{2,1,0:T(8,128)S(1)}, u32[]{:S(2)}, u32[]{:S(2)}) collective-permute-start(f32[1,8,512]{2,1,0:T(8,128)S(1)} %constant_dynamic-slice_fusion), channel_id=1, source_target_pairs={{0,3},{1,0},{2,1},{3,2},{4,7},{5,4},{6,5},{7,6},{8,11},{9,8},{10,9... | collective-permute-start | bytes 49160 | tf_op jit(solution)/shard_map/ppermute | solution.py:112
  (49 other events, 488.2 us)

commit v2 on v0

--- a/solution.py
+++ b/solution.py
@@ -100,11 +100,10 @@
 
 
 def reduce_scatter_rows(x):
-    rows_round = lax.axis_size("round")
-    side = int(round(rows_round ** 0.5))
+    peers = lax.axis_size("round")
     x = ring_stage(x, "dp", lax.axis_size("dp"), 1, 1)
-    x = ring_stage(x, "round", rows_round // side, side, 1)
-    return ring_stage(x, "round", side, 1, 1)
+    split = x.reshape(x.shape[0], peers, x.shape[1] // peers, x.shape[2])
+    return lax.all_to_all(split, "round", 1, 1, tiled=True).sum(axis=1)
 
 
 def passed_along(value, axis, steps):

time: 267 us -> 253 us (0.948)
  starting transfers between devices: 52.1 us -> 33.1 us
  blocking collectives: 90.6 us -> 105 us
  waiting for transfers between devices: 39.5 us -> 30.8 us
    ppermute x13 -> x7, waiting for transfers between devices: 32.8 us -> 7.12 us  [ring_stage(): lax.ppermute(acc_first, axis, ahead) + take(first, (pos - step - 2) % n)]
    ppermute x13 -> x7, waiting for transfers between devices: 5.74 us -> 22.8 us  [ring_stage(): lax.ppermute(acc_second, axis, behind) + take(second, (pos + step + 2) % n)]
    ppermute x13 -> x7, starting transfers between devices: 43.1 us -> 27 us  [ring_stage(): lax.ppermute(acc_second, axis, behind) + take(second, (pos + step + 2) % n)]
    all_to_all x0 -> x1, blocking collectives: none -> 14.4 us  [reduce_scatter_rows(): return lax.all_to_all(split, 'round', 1, 1, tiled=True).sum(axis=1)]
    add x13 -> x7, other arithmetic: 8.03 us -> 11.6 us  [ring_stage(): lax.ppermute(acc_second, axis, behind) + take(second, (pos + step + 2) % n)]
    add x12 -> x7, other arithmetic: 10.2 us -> 6.9 us  [ring_stage(): lax.ppermute(acc_first, axis, ahead) + take(first, (pos - step - 2) % n)]
    ppermute x13 -> x7, starting transfers between devices: 5.51 us -> 2.71 us  [ring_stage(): lax.ppermute(acc_first, axis, ahead) + take(first, (pos - step - 2) % n)]
  transfers between devices with their start and end apart: 28 -> 16, of which waited for: 22 -> 13; matrix products, arithmetic and copies ran while one was open for 8% -> 8% of each run, Pallas kernels for 0% -> 0%
where the time goes in v2:
time: 253 us; the launch traced here: 251 us
  blocking collectives  105 us (42%)
  other arithmetic  33.1 us (13%)
  starting transfers between devices  33.1 us (13%)
  waiting for transfers between devices  30.8 us (12%)
  local copies, waits for them, and re-layouts  21 us (8%)
  matrix products  13.1 us (5%)
  Pallas kernels  12.9 us (5%)
    all_gather x4, blocking collectives, entering(): everything = lax.all_gather(stacked, axis)  90.6 us
    ppermute x7, starting transfers between devices, ring_stage(): lax.ppermute(acc_second, axis, behind) + take(second, (pos + step + 2) % n)  27 us
    ppermute x7, waiting for transfers between devices, ring_stage(): lax.ppermute(acc_second, axis, behind) + take(second, (pos + step + 2) % n)  22.8 us
    all_to_all x1, blocking collectives, reduce_scatter_rows(): return lax.all_to_all(split, 'round', 1, 1, tiled=True).sum(axis=1)  14.4 us
    pallas_call x4, Pallas kernels, recurrence(): pl.pallas_call(functools.partial(_recurrence_kernel, reverse=reverse), ou...  12.9 us
    add x7, other arithmetic, ring_stage(): lax.ppermute(acc_second, axis, behind) + take(second, (pos + step + 2) % n)  11.6 us
    ppermute x7, waiting for transfers between devices, ring_stage(): lax.ppermute(acc_first, axis, ahead) + take(first, (pos - step - 2) % n)  7.12 us
    add x7, other arithmetic, ring_stage(): lax.ppermute(acc_first, axis, ahead) + take(first, (pos - step - 2) % n)  6.9 us
  transfers between devices with their start and end apart: 16, of which 13 were waited for; matrix products, arithmetic and copies ran while one was open for 8% of the time, Pallas kernels for 0%

profile of v2, /device:TPU:8, one launch (start us, length us, event | category | flops | bytes accessed | tf_op | source)
XLA Modules:
  0.0 250.6 jit_solution(9852745063225781921)
XLA Ops:
  8.1 3.3 %shard_map.104 = (f32[128,512]{1,0:T(8,128)}, f32[128,512]{1,0:T(8,128)}, f32[2,128,512]{2,1,0:T(8,128)}, f32[2,128,512]{2,1,0:T(8,128)}) custom-call(f32[128,512]{1,0:T(8,128)} %get-tuple-element.207.a_re_ref, f32[128,512]{1,0:T(8,128)} %get-tuple-element.206.a_im_ref, f32[2,128,512]{2,1,0:T(8,128)} %get-tuple-element.190.d_re_ref, ...), custom_call_target="tpu_custom_call" | custom-call | flops 1572864 | bytes 3145728 | tf_op jit(solution)/shard_map/pallas_call | solution.py:48
  13.7 23.7 %all-gather = f32[64,2,512]{2,1,0:T(2,128)S(1)} all-gather(f32[4,2,512]{2,1,0:T(2,128)S(1)} %copy.49), channel_id=2, replica_groups=mesh['dp'=8,'section'=2,'round'=16] {'round'}, dimensions={0}, use_global_device_ids=true | all-gather | bytes 278528 | tf_op jit(solution)/shard_map/all_gather | solution.py:65
  45.6 3.2 %shard_map.105 = (f32[128,512]{1,0:T(8,128)}, f32[128,512]{1,0:T(8,128)}, f32[2,128,512]{2,1,0:T(8,128)}, f32[2,128,512]{2,1,0:T(8,128)}) custom-call(f32[128,512]{1,0:T(8,128)} %get-tuple-element.207.a_re_ref, f32[128,512]{1,0:T(8,128)} %get-tuple-element.206.a_im_ref, f32[2,128,512]{2,1,0:T(8,128)} %get-tuple-element.188.d_re_ref, ...), custom_call_target="tpu_custom_call" | custom-call | flops 1572864 | bytes 3145728 | tf_op jit(solution)/shard_map/pallas_call | solution.py:48
  51.9 22.2 %all-gather.1 = f32[64,2,512]{2,1,0:T(2,128)S(1)} all-gather(f32[4,2,512]{2,1,0:T(2,128)S(1)} %copy.50), channel_id=3, replica_groups=mesh['dp'=8,'section'=2,'round'=16] {'round'}, dimensions={0}, use_global_device_ids=true | all-gather | bytes 278528 | tf_op jit(solution)/shard_map/all_gather | solution.py:65
  74.4 2.4 subtract_convert_fusion
  81.3 3.2 %shard_map.106 = (f32[128,512]{1,0:T(8,128)}, f32[128,512]{1,0:T(8,128)}, f32[2,128,512]{2,1,0:T(8,128)}, f32[2,128,512]{2,1,0:T(8,128)}) custom-call(f32[128,512]{1,0:T(8,128)} %get-tuple-element.207.a_re_ref, f32[128,512]{1,0:T(8,128)} %copy-done.3, f32[2,128,512]{2,1,0:T(8,128)} %get-tuple-element.182.d_re_ref, f32[2,128,512]{2,1,0:T(8,128)} %get-tuple-element.181.d_im_ref), custom_call_target="tpu_custom_call" | custom-call | flops 1572864 | bytes 3145728 | tf_op jit(solution)/shard_map/pallas_call | solution.py:48
  89.5 22.5 %all-gather.2 = f32[64,2,512]{2,1,0:T(2,128)S(1)} all-gather(f32[4,2,512]{2,1,0:T(2,128)S(1)} %copy.51), channel_id=4, replica_groups=mesh['dp'=8,'section'=2,'round'=16] {'round'}, dimensions={0}, use_global_device_ids=true | all-gather | bytes 278528 | tf_op jit(solution)/shard_map/all_gather | solution.py:65
  121.2 3.2 %shard_map.107 = (f32[128,512]{1,0:T(8,128)}, f32[128,512]{1,0:T(8,128)}, f32[2,128,512]{2,1,0:T(8,128)}, f32[2,128,512]{2,1,0:T(8,128)}) custom-call(f32[128,512]{1,0:T(8,128)} %get-tuple-element.207.a_re_ref, f32[128,512]{1,0:T(8,128)} %copy-done.3, f32[2,128,512]{2,1,0:T(8,128)} %get-tuple-element.180.d_re_ref, f32[2,128,512]{2,1,0:T(8,128)} %get-tuple-element.179.d_im_ref), custom_call_target="tpu_custom_call" | custom-call | flops 1572864 | bytes 3145728 | tf_op jit(solution)/shard_map/pallas_call | solution.py:48
  127.5 22.2 %all-gather.3 = f32[64,2,512]{2,1,0:T(2,128)S(1)} all-gather(f32[4,2,512]{2,1,0:T(2,128)S(1)} %copy.55), channel_id=5, replica_groups=mesh['dp'=8,'section'=2,'round'=16] {'round'}, dimensions={0}, use_global_device_ids=true | all-gather | bytes 278528 | tf_op jit(solution)/shard_map/all_gather | solution.py:65
  154.8 2.2 collective-permute-start.2
  159.5 4.8 %collective-permute-start.9 = (f32[1,128,512]{2,1,0:T(8,128)}, f32[1,128,512]{2,1,0:T(8,128)}, u32[]{:S(2)}, u32[]{:S(2)}) collective-permute-start(f32[1,128,512]{2,1,0:T(8,128)} %dynamic-slice_bitcast_fusion), channel_id=1, source_target_pairs={{0,224},{32,0},{64,32},{96,64},{128,96},{160,128},{192,160},{224,1... | collective-permute-start | bytes 786440 | tf_op jit(solution)/shard_map/ppermute | solution.py:98
  170.3 3.7 %collective-permute-start.10 = (f32[1,128,512]{2,1,0:T(8,128)}, f32[1,128,512]{2,1,0:T(8,128)}, u32[]{:S(2)}, u32[]{:S(2)}) collective-permute-start(f32[1,128,512]{2,1,0:T(8,128)} %bitcast_add_fusion.8), channel_id=1, source_target_pairs={{0,224},{32,0},{64,32},{96,64},{128,96},{160,128},{192,160},{224,1... | collective-permute-start | bytes 786440 | tf_op jit(solution)/shard_map/ppermute | solution.py:98
  180.6 3.7 %collective-permute-start.11 = (f32[1,128,512]{2,1,0:T(8,128)}, f32[1,128,512]{2,1,0:T(8,128)}, u32[]{:S(2)}, u32[]{:S(2)}) collective-permute-start(f32[1,128,512]{2,1,0:T(8,128)} %bitcast_add_fusion.7), channel_id=1, source_target_pairs={{0,224},{32,0},{64,32},{96,64},{128,96},{160,128},{192,160},{224,1... | collective-permute-start | bytes 786440 | tf_op jit(solution)/shard_map/ppermute | solution.py:98
  184.3 2.5 collective-permute-done.4
  187.9 2.4 collective-permute-done.11
  192.0 3.7 %collective-permute-start.12 = (f32[1,128,512]{2,1,0:T(8,128)}, f32[1,128,512]{2,1,0:T(8,128)}, u32[]{:S(2)}, u32[]{:S(2)}) collective-permute-start(f32[1,128,512]{2,1,0:T(8,128)} %bitcast_add_fusion.6), channel_id=1, source_target_pairs={{0,224},{32,0},{64,32},{96,64},{128,96},{160,128},{192,160},{224,1... | collective-permute-start | bytes 786440 | tf_op jit(solution)/shard_map/ppermute | solution.py:98
  198.7 3.9 %collective-permute-done.12 = f32[1,128,512]{2,1,0:T(8,128)} collective-permute-done((f32[1,128,512]{2,1,0:T(8,128)}, f32[1,128,512]{2,1,0:T(8,128)}, u32[]{:S(2)}, u32[]{:S(2)}) %collective-permute-start.12) | collective-permute-done | bytes 262176 | tf_op jit(solution)/shard_map/ppermute | solution.py:98
  204.4 3.7 %collective-permute-start.13 = (f32[1,128,512]{2,1,0:T(8,128)}, f32[1,128,512]{2,1,0:T(8,128)}, u32[]{:S(2)}, u32[]{:S(2)}) collective-permute-start(f32[1,128,512]{2,1,0:T(8,128)} %bitcast_add_fusion.5), channel_id=1, source_target_pairs={{0,224},{32,0},{64,32},{96,64},{128,96},{160,128},{192,160},{224,1... | collective-permute-start | bytes 786440 | tf_op jit(solution)/shard_map/ppermute | solution.py:98
  209.1 5.0 %collective-permute-done.13 = f32[1,128,512]{2,1,0:T(8,128)} collective-permute-done((f32[1,128,512]{2,1,0:T(8,128)}, f32[1,128,512]{2,1,0:T(8,128)}, u32[]{:S(2)}, u32[]{:S(2)}) %collective-permute-start.13) | collective-permute-done | bytes 262176 | tf_op jit(solution)/shard_map/ppermute | solution.py:98
  215.9 3.7 %collective-permute-start.14 = (f32[1,128,512]{2,1,0:T(8,128)}, f32[1,128,512]{2,1,0:T(8,128)}, u32[]{:S(2)}, u32[]{:S(2)}) collective-permute-start(f32[1,128,512]{2,1,0:T(8,128)} %bitcast_add_fusion.4), channel_id=1, source_target_pairs={{0,224},{32,0},{64,32},{96,64},{128,96},{160,128},{192,160},{224,1... | collective-permute-start | bytes 786440 | tf_op jit(solution)/shard_map/ppermute | solution.py:98
  220.7 4.1 %collective-permute-done.14 = f32[1,128,512]{2,1,0:T(8,128)} collective-permute-done((f32[1,128,512]{2,1,0:T(8,128)}, f32[1,128,512]{2,1,0:T(8,128)}, u32[]{:S(2)}, u32[]{:S(2)}) %collective-permute-start.14) | collective-permute-done | bytes 262176 | tf_op jit(solution)/shard_map/ppermute | solution.py:98
  226.5 3.7 %collective-permute-start.15 = (f32[1,128,512]{2,1,0:T(8,128)}, f32[1,128,512]{2,1,0:T(8,128)}, u32[]{:S(2)}, u32[]{:S(2)}) collective-permute-start(f32[1,128,512]{2,1,0:T(8,128)} %bitcast_add_fusion.3), channel_id=1, source_target_pairs={{0,224},{32,0},{64,32},{96,64},{128,96},{160,128},{192,160},{224,1... | collective-permute-start | bytes 786440 | tf_op jit(solution)/shard_map/ppermute | solution.py:98
  231.2 3.2 %collective-permute-done.15 = f32[1,128,512]{2,1,0:T(8,128)} collective-permute-done((f32[1,128,512]{2,1,0:T(8,128)}, f32[1,128,512]{2,1,0:T(8,128)}, u32[]{:S(2)}, u32[]{:S(2)}) %collective-permute-start.15) | collective-permute-done | bytes 262176 | tf_op jit(solution)/shard_map/ppermute | solution.py:98
  235.6 14.4 %all_to_all.5 = f32[2,16,8,512]{3,2,0,1:T(8,128)S(1)} all-to-all(f32[2,16,8,512]{3,2,0,1:T(8,128)S(1)} %copy.68), channel_id=1, replica_groups=mesh['dp'=8,'section'=2,'round'=16] {'round'}, dimensions={1} | all-to-all | bytes 1048576 | tf_op jit(solution)/shard_map/all_to_all | solution.py:106
  (228 shorter events, 78.4 us)
Async XLA Ops:
  0.6 5.9 %copy-start = (bf16[1,512,1024]{2,1,0:T(8,128)(2,1)S(1)}, bf16[1,512,1024]{2,1,0:T(8,128)(2,1)}, u32[]{:S(2)}) copy-start(bf16[1,512,1024]{2,1,0:T(8,128)(2,1)} %param.13) | copy-start | bytes 3145732
  2.7 77.4 %copy-start.3 = (f32[128,512]{1,0:T(8,128)}, f32[128,512]{1,0:T(8,128)S(1)}, u32[]{:S(2)}) copy-start(f32[128,512]{1,0:T(8,128)S(1)} %get-tuple-element.204.a_im_ref) | copy-start | bytes 786436
  8.1 31.8 %copy-start.5 = (bf16[1,1024,512]{2,1,0:T(8,128)(2,1)S(1)}, bf16[1,1024,512]{2,1,0:T(8,128)(2,1)}, u32[]{:S(2)}) copy-start(bf16[1,1024,512]{2,1,0:T(8,128)(2,1)} %param.14) | copy-start | bytes 3145732
  41.0 2.8 %collective-permute-start = (bf16[2,128,512]{2,1,0:T(8,128)(2,1)}, bf16[2,128,512]{2,1,0:T(8,128)(2,1)}, u32[]{:S(2)}, u32[]{:S(2)}) collective-permute-start(bf16[2,128,512]{2,1,0:T(8,128)(2,1)} %fusion), channel_id=1, source_target_pairs={{0,16},{1,17},{2,18},{3,19},{4,20},{5,21},{6,22},{7,23},{8,24},{9,... | collective-permute-start | bytes 786440 | tf_op jit(solution)/shard_map/ppermute | solution.py:112
  44.0 69.7 %copy-start.7 = (bf16[2,128,512]{2,1,0:T(8,128)(2,1)}, bf16[2,128,512]{2,1,0:T(8,128)(2,1)S(1)}, u32[]{:S(2)}) copy-start(bf16[2,128,512]{2,1,0:T(8,128)(2,1)S(1)} %get-tuple-element.154) | copy-start | bytes 786436
  84.5 28.1 %copy-start.25 = (f32[2,128,512]{2,1,0:T(8,128)S(1)}, f32[2,128,512]{2,1,0:T(8,128)}, u32[]{:S(2)}) copy-start(f32[2,128,512]{2,1,0:T(8,128)} %get-tuple-element.26) | copy-start | bytes 1572868
  84.5 28.1 %copy-start.26 = (f32[2,128,512]{2,1,0:T(8,128)S(1)}, f32[2,128,512]{2,1,0:T(8,128)}, u32[]{:S(2)}) copy-start(f32[2,128,512]{2,1,0:T(8,128)} %get-tuple-element.29) | copy-start | bytes 1572868
  116.0 3.6 %collective-permute-start.1 = (bf16[2,128,512]{2,1,0:T(8,128)(2,1)S(1)}, bf16[2,128,512]{2,1,0:T(8,128)(2,1)S(1)}, u32[]{:S(2)}, u32[]{:S(2)}) collective-permute-start(bf16[2,128,512]{2,1,0:T(8,128)(2,1)S(1)} %fusion.28), channel_id=1, source_target_pairs={{16,0},{17,1},{18,2},{19,3},{20,4},{21,5},{22,6},{23,7},{24,8},{25... | collective-permute-start | bytes 786440 | tf_op jit(solution)/shard_map/ppermute | solution.py:112
  124.4 27.8 %copy-start.23 = (f32[2,128,512]{2,1,0:T(8,128)S(1)}, f32[2,128,512]{2,1,0:T(8,128)}, u32[]{:S(2)}) copy-start(f32[2,128,512]{2,1,0:T(8,128)} %get-tuple-element.30) | copy-start | bytes 1572868
  124.4 27.9 %copy-start.24 = (f32[2,128,512]{2,1,0:T(8,128)S(1)}, f32[2,128,512]{2,1,0:T(8,128)}, u32[]{:S(2)}) copy-start(f32[2,128,512]{2,1,0:T(8,128)} %get-tuple-element.33) | copy-start | bytes 1572868
  154.8 10.6 %collective-permute-start.2 = (f32[1,128,512]{2,1,0:T(8,128)S(1)}, f32[1,128,512]{2,1,0:T(8,128)}, u32[]{:S(2)}, u32[]{:S(2)}) collective-permute-start(f32[1,128,512]{2,1,0:T(8,128)S(1)} %dynamic-slice_bitcast_fusion.1), channel_id=1, source_target_pairs={{0,32},{32,64},{64,96},{96,128},{128,160},{160,192},{192,224},{224... | collective-permute-start | bytes 786440 | tf_op jit(solution)/shard_map/ppermute | solution.py:97
  159.5 9.0 %collective-permute-start.9 = (f32[1,128,512]{2,1,0:T(8,128)}, f32[1,128,512]{2,1,0:T(8,128)}, u32[]{:S(2)}, u32[]{:S(2)}) collective-permute-start(f32[1,128,512]{2,1,0:T(8,128)} %dynamic-slice_bitcast_fusion), channel_id=1, source_target_pairs={{0,224},{32,0},{64,32},{96,64},{128,96},{160,128},{192,160},{224,1... | collective-permute-start | bytes 786440 | tf_op jit(solution)/shard_map/ppermute | solution.py:98
  166.4 9.1 %collective-permute-start.3 = (f32[1,128,512]{2,1,0:T(8,128)S(1)}, f32[1,128,512]{2,1,0:T(8,128)}, u32[]{:S(2)}, u32[]{:S(2)}) collective-permute-start(f32[1,128,512]{2,1,0:T(8,128)S(1)} %bitcast_add_fusion.15), channel_id=1, source_target_pairs={{0,32},{32,64},{64,96},{96,128},{128,160},{160,192},{192,224},{224... | collective-permute-start | bytes 786440 | tf_op jit(solution)/shard_map/ppermute | solution.py:97
  170.3 8.5 %collective-permute-start.10 = (f32[1,128,512]{2,1,0:T(8,128)}, f32[1,128,512]{2,1,0:T(8,128)}, u32[]{:S(2)}, u32[]{:S(2)}) collective-permute-start(f32[1,128,512]{2,1,0:T(8,128)} %bitcast_add_fusion.8), channel_id=1, source_target_pairs={{0,224},{32,0},{64,32},{96,64},{128,96},{160,128},{192,160},{224,1... | collective-permute-start | bytes 786440 | tf_op jit(solution)/shard_map/ppermute | solution.py:98
  176.6 10.2 %collective-permute-start.4 = (f32[1,128,512]{2,1,0:T(8,128)S(1)}, f32[1,128,512]{2,1,0:T(8,128)}, u32[]{:S(2)}, u32[]{:S(2)}) collective-permute-start(f32[1,128,512]{2,1,0:T(8,128)S(1)} %bitcast_add_fusion.14), channel_id=1, source_target_pairs={{0,32},{32,64},{64,96},{96,128},{128,160},{160,192},{192,224},{224... | collective-permute-start | bytes 786440 | tf_op jit(solution)/shard_map/ppermute | solution.py:97
  180.6 9.6 %collective-permute-start.11 = (f32[1,128,512]{2,1,0:T(8,128)}, f32[1,128,512]{2,1,0:T(8,128)}, u32[]{:S(2)}, u32[]{:S(2)}) collective-permute-start(f32[1,128,512]{2,1,0:T(8,128)} %bitcast_add_fusion.7), channel_id=1, source_target_pairs={{0,224},{32,0},{64,32},{96,64},{128,96},{160,128},{192,160},{224,1... | collective-permute-start | bytes 786440 | tf_op jit(solution)/shard_map/ppermute | solution.py:98
  187.8 9.9 %collective-permute-start.5 = (f32[1,128,512]{2,1,0:T(8,128)S(1)}, f32[1,128,512]{2,1,0:T(8,128)}, u32[]{:S(2)}, u32[]{:S(2)}) collective-permute-start(f32[1,128,512]{2,1,0:T(8,128)S(1)} %bitcast_add_fusion.13), channel_id=1, source_target_pairs={{0,32},{32,64},{64,96},{96,128},{128,160},{160,192},{192,224},{224... | collective-permute-start | bytes 786440 | tf_op jit(solution)/shard_map/ppermute | solution.py:97
  192.0 10.6 %collective-permute-start.12 = (f32[1,128,512]{2,1,0:T(8,128)}, f32[1,128,512]{2,1,0:T(8,128)}, u32[]{:S(2)}, u32[]{:S(2)}) collective-permute-start(f32[1,128,512]{2,1,0:T(8,128)} %bitcast_add_fusion.6), channel_id=1, source_target_pairs={{0,224},{32,0},{64,32},{96,64},{128,96},{160,128},{192,160},{224,1... | collective-permute-start | bytes 786440 | tf_op jit(solution)/shard_map/ppermute | solution.py:98
  198.6 9.4 %collective-permute-start.6 = (f32[1,128,512]{2,1,0:T(8,128)S(1)}, f32[1,128,512]{2,1,0:T(8,128)}, u32[]{:S(2)}, u32[]{:S(2)}) collective-permute-start(f32[1,128,512]{2,1,0:T(8,128)S(1)} %bitcast_add_fusion.12), channel_id=1, source_target_pairs={{0,32},{32,64},{64,96},{96,128},{128,160},{160,192},{192,224},{224... | collective-permute-start | bytes 786440 | tf_op jit(solution)/shard_map/ppermute | solution.py:97
  204.4 9.8 %collective-permute-start.13 = (f32[1,128,512]{2,1,0:T(8,128)}, f32[1,128,512]{2,1,0:T(8,128)}, u32[]{:S(2)}, u32[]{:S(2)}) collective-permute-start(f32[1,128,512]{2,1,0:T(8,128)} %bitcast_add_fusion.5), channel_id=1, source_target_pairs={{0,224},{32,0},{64,32},{96,64},{128,96},{160,128},{192,160},{224,1... | collective-permute-start | bytes 786440 | tf_op jit(solution)/shard_map/ppermute | solution.py:98
  209.0 10.5 %collective-permute-start.7 = (f32[1,128,512]{2,1,0:T(8,128)S(1)}, f32[1,128,512]{2,1,0:T(8,128)}, u32[]{:S(2)}, u32[]{:S(2)}) collective-permute-start(f32[1,128,512]{2,1,0:T(8,128)S(1)} %bitcast_add_fusion.11), channel_id=1, source_target_pairs={{0,32},{32,64},{64,96},{96,128},{128,160},{160,192},{192,224},{224... | collective-permute-start | bytes 786440 | tf_op jit(solution)/shard_map/ppermute | solution.py:97
  215.9 8.9 %collective-permute-start.14 = (f32[1,128,512]{2,1,0:T(8,128)}, f32[1,128,512]{2,1,0:T(8,128)}, u32[]{:S(2)}, u32[]{:S(2)}) collective-permute-start(f32[1,128,512]{2,1,0:T(8,128)} %bitcast_add_fusion.4), channel_id=1, source_target_pairs={{0,224},{32,0},{64,32},{96,64},{128,96},{160,128},{192,160},{224,1... | collective-permute-start | bytes 786440 | tf_op jit(solution)/shard_map/ppermute | solution.py:98
  220.6 9.7 %collective-permute-start.8 = (f32[1,128,512]{2,1,0:T(8,128)S(1)}, f32[1,128,512]{2,1,0:T(8,128)}, u32[]{:S(2)}, u32[]{:S(2)}) collective-permute-start(f32[1,128,512]{2,1,0:T(8,128)S(1)} %bitcast_add_fusion.10), channel_id=1, source_target_pairs={{0,32},{32,64},{64,96},{96,128},{128,160},{160,192},{192,224},{224... | collective-permute-start | bytes 786440 | tf_op jit(solution)/shard_map/ppermute | solution.py:97
  226.5 7.9 %collective-permute-start.15 = (f32[1,128,512]{2,1,0:T(8,128)}, f32[1,128,512]{2,1,0:T(8,128)}, u32[]{:S(2)}, u32[]{:S(2)}) collective-permute-start(f32[1,128,512]{2,1,0:T(8,128)} %bitcast_add_fusion.3), channel_id=1, source_target_pairs={{0,224},{32,0},{64,32},{96,64},{128,96},{160,128},{192,160},{224,1... | collective-permute-start | bytes 786440 | tf_op jit(solution)/shard_map/ppermute | solution.py:98
  (22 other events, 70.0 us)

commit v3 on v2

--- a/solution.py
+++ b/solution.py
@@ -10,7 +10,9 @@
 MICRO = 1
 
 
-def _recurrence_kernel(a_re_ref, a_im_ref, d_re_ref, d_im_ref, p_re_ref, p_im_ref, h_re_ref, h_im_ref, *, reverse):
+def _recurrence_kernel(
+    a_re_ref, a_im_ref, d_re_ref, d_im_ref, p_re_ref, p_im_ref, h_re_ref, h_im_ref, end_ref, *, reverse
+):
     rounds, width = a_re_ref.shape
     shots = d_re_ref.shape[0]
 
@@ -36,7 +38,12 @@
 
     zero = jnp.zeros((1, width), jnp.float32)
     start = (jnp.ones((1, width), jnp.float32), zero, tuple((zero, zero) for _ in range(shots)))
-    lax.fori_loop(0, rounds, step, start, unroll=8)
+    p_re, p_im, states = lax.fori_loop(0, rounds, step, start, unroll=8)
+    for b in range(shots):
+        end_ref[0, pl.ds(b, 1), :] = p_re
+        end_ref[1, pl.ds(b, 1), :] = p_im
+        end_ref[2, pl.ds(b, 1), :] = states[b][0]
+        end_ref[3, pl.ds(b, 1), :] = states[b][1]
 
 
 def recurrence(a_re, a_im, d_re, d_im, reverse=False):
@@ -47,9 +54,9 @@
     state = jax.ShapeDtypeStruct((shots, rounds, width), jnp.float32)
     return pl.pallas_call(
         functools.partial(_recurrence_kernel, reverse=reverse),
-        out_shape=(coeff, coeff, state, state),
+        out_shape=(coeff, coeff, state, state, jax.ShapeDtypeStruct((4, shots, width), jnp.float32)),
         in_specs=[vmem] * 4,
-        out_specs=(vmem,) * 4,
+        out_specs=(vmem,) * 5,
         cost_estimate=pl.CostEstimate(
             flops=8 * rounds * width * (shots + 1),
             transcendentals=0,
@@ -74,7 +81,7 @@
     return state
 
 
-def ring_stage(x, axis, n, stride, dim):
+def ring_stage(first, second, axis, n, stride, dim):
     index = lax.axis_index(axis)
     size = lax.axis_size(axis)
     pos = (index // stride) % n
@@ -85,12 +92,11 @@
 
     ahead = [(j, moved(j, 1)) for j in range(size)]
     behind = [(j, moved(j, -1)) for j in range(size)]
-    chunk = x.shape[dim] // n
+    chunk = first.shape[dim] // n
 
     def take(part, c):
         return lax.dynamic_slice_in_dim(part, c * chunk, chunk, dim)
 
-    first, second = x[0:1], x[1:2]
     acc_first = take(first, (pos - 1) % n)
     acc_second = take(second, (pos + 1) % n)
     for step in range(n - 1):
@@ -99,9 +105,9 @@
     return jnp.concatenate([acc_first, acc_second], 0)
 
 
-def reduce_scatter_rows(x):
+def reduce_scatter_rows(first, second):
     peers = lax.axis_size("round")
-    x = ring_stage(x, "dp", lax.axis_size("dp"), 1, 1)
+    x = ring_stage(first, second, "dp", lax.axis_size("dp"), 1, 1)
     split = x.reshape(x.shape[0], peers, x.shape[1] // peers, x.shape[2])
     return lax.all_to_all(split, "round", 1, 1, tiled=True).sum(axis=1)
 
@@ -152,11 +158,11 @@
     driven = driven * valid_rounds[:, :, None]
     drive_real = driven[:, :, :feature_count] * input_gain
     drive_imag = driven[:, :, feature_count:] * input_gain
-    prod_real, prod_imag, local_real, local_imag = recurrence(
+    prod_real, prod_imag, local_real, local_imag, ends = recurrence(
         trans_real, trans_imag, drive_real, drive_imag
     )
     prod_real, prod_imag = (prod_real[None], prod_imag[None])
-    summary = (prod_real[:, -1], prod_imag[:, -1], local_real[:, -1], local_imag[:, -1])
+    summary = (ends[0], ends[1], ends[2], ends[3])
     carried = incoming_state(summary, neutral_of(summary))
     carry_real = carried[2][:, None]
     carry_imag = carried[3][:, None]
@@ -192,11 +198,11 @@
     back_imag = -trans_imag[None]
     pushed_real = back_real * error_real - back_imag * error_imag
     pushed_imag = back_real * error_imag + back_imag * error_real
-    suffix_real, suffix_imag, local_real, local_imag = recurrence(
+    suffix_real, suffix_imag, local_real, local_imag, ends = recurrence(
         back_real[0], back_imag[0], pushed_real, pushed_imag, reverse=True
     )
     suffix_real, suffix_imag = (suffix_real[None], suffix_imag[None])
-    summary = (suffix_real[:, 0], suffix_imag[:, 0], local_real[:, 0], local_imag[:, 0])
+    summary = (ends[0], ends[1], ends[2], ends[3])
     carried = incoming_adjoint(summary, neutral_of(summary))
     carry_real = carried[2][:, None]
     carry_imag = carried[3][:, None]
@@ -301,7 +307,7 @@
         grad_out_sum = grad_out_sum + grad_out_part
         if tick_index < MICRO:
             arriving = passed_along(input_grad.astype(jnp.bfloat16), "section", -1)
-    reduced = reduce_scatter_rows(jnp.stack([grad_in_sum, grad_out_sum]))
+    reduced = reduce_scatter_rows(grad_in_sum[None], grad_out_sum[None])
     return (jnp.swapaxes(reduced[0:1], 1, 2), reduced[1:2])
 
 

time: 253 us -> 241 us (0.953)
  local copies, waits for them, and re-layouts: 21 us -> 9.61 us
    slice x8 -> x0, local copies, waits for them, and re-layouts: 5.85 us -> none  [the longest x2 1.53 us: backward_block(): suffix_real[:, 0]]
    another operation x19 -> x0, local copies, waits for them, and re-layouts: 5.41 us -> none  [entering(): stacked = jnp.stack([jnp.broadcast_to(part, common) for part in shard])]
  transfers between devices with their start and end apart: 16 -> 16, of which waited for: 13 -> 13; matrix products, arithmetic and copies ran while one was open for 8% -> 9% of each run, Pallas kernels for 0% -> 0%
where the time goes in v3:
time: 241 us; the launch traced here: 239 us
  blocking collectives  105 us (44%)
  starting transfers between devices  33.1 us (14%)
  other arithmetic  33 us (14%)
  waiting for transfers between devices  30.8 us (13%)
  matrix products  13.1 us (5%)
  Pallas kernels  12.9 us (5%)
  local copies, waits for them, and re-layouts  9.61 us (4%)
    all_gather x4, blocking collectives, entering(): everything = lax.all_gather(stacked, axis)  90.9 us
    ppermute x7, starting transfers between devices, ring_stage(): lax.ppermute(acc_second, axis, behind) + take(second, (pos + step + 2) % n)  27 us
    ppermute x7, waiting for transfers between devices, ring_stage(): lax.ppermute(acc_second, axis, behind) + take(second, (pos + step + 2) % n)  22.3 us
    all_to_all x1, blocking collectives, reduce_scatter_rows(): return lax.all_to_all(split, 'round', 1, 1, tiled=True).sum(axis=1)  14.4 us
    pallas_call x4, Pallas kernels, recurrence(): pl.pallas_call(functools.partial(_recurrence_kernel, reverse=reverse), ou...  12.9 us
    add x7, other arithmetic, ring_stage(): lax.ppermute(acc_second, axis, behind) + take(second, (pos + step + 2) % n)  11.6 us
    ppermute x7, waiting for transfers between devices, ring_stage(): lax.ppermute(acc_first, axis, ahead) + take(first, (pos - step - 2) % n)  7.56 us
    add x7, other arithmetic, ring_stage(): lax.ppermute(acc_first, axis, ahead) + take(first, (pos - step - 2) % n)  6.9 us
  transfers between devices with their start and end apart: 16, of which 13 were waited for; matrix products, arithmetic and copies ran while one was open for 9% of the time, Pallas kernels for 0%

profile of v3, /device:TPU:8, one launch (start us, length us, event | category | flops | bytes accessed | tf_op | source)
XLA Modules:
  0.0 239.3 jit_solution(11888695160143817278)
XLA Ops:
  8.1 3.3 %shard_map.104 = (f32[128,512]{1,0:T(8,128)}, f32[128,512]{1,0:T(8,128)}, f32[2,128,512]{2,1,0:T(8,128)}, f32[2,128,512]{2,1,0:T(8,128)}, f32[4,2,512]{2,1,0:T(2,128)}) custom-call(f32[128,512]{1,0:T(8,128)} %get-tuple-element.215.a_re_ref, f32[128,512]{1,0:T(8,128)} %get-tuple-element.214.a_im_ref, f32[2,128,512]{2,1,0:T(8,128)} %get-tuple-element.198.d_re_ref, ...), custom_call_target="tpu_custom_call" | custom-call | flops 1572864 | bytes 3145728 | tf_op jit(solution)/shard_map/pallas_call | solution.py:55
  11.4 23.7 %all-gather = f32[64,2,512]{2,1,0:T(2,128)S(1)} all-gather(f32[4,2,512]{2,1,0:T(2,128)} %get-tuple-element.24), channel_id=2, replica_groups=mesh['dp'=8,'section'=2,'round'=16] {'round'}, dimensions={0}, use_global_device_ids=true | all-gather | bytes 278528 | tf_op jit(solution)/shard_map/all_gather | solution.py:72
  43.3 3.2 %shard_map.105 = (f32[128,512]{1,0:T(8,128)}, f32[128,512]{1,0:T(8,128)}, f32[2,128,512]{2,1,0:T(8,128)}, f32[2,128,512]{2,1,0:T(8,128)}, f32[4,2,512]{2,1,0:T(2,128)}) custom-call(f32[128,512]{1,0:T(8,128)} %get-tuple-element.215.a_re_ref, f32[128,512]{1,0:T(8,128)} %get-tuple-element.214.a_im_ref, f32[2,128,512]{2,1,0:T(8,128)} %get-tuple-element.196.d_re_ref, ...), custom_call_target="tpu_custom_call" | custom-call | flops 1572864 | bytes 3145728 | tf_op jit(solution)/shard_map/pallas_call | solution.py:55
  46.6 22.2 %all-gather.1 = f32[64,2,512]{2,1,0:T(2,128)S(1)} all-gather(f32[4,2,512]{2,1,0:T(2,128)} %get-tuple-element.29), channel_id=3, replica_groups=mesh['dp'=8,'section'=2,'round'=16] {'round'}, dimensions={0}, use_global_device_ids=true | all-gather | bytes 278528 | tf_op jit(solution)/shard_map/all_gather | solution.py:72
  69.0 2.4 subtract_convert_fusion
  75.9 3.2 %shard_map.106 = (f32[128,512]{1,0:T(8,128)}, f32[128,512]{1,0:T(8,128)}, f32[2,128,512]{2,1,0:T(8,128)}, f32[2,128,512]{2,1,0:T(8,128)}, f32[4,2,512]{2,1,0:T(2,128)}) custom-call(f32[128,512]{1,0:T(8,128)} %get-tuple-element.215.a_re_ref, f32[128,512]{1,0:T(8,128)} %copy-done.3, f32[2,128,512]{2,1,0:T(8,128)} %get-tuple-element.190.d_re_ref, ...), custom_call_target="tpu_custom_call" | custom-call | flops 1572864 | bytes 3145728 | tf_op jit(solution)/shard_map/pallas_call | solution.py:55
  79.2 22.7 %all-gather.2 = f32[64,2,512]{2,1,0:T(2,128)S(1)} all-gather(f32[4,2,512]{2,1,0:T(2,128)} %get-tuple-element.34), channel_id=4, replica_groups=mesh['dp'=8,'section'=2,'round'=16] {'round'}, dimensions={0}, use_global_device_ids=true | all-gather | bytes 278528 | tf_op jit(solution)/shard_map/all_gather | solution.py:72
  112.9 3.2 %shard_map.107 = (f32[128,512]{1,0:T(8,128)}, f32[128,512]{1,0:T(8,128)}, f32[2,128,512]{2,1,0:T(8,128)}, f32[2,128,512]{2,1,0:T(8,128)}, f32[4,2,512]{2,1,0:T(2,128)}) custom-call(f32[128,512]{1,0:T(8,128)} %get-tuple-element.215.a_re_ref, f32[128,512]{1,0:T(8,128)} %copy-done.3, f32[2,128,512]{2,1,0:T(8,128)} %get-tuple-element.188.d_re_ref, ...), custom_call_target="tpu_custom_call" | custom-call | flops 1572864 | bytes 3145728 | tf_op jit(solution)/shard_map/pallas_call | solution.py:55
  116.1 22.4 %all-gather.3 = f32[64,2,512]{2,1,0:T(2,128)S(1)} all-gather(f32[4,2,512]{2,1,0:T(2,128)} %get-tuple-element.39), channel_id=5, replica_groups=mesh['dp'=8,'section'=2,'round'=16] {'round'}, dimensions={0}, use_global_device_ids=true | all-gather | bytes 278528 | tf_op jit(solution)/shard_map/all_gather | solution.py:72
  143.5 2.2 collective-permute-start.2
  148.3 4.9 %collective-permute-start.9 = (f32[1,128,512]{2,1,0:T(8,128)}, f32[1,128,512]{2,1,0:T(8,128)}, u32[]{:S(2)}, u32[]{:S(2)}) collective-permute-start(f32[1,128,512]{2,1,0:T(8,128)} %dynamic-slice_bitcast_fusion), channel_id=1, source_target_pairs={{0,224},{32,0},{64,32},{96,64},{128,96},{160,128},{192,160},{224,1... | collective-permute-start | bytes 786440 | tf_op jit(solution)/shard_map/ppermute | solution.py:104
  159.1 3.7 %collective-permute-start.10 = (f32[1,128,512]{2,1,0:T(8,128)}, f32[1,128,512]{2,1,0:T(8,128)}, u32[]{:S(2)}, u32[]{:S(2)}) collective-permute-start(f32[1,128,512]{2,1,0:T(8,128)} %bitcast_add_fusion.8), channel_id=1, source_target_pairs={{0,224},{32,0},{64,32},{96,64},{128,96},{160,128},{192,160},{224,1... | collective-permute-start | bytes 786440 | tf_op jit(solution)/shard_map/ppermute | solution.py:104
  169.4 3.7 %collective-permute-start.11 = (f32[1,128,512]{2,1,0:T(8,128)}, f32[1,128,512]{2,1,0:T(8,128)}, u32[]{:S(2)}, u32[]{:S(2)}) collective-permute-start(f32[1,128,512]{2,1,0:T(8,128)} %bitcast_add_fusion.7), channel_id=1, source_target_pairs={{0,224},{32,0},{64,32},{96,64},{128,96},{160,128},{192,160},{224,1... | collective-permute-start | bytes 786440 | tf_op jit(solution)/shard_map/ppermute | solution.py:104
  173.1 2.6 %collective-permute-done.4 = f32[1,128,512]{2,1,0:T(8,128)} collective-permute-done((f32[1,128,512]{2,1,0:T(8,128)S(1)}, f32[1,128,512]{2,1,0:T(8,128)}, u32[]{:S(2)}, u32[]{:S(2)}) %collective-permute-start.4) | collective-permute-done | bytes 262176 | tf_op jit(solution)/shard_map/ppermute | solution.py:103
  176.8 2.3 collective-permute-done.11
  180.9 3.7 %collective-permute-start.12 = (f32[1,128,512]{2,1,0:T(8,128)}, f32[1,128,512]{2,1,0:T(8,128)}, u32[]{:S(2)}, u32[]{:S(2)}) collective-permute-start(f32[1,128,512]{2,1,0:T(8,128)} %bitcast_add_fusion.6), channel_id=1, source_target_pairs={{0,224},{32,0},{64,32},{96,64},{128,96},{160,128},{192,160},{224,1... | collective-permute-start | bytes 786440 | tf_op jit(solution)/shard_map/ppermute | solution.py:104
  187.6 3.8 %collective-permute-done.12 = f32[1,128,512]{2,1,0:T(8,128)} collective-permute-done((f32[1,128,512]{2,1,0:T(8,128)}, f32[1,128,512]{2,1,0:T(8,128)}, u32[]{:S(2)}, u32[]{:S(2)}) %collective-permute-start.12) | collective-permute-done | bytes 262176 | tf_op jit(solution)/shard_map/ppermute | solution.py:104
  193.2 3.7 %collective-permute-start.13 = (f32[1,128,512]{2,1,0:T(8,128)}, f32[1,128,512]{2,1,0:T(8,128)}, u32[]{:S(2)}, u32[]{:S(2)}) collective-permute-start(f32[1,128,512]{2,1,0:T(8,128)} %bitcast_add_fusion.5), channel_id=1, source_target_pairs={{0,224},{32,0},{64,32},{96,64},{128,96},{160,128},{192,160},{224,1... | collective-permute-start | bytes 786440 | tf_op jit(solution)/shard_map/ppermute | solution.py:104
  198.0 4.9 %collective-permute-done.13 = f32[1,128,512]{2,1,0:T(8,128)} collective-permute-done((f32[1,128,512]{2,1,0:T(8,128)}, f32[1,128,512]{2,1,0:T(8,128)}, u32[]{:S(2)}, u32[]{:S(2)}) %collective-permute-start.13) | collective-permute-done | bytes 262176 | tf_op jit(solution)/shard_map/ppermute | solution.py:104
  204.6 3.7 %collective-permute-start.14 = (f32[1,128,512]{2,1,0:T(8,128)}, f32[1,128,512]{2,1,0:T(8,128)}, u32[]{:S(2)}, u32[]{:S(2)}) collective-permute-start(f32[1,128,512]{2,1,0:T(8,128)} %bitcast_add_fusion.4), channel_id=1, source_target_pairs={{0,224},{32,0},{64,32},{96,64},{128,96},{160,128},{192,160},{224,1... | collective-permute-start | bytes 786440 | tf_op jit(solution)/shard_map/ppermute | solution.py:104
  209.4 4.1 %collective-permute-done.14 = f32[1,128,512]{2,1,0:T(8,128)} collective-permute-done((f32[1,128,512]{2,1,0:T(8,128)}, f32[1,128,512]{2,1,0:T(8,128)}, u32[]{:S(2)}, u32[]{:S(2)}) %collective-permute-start.14) | collective-permute-done | bytes 262176 | tf_op jit(solution)/shard_map/ppermute | solution.py:104
  215.2 3.7 %collective-permute-start.15 = (f32[1,128,512]{2,1,0:T(8,128)}, f32[1,128,512]{2,1,0:T(8,128)}, u32[]{:S(2)}, u32[]{:S(2)}) collective-permute-start(f32[1,128,512]{2,1,0:T(8,128)} %bitcast_add_fusion.3), channel_id=1, source_target_pairs={{0,224},{32,0},{64,32},{96,64},{128,96},{160,128},{192,160},{224,1... | collective-permute-start | bytes 786440 | tf_op jit(solution)/shard_map/ppermute | solution.py:104
  219.9 3.2 %collective-permute-done.15 = f32[1,128,512]{2,1,0:T(8,128)} collective-permute-done((f32[1,128,512]{2,1,0:T(8,128)}, f32[1,128,512]{2,1,0:T(8,128)}, u32[]{:S(2)}, u32[]{:S(2)}) %collective-permute-start.15) | collective-permute-done | bytes 262176 | tf_op jit(solution)/shard_map/ppermute | solution.py:104
  224.3 14.4 %all_to_all.5 = f32[2,16,8,512]{3,2,0,1:T(8,128)S(1)} all-to-all(f32[2,16,8,512]{3,2,0,1:T(8,128)S(1)} %copy.56), channel_id=1, replica_groups=mesh['dp'=8,'section'=2,'round'=16] {'round'}, dimensions={1} | all-to-all | bytes 1048576 | tf_op jit(solution)/shard_map/all_to_all | solution.py:112
  (196 shorter events, 67.0 us)
Async XLA Ops:
  0.6 5.9 %copy-start = (bf16[1,512,1024]{2,1,0:T(8,128)(2,1)S(1)}, bf16[1,512,1024]{2,1,0:T(8,128)(2,1)}, u32[]{:S(2)}) copy-start(bf16[1,512,1024]{2,1,0:T(8,128)(2,1)} %param.13) | copy-start | bytes 3145732
  2.7 72.0 %copy-start.3 = (f32[128,512]{1,0:T(8,128)}, f32[128,512]{1,0:T(8,128)S(1)}, u32[]{:S(2)}) copy-start(f32[128,512]{1,0:T(8,128)S(1)} %get-tuple-element.212.a_im_ref) | copy-start | bytes 786436
  8.1 29.5 %copy-start.5 = (bf16[1,1024,512]{2,1,0:T(8,128)(2,1)S(1)}, bf16[1,1024,512]{2,1,0:T(8,128)(2,1)}, u32[]{:S(2)}) copy-start(bf16[1,1024,512]{2,1,0:T(8,128)(2,1)} %param.14) | copy-start | bytes 3145732
  38.7 2.8 %collective-permute-start = (bf16[2,128,512]{2,1,0:T(8,128)(2,1)}, bf16[2,128,512]{2,1,0:T(8,128)(2,1)}, u32[]{:S(2)}, u32[]{:S(2)}) collective-permute-start(bf16[2,128,512]{2,1,0:T(8,128)(2,1)} %fusion), channel_id=1, source_target_pairs={{0,16},{1,17},{2,18},{3,19},{4,20},{5,21},{6,22},{7,23},{8,24},{9,... | collective-permute-start | bytes 786440 | tf_op jit(solution)/shard_map/ppermute | solution.py:118
  41.7 63.7 %copy-start.7 = (bf16[2,128,512]{2,1,0:T(8,128)(2,1)}, bf16[2,128,512]{2,1,0:T(8,128)(2,1)S(1)}, u32[]{:S(2)}) copy-start(bf16[2,128,512]{2,1,0:T(8,128)(2,1)S(1)} %get-tuple-element.162) | copy-start | bytes 786436
  79.2 25.1 %copy-start.25 = (f32[2,128,512]{2,1,0:T(8,128)S(1)}, f32[2,128,512]{2,1,0:T(8,128)}, u32[]{:S(2)}) copy-start(f32[2,128,512]{2,1,0:T(8,128)} %get-tuple-element.32) | copy-start | bytes 1572868
  79.2 25.2 %copy-start.26 = (f32[2,128,512]{2,1,0:T(8,128)S(1)}, f32[2,128,512]{2,1,0:T(8,128)}, u32[]{:S(2)}) copy-start(f32[2,128,512]{2,1,0:T(8,128)} %get-tuple-element.36) | copy-start | bytes 1572868
  107.7 3.6 %collective-permute-start.1 = (bf16[2,128,512]{2,1,0:T(8,128)(2,1)S(1)}, bf16[2,128,512]{2,1,0:T(8,128)(2,1)S(1)}, u32[]{:S(2)}, u32[]{:S(2)}) collective-permute-start(bf16[2,128,512]{2,1,0:T(8,128)(2,1)S(1)} %fusion.28), channel_id=1, source_target_pairs={{16,0},{17,1},{18,2},{19,3},{20,4},{21,5},{22,6},{23,7},{24,8},{25... | collective-permute-start | bytes 786440 | tf_op jit(solution)/shard_map/ppermute | solution.py:118
  116.1 24.9 %copy-start.23 = (f32[2,128,512]{2,1,0:T(8,128)S(1)}, f32[2,128,512]{2,1,0:T(8,128)}, u32[]{:S(2)}) copy-start(f32[2,128,512]{2,1,0:T(8,128)} %get-tuple-element.37) | copy-start | bytes 1572868
  116.1 24.9 %copy-start.24 = (f32[2,128,512]{2,1,0:T(8,128)S(1)}, f32[2,128,512]{2,1,0:T(8,128)}, u32[]{:S(2)}) copy-start(f32[2,128,512]{2,1,0:T(8,128)} %get-tuple-element.41) | copy-start | bytes 1572868
  143.5 10.7 %collective-permute-start.2 = (f32[1,128,512]{2,1,0:T(8,128)S(1)}, f32[1,128,512]{2,1,0:T(8,128)}, u32[]{:S(2)}, u32[]{:S(2)}) collective-permute-start(f32[1,128,512]{2,1,0:T(8,128)S(1)} %dynamic-slice_bitcast_fusion.1), channel_id=1, source_target_pairs={{0,32},{32,64},{64,96},{96,128},{128,160},{160,192},{192,224},{224... | collective-permute-start | bytes 786440 | tf_op jit(solution)/shard_map/ppermute | solution.py:103
  148.3 9.1 %collective-permute-start.9 = (f32[1,128,512]{2,1,0:T(8,128)}, f32[1,128,512]{2,1,0:T(8,128)}, u32[]{:S(2)}, u32[]{:S(2)}) collective-permute-start(f32[1,128,512]{2,1,0:T(8,128)} %dynamic-slice_bitcast_fusion), channel_id=1, source_target_pairs={{0,224},{32,0},{64,32},{96,64},{128,96},{160,128},{192,160},{224,1... | collective-permute-start | bytes 786440 | tf_op jit(solution)/shard_map/ppermute | solution.py:104
  155.3 9.3 %collective-permute-start.3 = (f32[1,128,512]{2,1,0:T(8,128)S(1)}, f32[1,128,512]{2,1,0:T(8,128)}, u32[]{:S(2)}, u32[]{:S(2)}) collective-permute-start(f32[1,128,512]{2,1,0:T(8,128)S(1)} %bitcast_add_fusion.15), channel_id=1, source_target_pairs={{0,32},{32,64},{64,96},{96,128},{128,160},{160,192},{192,224},{224... | collective-permute-start | bytes 786440 | tf_op jit(solution)/shard_map/ppermute | solution.py:103
  159.1 8.6 %collective-permute-start.10 = (f32[1,128,512]{2,1,0:T(8,128)}, f32[1,128,512]{2,1,0:T(8,128)}, u32[]{:S(2)}, u32[]{:S(2)}) collective-permute-start(f32[1,128,512]{2,1,0:T(8,128)} %bitcast_add_fusion.8), channel_id=1, source_target_pairs={{0,224},{32,0},{64,32},{96,64},{128,96},{160,128},{192,160},{224,1... | collective-permute-start | bytes 786440 | tf_op jit(solution)/shard_map/ppermute | solution.py:104
  165.5 10.2 %collective-permute-start.4 = (f32[1,128,512]{2,1,0:T(8,128)S(1)}, f32[1,128,512]{2,1,0:T(8,128)}, u32[]{:S(2)}, u32[]{:S(2)}) collective-permute-start(f32[1,128,512]{2,1,0:T(8,128)S(1)} %bitcast_add_fusion.14), channel_id=1, source_target_pairs={{0,32},{32,64},{64,96},{96,128},{128,160},{160,192},{192,224},{224... | collective-permute-start | bytes 786440 | tf_op jit(solution)/shard_map/ppermute | solution.py:103
  169.4 9.7 %collective-permute-start.11 = (f32[1,128,512]{2,1,0:T(8,128)}, f32[1,128,512]{2,1,0:T(8,128)}, u32[]{:S(2)}, u32[]{:S(2)}) collective-permute-start(f32[1,128,512]{2,1,0:T(8,128)} %bitcast_add_fusion.7), channel_id=1, source_target_pairs={{0,224},{32,0},{64,32},{96,64},{128,96},{160,128},{192,160},{224,1... | collective-permute-start | bytes 786440 | tf_op jit(solution)/shard_map/ppermute | solution.py:104
  176.7 9.8 %collective-permute-start.5 = (f32[1,128,512]{2,1,0:T(8,128)S(1)}, f32[1,128,512]{2,1,0:T(8,128)}, u32[]{:S(2)}, u32[]{:S(2)}) collective-permute-start(f32[1,128,512]{2,1,0:T(8,128)S(1)} %bitcast_add_fusion.13), channel_id=1, source_target_pairs={{0,32},{32,64},{64,96},{96,128},{128,160},{160,192},{192,224},{224... | collective-permute-start | bytes 786440 | tf_op jit(solution)/shard_map/ppermute | solution.py:103
  180.9 10.6 %collective-permute-start.12 = (f32[1,128,512]{2,1,0:T(8,128)}, f32[1,128,512]{2,1,0:T(8,128)}, u32[]{:S(2)}, u32[]{:S(2)}) collective-permute-start(f32[1,128,512]{2,1,0:T(8,128)} %bitcast_add_fusion.6), channel_id=1, source_target_pairs={{0,224},{32,0},{64,32},{96,64},{128,96},{160,128},{192,160},{224,1... | collective-permute-start | bytes 786440 | tf_op jit(solution)/shard_map/ppermute | solution.py:104
  187.5 9.3 %collective-permute-start.6 = (f32[1,128,512]{2,1,0:T(8,128)S(1)}, f32[1,128,512]{2,1,0:T(8,128)}, u32[]{:S(2)}, u32[]{:S(2)}) collective-permute-start(f32[1,128,512]{2,1,0:T(8,128)S(1)} %bitcast_add_fusion.12), channel_id=1, source_target_pairs={{0,32},{32,64},{64,96},{96,128},{128,160},{160,192},{192,224},{224... | collective-permute-start | bytes 786440 | tf_op jit(solution)/shard_map/ppermute | solution.py:103
  193.2 9.7 %collective-permute-start.13 = (f32[1,128,512]{2,1,0:T(8,128)}, f32[1,128,512]{2,1,0:T(8,128)}, u32[]{:S(2)}, u32[]{:S(2)}) collective-permute-start(f32[1,128,512]{2,1,0:T(8,128)} %bitcast_add_fusion.5), channel_id=1, source_target_pairs={{0,224},{32,0},{64,32},{96,64},{128,96},{160,128},{192,160},{224,1... | collective-permute-start | bytes 786440 | tf_op jit(solution)/shard_map/ppermute | solution.py:104
  197.9 10.5 %collective-permute-start.7 = (f32[1,128,512]{2,1,0:T(8,128)S(1)}, f32[1,128,512]{2,1,0:T(8,128)}, u32[]{:S(2)}, u32[]{:S(2)}) collective-permute-start(f32[1,128,512]{2,1,0:T(8,128)S(1)} %bitcast_add_fusion.11), channel_id=1, source_target_pairs={{0,32},{32,64},{64,96},{96,128},{128,160},{160,192},{192,224},{224... | collective-permute-start | bytes 786440 | tf_op jit(solution)/shard_map/ppermute | solution.py:103
  204.6 8.8 %collective-permute-start.14 = (f32[1,128,512]{2,1,0:T(8,128)}, f32[1,128,512]{2,1,0:T(8,128)}, u32[]{:S(2)}, u32[]{:S(2)}) collective-permute-start(f32[1,128,512]{2,1,0:T(8,128)} %bitcast_add_fusion.4), channel_id=1, source_target_pairs={{0,224},{32,0},{64,32},{96,64},{128,96},{160,128},{192,160},{224,1... | collective-permute-start | bytes 786440 | tf_op jit(solution)/shard_map/ppermute | solution.py:104
  209.3 9.6 %collective-permute-start.8 = (f32[1,128,512]{2,1,0:T(8,128)S(1)}, f32[1,128,512]{2,1,0:T(8,128)}, u32[]{:S(2)}, u32[]{:S(2)}) collective-permute-start(f32[1,128,512]{2,1,0:T(8,128)S(1)} %bitcast_add_fusion.10), channel_id=1, source_target_pairs={{0,32},{32,64},{64,96},{96,128},{128,160},{160,192},{192,224},{224... | collective-permute-start | bytes 786440 | tf_op jit(solution)/shard_map/ppermute | solution.py:103
  215.2 7.9 %collective-permute-start.15 = (f32[1,128,512]{2,1,0:T(8,128)}, f32[1,128,512]{2,1,0:T(8,128)}, u32[]{:S(2)}, u32[]{:S(2)}) collective-permute-start(f32[1,128,512]{2,1,0:T(8,128)} %bitcast_add_fusion.3), channel_id=1, source_target_pairs={{0,224},{32,0},{64,32},{96,64},{128,96},{160,128},{192,160},{224,1... | collective-permute-start | bytes 786440 | tf_op jit(solution)/shard_map/ppermute | solution.py:104
  (22 other events, 69.9 us)

commit v4 on v3

--- a/solution.py
+++ b/solution.py
@@ -69,7 +69,8 @@
     peers, position = (lax.axis_size(axis), lax.axis_index(axis))
     common = jnp.broadcast_shapes(*(part.shape for part in shard))
     stacked = jnp.stack([jnp.broadcast_to(part, common) for part in shard])
-    everything = lax.all_gather(stacked, axis)
+    copies = jnp.broadcast_to(stacked[None], (peers,) + stacked.shape)
+    everything = lax.all_to_all(copies, axis, 0, 0, tiled=True)
     state = tuple(
         jnp.broadcast_to(jnp.asarray(zero, part.dtype), common) for part, zero in zip(shard, identity)
     )

time: 241 us -> 205 us (0.85)
  blocking collectives: 105 us -> 15 us
  starting transfers between devices: 33.1 us -> 56 us
  waiting for transfers between devices: 30.8 us -> 43 us
  other arithmetic: 33 us -> 42.9 us
  local copies, waits for them, and re-layouts: 9.61 us -> 16.4 us
    all_gather x4 -> x0, blocking collectives: 90.9 us -> none  [entering(): everything = lax.all_gather(stacked, axis)]
    all_to_all x0 -> x4, starting transfers between devices: none -> 24.7 us  [entering(): everything = lax.all_to_all(copies, axis, 0, 0, tiled=True)]
    ppermute x7, waiting for transfers between devices: 22.3 us -> 6.61 us  [ring_stage(): lax.ppermute(acc_second, axis, behind) + take(second, (pos + step + 2) % n)]
    all_to_all x0 -> x4, waiting for transfers between devices: none -> 15.5 us  [entering(): everything = lax.all_to_all(copies, axis, 0, 0, tiled=True)]
    ppermute x7, waiting for transfers between devices: 7.56 us -> 19.5 us  [ring_stage(): lax.ppermute(acc_first, axis, ahead) + take(first, (pos - step - 2) % n)]
    select_n x54, other arithmetic: 1.19 us -> 7.67 us  [entering(): state = tuple((jnp.where(reached, a, b) for a, b in zip(new, state)))]
    broadcast_in_dim x0 -> x4, local copies, waits for them, and re-layouts: none -> 6.24 us  [entering(): copies = jnp.broadcast_to(stacked[None], (peers,) + stacked.shape)]
    dot_general x2, matrix products: 2.32 us -> 5.42 us  [backward_block(): jnp.einsum('brk,brw->kw', hidden, upstream_low, preferred_element_type=jn...]
  transfers between devices with their start and end apart: 16 -> 20, of which waited for: 13 -> 19; matrix products, arithmetic and copies ran while one was open for 9% -> 17% of each run, Pallas kernels for 0% -> 0%
where the time goes in v4:
time: 205 us; the launch traced here: 203 us
  starting transfers between devices  56 us (27%)
  waiting for transfers between devices  43 us (21%)
  other arithmetic  42.9 us (21%)
  local copies, waits for them, and re-layouts  16.4 us (8%)
  matrix products  15.4 us (8%)
  blocking collectives  15 us (7%)
  Pallas kernels  13 us (6%)
    ppermute x7, starting transfers between devices, ring_stage(): lax.ppermute(acc_second, axis, behind) + take(second, (pos + step + 2) % n)  28.1 us
    all_to_all x4, starting transfers between devices, entering(): everything = lax.all_to_all(copies, axis, 0, 0, tiled=True)  24.7 us
    ppermute x7, waiting for transfers between devices, ring_stage(): lax.ppermute(acc_first, axis, ahead) + take(first, (pos - step - 2) % n)  19.5 us
    all_to_all x4, waiting for transfers between devices, entering(): everything = lax.all_to_all(copies, axis, 0, 0, tiled=True)  15.5 us
    all_to_all x1, blocking collectives, reduce_scatter_rows(): return lax.all_to_all(split, 'round', 1, 1, tiled=True).sum(axis=1)  15 us
    pallas_call x4, Pallas kernels, recurrence(): pl.pallas_call(functools.partial(_recurrence_kernel, reverse=reverse), ou...  13 us
    add x7, other arithmetic, ring_stage(): lax.ppermute(acc_second, axis, behind) + take(second, (pos + step + 2) % n)  10.4 us
    add x7, other arithmetic, ring_stage(): lax.ppermute(acc_first, axis, ahead) + take(first, (pos - step - 2) % n)  8.87 us
  transfers between devices with their start and end apart: 20, of which 19 were waited for; matrix products, arithmetic and copies ran while one was open for 17% of the time, Pallas kernels for 0%

profile of v4, /device:TPU:8, one launch (start us, length us, event | category | flops | bytes accessed | tf_op | source)
XLA Modules:
  0.0 203.4 jit_solution(18047322331628932302)
XLA Ops:
  8.1 3.2 %shard_map.104 = (f32[128,512]{1,0:T(8,128)}, f32[128,512]{1,0:T(8,128)}, f32[2,128,512]{2,1,0:T(8,128)}, f32[2,128,512]{2,1,0:T(8,128)}, f32[4,2,512]{2,1,0:T(2,128)}) custom-call(f32[128,512]{1,0:T(8,128)} %get-tuple-element.215.a_re_ref, f32[128,512]{1,0:T(8,128)} %get-tuple-element.214.a_im_ref, f32[2,128,512]{2,1,0:T(8,128)} %get-tuple-element.198.d_re_ref, ...), custom_call_target="tpu_custom_call" | custom-call | flops 1572864 | bytes 3145728 | tf_op jit(solution)/shard_map/pallas_call | solution.py:55
  12.9 7.4 %all-to-all-start = ((f32[16,4,2,512]{3,2,1,0:T(2,128)}), f32[16,4,2,512]{3,2,1,0:T(2,128)S(1)}, u32[]{:S(2)}, u32[]{:S(2)}) async-start(f32[16,4,2,512]{3,2,1,0:T(2,128)} %broadcast_in_dim.8), calls=%async_computation | async-start | bytes 524288 | tf_op jit(solution)/shard_map/all_to_all | solution.py:73
  20.3 7.1 %all-to-all-done = f32[16,4,2,512]{3,2,1,0:T(2,128)S(1)} async-done(((f32[16,4,2,512]{3,2,1,0:T(2,128)}), f32[16,4,2,512]{3,2,1,0:T(2,128)S(1)}, u32[]{:S(2)}, u32[]{:S(2)}) %all-to-all-start) | async-done | bytes 262176 | tf_op jit(solution)/shard_map/all_to_all | solution.py:73
  34.0 3.2 %shard_map.105 = (f32[128,512]{1,0:T(8,128)}, f32[128,512]{1,0:T(8,128)}, f32[2,128,512]{2,1,0:T(8,128)}, f32[2,128,512]{2,1,0:T(8,128)}, f32[4,2,512]{2,1,0:T(2,128)}) custom-call(f32[128,512]{1,0:T(8,128)} %get-tuple-element.215.a_re_ref, f32[128,512]{1,0:T(8,128)} %get-tuple-element.214.a_im_ref, f32[2,128,512]{2,1,0:T(8,128)} %get-tuple-element.196.d_re_ref, ...), custom_call_target="tpu_custom_call" | custom-call | flops 1572864 | bytes 3145728 | tf_op jit(solution)/shard_map/pallas_call | solution.py:55
  38.8 5.4 %all-to-all-start.1 = ((f32[16,4,2,512]{3,2,1,0:T(2,128)}), f32[16,4,2,512]{3,2,1,0:T(2,128)}, u32[]{:S(2)}, u32[]{:S(2)}) async-start(f32[16,4,2,512]{3,2,1,0:T(2,128)} %broadcast_in_dim.9), calls=%async_computation.1 | async-start | bytes 524288 | tf_op jit(solution)/shard_map/all_to_all | solution.py:73
  44.3 7.9 %all-to-all-done.1 = f32[16,4,2,512]{3,2,1,0:T(2,128)} async-done(((f32[16,4,2,512]{3,2,1,0:T(2,128)}), f32[16,4,2,512]{3,2,1,0:T(2,128)}, u32[]{:S(2)}, u32[]{:S(2)}) %all-to-all-start.1) | async-done | bytes 262176 | tf_op jit(solution)/shard_map/all_to_all | solution.py:73
  58.9 2.4 %subtract_convert_fusion = (bf16[2,128,512]{2,1,0:T(8,128)(2,1)}, bf16[2,128,512]{2,1,0:T(8,128)(2,1)}) fusion(f32[2,128,512]{2,1,0:T(8,128)} %get-tuple-element.27, f32[2,512]{1,0:T(2,128)S(1)} %fusion.64, f32[128,512]{1,0:T(8,128)} %get-tuple-element.30, f32[2,512]{1,0:T(2,128)S(1)} %get-tuple-element.137, f32[128,512]{1,0:T(8,128)} %get-tuple-element.28, ...), kind=kLoop, calls=%fused_computation.76 | loop fusion | flops 1310720 | bytes 2105344 | tf_op jit(solution)/shard_map/convert
  65.8 3.3 %shard_map.106 = (f32[128,512]{1,0:T(8,128)}, f32[128,512]{1,0:T(8,128)}, f32[2,128,512]{2,1,0:T(8,128)}, f32[2,128,512]{2,1,0:T(8,128)}, f32[4,2,512]{2,1,0:T(2,128)}) custom-call(f32[128,512]{1,0:T(8,128)} %get-tuple-element.215.a_re_ref, f32[128,512]{1,0:T(8,128)} %copy-done.5, f32[2,128,512]{2,1,0:T(8,128)} %get-tuple-element.190.d_re_ref, ...), custom_call_target="tpu_custom_call" | custom-call | flops 1572864 | bytes 3145728 | tf_op jit(solution)/shard_map/pallas_call | solution.py:55
  70.6 5.2 %all-to-all-start.2 = ((f32[16,4,2,512]{3,2,1,0:T(2,128)}), f32[16,4,2,512]{3,2,1,0:T(2,128)S(1)}, u32[]{:S(2)}, u32[]{:S(2)}) async-start(f32[16,4,2,512]{3,2,1,0:T(2,128)} %broadcast_in_dim.10), calls=%async_computation.2 | async-start | bytes 524288 | tf_op jit(solution)/shard_map/all_to_all | solution.py:73
  79.1 3.1 %fusion.42 = f32[1024,512,1]{1,0,2:T(8,128)} fusion(f32[512]{0:T(512)S(1)} %convert_element_type.76, f32[2,128]{1,0:T(2,128)S(1)} %fusion.429, pred[]{:T(512)S(6)} %eq.21, bf16[2,128,512]{2,1,0:T(8,128)(2,1)} %get-tuple-element.204, bf16[2,128,512]{2,1,0:T(8,128)(2,1)} %get-tuple-element.203, bf16[2,128,512]{2,1,0:T(8,128)(2,1)} %copy-done.15, ...), kind=kOutput, calls=%fused_computation.82 | convolution fusion | flops 271187968 | bytes 3148801 | tf_op jit(solution)/shard_map/brk,brw->kw/dot_general | solution.py:192
  91.4 3.3 %shard_map.107 = (f32[128,512]{1,0:T(8,128)}, f32[128,512]{1,0:T(8,128)}, f32[2,128,512]{2,1,0:T(8,128)}, f32[2,128,512]{2,1,0:T(8,128)}, f32[4,2,512]{2,1,0:T(2,128)}) custom-call(f32[128,512]{1,0:T(8,128)} %get-tuple-element.215.a_re_ref, f32[128,512]{1,0:T(8,128)} %copy-done.5, f32[2,128,512]{2,1,0:T(8,128)} %get-tuple-element.188.d_re_ref, ...), custom_call_target="tpu_custom_call" | custom-call | flops 1572864 | bytes 3145728 | tf_op jit(solution)/shard_map/pallas_call | solution.py:55
  96.3 6.7 %all-to-all-start.3 = ((f32[16,4,2,512]{3,2,1,0:T(2,128)}), f32[16,4,2,512]{3,2,1,0:T(2,128)S(1)}, u32[]{:S(2)}, u32[]{:S(2)}) async-start(f32[16,4,2,512]{3,2,1,0:T(2,128)} %broadcast_in_dim.11), calls=%async_computation.3 | async-start | bytes 524288 | tf_op jit(solution)/shard_map/all_to_all | solution.py:73
  103.1 2.4 %bitcast_add_fusion = f32[1024,512]{1,0:T(8,128)S(1)} fusion(f32[1024,512,1]{1,0,2:T(8,128)} %fusion.42, bf16[2,128,512]{2,1,0:T(8,128)(2,1)S(1)} %copy-done.12, pred[]{:T(512)S(6)} %eq.21, bf16[2,128,512]{2,1,0:T(8,128)(2,1)} %get-tuple-element.204, bf16[2,128,512]{2,1,0:T(8,128)(2,1)} %get-tuple-element.203, bf16[2,128,512]{2,1,0:T(8,128)(2,1)} %copy-done.15, ...), kind=kOutput, calls=%fused_computation | convolution fusion | flops 271712256 | bytes 5505025 | tf_op jit(solution)/shard_map/brk,brw->kw/dot_general | solution.py:192
  107.7 5.9 %collective-permute-start.9 = (f32[1,128,512]{2,1,0:T(8,128)}, f32[1,128,512]{2,1,0:T(8,128)}, u32[]{:S(2)}, u32[]{:S(2)}) collective-permute-start(f32[1,128,512]{2,1,0:T(8,128)} %dynamic-slice_bitcast_fusion), channel_id=1, source_target_pairs={{0,224},{32,0},{64,32},{96,64},{128,96},{160,128},{192,160},{224,1... | collective-permute-start | bytes 786440 | tf_op jit(solution)/shard_map/ppermute | solution.py:105
  122.0 3.7 %collective-permute-start.10 = (f32[1,128,512]{2,1,0:T(8,128)}, f32[1,128,512]{2,1,0:T(8,128)}, u32[]{:S(2)}, u32[]{:S(2)}) collective-permute-start(f32[1,128,512]{2,1,0:T(8,128)} %bitcast_add_fusion.8), channel_id=1, source_target_pairs={{0,224},{32,0},{64,32},{96,64},{128,96},{160,128},{192,160},{224,1... | collective-permute-start | bytes 786440 | tf_op jit(solution)/shard_map/ppermute | solution.py:105
  125.6 4.4 %collective-permute-done.2 = f32[1,128,512]{2,1,0:T(8,128)} collective-permute-done((f32[1,128,512]{2,1,0:T(8,128)S(1)}, f32[1,128,512]{2,1,0:T(8,128)}, u32[]{:S(2)}, u32[]{:S(2)}) %collective-permute-start.2) | collective-permute-done | bytes 262176 | tf_op jit(solution)/shard_map/ppermute | solution.py:104
  133.2 3.7 %collective-permute-start.11 = (f32[1,128,512]{2,1,0:T(8,128)}, f32[1,128,512]{2,1,0:T(8,128)}, u32[]{:S(2)}, u32[]{:S(2)}) collective-permute-start(f32[1,128,512]{2,1,0:T(8,128)} %bitcast_add_fusion.7), channel_id=1, source_target_pairs={{0,224},{32,0},{64,32},{96,64},{128,96},{160,128},{192,160},{224,1... | collective-permute-start | bytes 786440 | tf_op jit(solution)/shard_map/ppermute | solution.py:105
  136.9 3.4 %collective-permute-done.3 = f32[1,128,512]{2,1,0:T(8,128)} collective-permute-done((f32[1,128,512]{2,1,0:T(8,128)S(1)}, f32[1,128,512]{2,1,0:T(8,128)}, u32[]{:S(2)}, u32[]{:S(2)}) %collective-permute-start.3) | collective-permute-done | bytes 262176 | tf_op jit(solution)/shard_map/ppermute | solution.py:104
  143.6 3.7 %collective-permute-start.12 = (f32[1,128,512]{2,1,0:T(8,128)}, f32[1,128,512]{2,1,0:T(8,128)}, u32[]{:S(2)}, u32[]{:S(2)}) collective-permute-start(f32[1,128,512]{2,1,0:T(8,128)} %bitcast_add_fusion.6), channel_id=1, source_target_pairs={{0,224},{32,0},{64,32},{96,64},{128,96},{160,128},{192,160},{224,1... | collective-permute-start | bytes 786440 | tf_op jit(solution)/shard_map/ppermute | solution.py:105
  153.1 3.7 %collective-permute-start.13 = (f32[1,128,512]{2,1,0:T(8,128)}, f32[1,128,512]{2,1,0:T(8,128)}, u32[]{:S(2)}, u32[]{:S(2)}) collective-permute-start(f32[1,128,512]{2,1,0:T(8,128)} %bitcast_add_fusion.5), channel_id=1, source_target_pairs={{0,224},{32,0},{64,32},{96,64},{128,96},{160,128},{192,160},{224,1... | collective-permute-start | bytes 786440 | tf_op jit(solution)/shard_map/ppermute | solution.py:105
  162.7 3.7 %collective-permute-start.14 = (f32[1,128,512]{2,1,0:T(8,128)}, f32[1,128,512]{2,1,0:T(8,128)}, u32[]{:S(2)}, u32[]{:S(2)}) collective-permute-start(f32[1,128,512]{2,1,0:T(8,128)} %bitcast_add_fusion.4), channel_id=1, source_target_pairs={{0,224},{32,0},{64,32},{96,64},{128,96},{160,128},{192,160},{224,1... | collective-permute-start | bytes 786440 | tf_op jit(solution)/shard_map/ppermute | solution.py:105
  172.0 3.8 %collective-permute-start.15 = (f32[1,128,512]{2,1,0:T(8,128)S(1)}, f32[1,128,512]{2,1,0:T(8,128)}, u32[]{:S(2)}, u32[]{:S(2)}) collective-permute-start(f32[1,128,512]{2,1,0:T(8,128)S(1)} %bitcast_add_fusion.3), channel_id=1, source_target_pairs={{0,224},{32,0},{64,32},{96,64},{128,96},{160,128},{192,160},{224,1... | collective-permute-start | bytes 786440 | tf_op jit(solution)/shard_map/ppermute | solution.py:105
  180.6 5.9 %collective-permute-done.8 = f32[1,128,512]{2,1,0:T(8,128)} collective-permute-done((f32[1,128,512]{2,1,0:T(8,128)}, f32[1,128,512]{2,1,0:T(8,128)}, u32[]{:S(2)}, u32[]{:S(2)}) %collective-permute-start.8) | collective-permute-done | bytes 262176 | tf_op jit(solution)/shard_map/ppermute | solution.py:104
  187.7 15.0 %all_to_all.25 = f32[2,16,8,512]{3,2,0,1:T(8,128)S(1)} all-to-all(f32[2,16,8,512]{3,2,0,1:T(8,128)S(1)} %copy.56), channel_id=1, replica_groups=mesh['dp'=8,'section'=2,'round'=16] {'round'}, dimensions={1} | all-to-all | bytes 1048576 | tf_op jit(solution)/shard_map/all_to_all | solution.py:113
  (188 shorter events, 84.5 us)
Async XLA Ops:
  2.7 61.9 %copy-start.5 = (f32[128,512]{1,0:T(8,128)}, f32[128,512]{1,0:T(8,128)S(1)}, u32[]{:S(2)}) copy-start(f32[128,512]{1,0:T(8,128)S(1)} %get-tuple-element.212.a_im_ref) | copy-start | bytes 786436
  11.3 17.9 %copy-start.7 = (bf16[1,1024,512]{2,1,0:T(8,128)(2,1)S(1)}, bf16[1,1024,512]{2,1,0:T(8,128)(2,1)}, u32[]{:S(2)}) copy-start(bf16[1,1024,512]{2,1,0:T(8,128)(2,1)} %param.14) | copy-start | bytes 3145732
  12.9 14.5 %all-to-all-start = ((f32[16,4,2,512]{3,2,1,0:T(2,128)}), f32[16,4,2,512]{3,2,1,0:T(2,128)S(1)}, u32[]{:S(2)}, u32[]{:S(2)}) async-start(f32[16,4,2,512]{3,2,1,0:T(2,128)} %broadcast_in_dim.8), calls=%async_computation | async-start | bytes 524288 | tf_op jit(solution)/shard_map/all_to_all | solution.py:73
  29.7 2.4 %collective-permute-start = (bf16[2,128,512]{2,1,0:T(8,128)(2,1)S(1)}, bf16[2,128,512]{2,1,0:T(8,128)(2,1)S(1)}, u32[]{:S(2)}, u32[]{:S(2)}) collective-permute-start(bf16[2,128,512]{2,1,0:T(8,128)(2,1)S(1)} %fusion), channel_id=1, source_target_pairs={{0,16},{1,17},{2,18},{3,19},{4,20},{5,21},{6,22},{7,23},{8,24},{9,... | collective-permute-start | bytes 786440 | tf_op jit(solution)/shard_map/ppermute | solution.py:119
  32.3 55.1 %copy-start.9 = (bf16[2,128,512]{2,1,0:T(8,128)(2,1)}, bf16[2,128,512]{2,1,0:T(8,128)(2,1)S(1)}, u32[]{:S(2)}) copy-start(bf16[2,128,512]{2,1,0:T(8,128)(2,1)S(1)} %get-tuple-element.162) | copy-start | bytes 786436
  38.8 13.4 %all-to-all-start.1 = ((f32[16,4,2,512]{3,2,1,0:T(2,128)}), f32[16,4,2,512]{3,2,1,0:T(2,128)}, u32[]{:S(2)}, u32[]{:S(2)}) async-start(f32[16,4,2,512]{3,2,1,0:T(2,128)} %broadcast_in_dim.9), calls=%async_computation.1 | async-start | bytes 524288 | tf_op jit(solution)/shard_map/all_to_all | solution.py:73
  70.6 12.1 %all-to-all-start.2 = ((f32[16,4,2,512]{3,2,1,0:T(2,128)}), f32[16,4,2,512]{3,2,1,0:T(2,128)S(1)}, u32[]{:S(2)}, u32[]{:S(2)}) async-start(f32[16,4,2,512]{3,2,1,0:T(2,128)} %broadcast_in_dim.10), calls=%async_computation.2 | async-start | bytes 524288 | tf_op jit(solution)/shard_map/all_to_all | solution.py:73
  86.0 3.6 %collective-permute-start.1 = (bf16[2,128,512]{2,1,0:T(8,128)(2,1)S(1)}, bf16[2,128,512]{2,1,0:T(8,128)(2,1)S(1)}, u32[]{:S(2)}, u32[]{:S(2)}) collective-permute-start(bf16[2,128,512]{2,1,0:T(8,128)(2,1)S(1)} %fusion.28), channel_id=1, source_target_pairs={{16,0},{17,1},{18,2},{19,3},{20,4},{21,5},{22,6},{23,7},{24,8},{25... | collective-permute-start | bytes 786440 | tf_op jit(solution)/shard_map/ppermute | solution.py:119
  91.4 11.6 %copy-start.12 = (bf16[2,128,512]{2,1,0:T(8,128)(2,1)S(1)}, bf16[2,128,512]{2,1,0:T(8,128)(2,1)}, u32[]{:S(2)}) copy-start(bf16[2,128,512]{2,1,0:T(8,128)(2,1)} %copy-done.11) | copy-start | bytes 786436
  96.3 17.2 %all-to-all-start.3 = ((f32[16,4,2,512]{3,2,1,0:T(2,128)}), f32[16,4,2,512]{3,2,1,0:T(2,128)S(1)}, u32[]{:S(2)}, u32[]{:S(2)}) async-start(f32[16,4,2,512]{3,2,1,0:T(2,128)} %broadcast_in_dim.11), calls=%async_computation.3 | async-start | bytes 524288 | tf_op jit(solution)/shard_map/all_to_all | solution.py:73
  107.7 12.6 %collective-permute-start.9 = (f32[1,128,512]{2,1,0:T(8,128)}, f32[1,128,512]{2,1,0:T(8,128)}, u32[]{:S(2)}, u32[]{:S(2)}) collective-permute-start(f32[1,128,512]{2,1,0:T(8,128)} %dynamic-slice_bitcast_fusion), channel_id=1, source_target_pairs={{0,224},{32,0},{64,32},{96,64},{128,96},{160,128},{192,160},{224,1... | collective-permute-start | bytes 786440 | tf_op jit(solution)/shard_map/ppermute | solution.py:105
  119.2 10.8 %collective-permute-start.2 = (f32[1,128,512]{2,1,0:T(8,128)S(1)}, f32[1,128,512]{2,1,0:T(8,128)}, u32[]{:S(2)}, u32[]{:S(2)}) collective-permute-start(f32[1,128,512]{2,1,0:T(8,128)S(1)} %dynamic-slice_bitcast_fusion.1), channel_id=1, source_target_pairs={{0,32},{32,64},{64,96},{96,128},{128,160},{160,192},{192,224},{224... | collective-permute-start | bytes 786440 | tf_op jit(solution)/shard_map/ppermute | solution.py:104
  122.0 9.6 %collective-permute-start.10 = (f32[1,128,512]{2,1,0:T(8,128)}, f32[1,128,512]{2,1,0:T(8,128)}, u32[]{:S(2)}, u32[]{:S(2)}) collective-permute-start(f32[1,128,512]{2,1,0:T(8,128)} %bitcast_add_fusion.8), channel_id=1, source_target_pairs={{0,224},{32,0},{64,32},{96,64},{128,96},{160,128},{192,160},{224,1... | collective-permute-start | bytes 786440 | tf_op jit(solution)/shard_map/ppermute | solution.py:105
  131.1 9.1 %collective-permute-start.3 = (f32[1,128,512]{2,1,0:T(8,128)S(1)}, f32[1,128,512]{2,1,0:T(8,128)}, u32[]{:S(2)}, u32[]{:S(2)}) collective-permute-start(f32[1,128,512]{2,1,0:T(8,128)S(1)} %bitcast_add_fusion.15), channel_id=1, source_target_pairs={{0,32},{32,64},{64,96},{96,128},{128,160},{160,192},{192,224},{224... | collective-permute-start | bytes 786440 | tf_op jit(solution)/shard_map/ppermute | solution.py:104
  133.2 8.7 %collective-permute-start.11 = (f32[1,128,512]{2,1,0:T(8,128)}, f32[1,128,512]{2,1,0:T(8,128)}, u32[]{:S(2)}, u32[]{:S(2)}) collective-permute-start(f32[1,128,512]{2,1,0:T(8,128)} %bitcast_add_fusion.7), channel_id=1, source_target_pairs={{0,224},{32,0},{64,32},{96,64},{128,96},{160,128},{192,160},{224,1... | collective-permute-start | bytes 786440 | tf_op jit(solution)/shard_map/ppermute | solution.py:105
  141.3 8.3 %collective-permute-start.4 = (f32[1,128,512]{2,1,0:T(8,128)S(1)}, f32[1,128,512]{2,1,0:T(8,128)}, u32[]{:S(2)}, u32[]{:S(2)}) collective-permute-start(f32[1,128,512]{2,1,0:T(8,128)S(1)} %bitcast_add_fusion.14), channel_id=1, source_target_pairs={{0,32},{32,64},{64,96},{96,128},{128,160},{160,192},{192,224},{224... | collective-permute-start | bytes 786440 | tf_op jit(solution)/shard_map/ppermute | solution.py:104
  143.6 7.9 %collective-permute-start.12 = (f32[1,128,512]{2,1,0:T(8,128)}, f32[1,128,512]{2,1,0:T(8,128)}, u32[]{:S(2)}, u32[]{:S(2)}) collective-permute-start(f32[1,128,512]{2,1,0:T(8,128)} %bitcast_add_fusion.6), channel_id=1, source_target_pairs={{0,224},{32,0},{64,32},{96,64},{128,96},{160,128},{192,160},{224,1... | collective-permute-start | bytes 786440 | tf_op jit(solution)/shard_map/ppermute | solution.py:105
  150.6 7.8 %collective-permute-start.5 = (f32[1,128,512]{2,1,0:T(8,128)S(1)}, f32[1,128,512]{2,1,0:T(8,128)}, u32[]{:S(2)}, u32[]{:S(2)}) collective-permute-start(f32[1,128,512]{2,1,0:T(8,128)S(1)} %bitcast_add_fusion.13), channel_id=1, source_target_pairs={{0,32},{32,64},{64,96},{96,128},{128,160},{160,192},{192,224},{224... | collective-permute-start | bytes 786440 | tf_op jit(solution)/shard_map/ppermute | solution.py:104
  153.1 7.9 %collective-permute-start.13 = (f32[1,128,512]{2,1,0:T(8,128)}, f32[1,128,512]{2,1,0:T(8,128)}, u32[]{:S(2)}, u32[]{:S(2)}) collective-permute-start(f32[1,128,512]{2,1,0:T(8,128)} %bitcast_add_fusion.5), channel_id=1, source_target_pairs={{0,224},{32,0},{64,32},{96,64},{128,96},{160,128},{192,160},{224,1... | collective-permute-start | bytes 786440 | tf_op jit(solution)/shard_map/ppermute | solution.py:105
  159.5 7.8 %collective-permute-start.6 = (f32[1,128,512]{2,1,0:T(8,128)S(1)}, f32[1,128,512]{2,1,0:T(8,128)}, u32[]{:S(2)}, u32[]{:S(2)}) collective-permute-start(f32[1,128,512]{2,1,0:T(8,128)S(1)} %bitcast_add_fusion.12), channel_id=1, source_target_pairs={{0,32},{32,64},{64,96},{96,128},{128,160},{160,192},{192,224},{224... | collective-permute-start | bytes 786440 | tf_op jit(solution)/shard_map/ppermute | solution.py:104
  162.7 8.3 %collective-permute-start.14 = (f32[1,128,512]{2,1,0:T(8,128)}, f32[1,128,512]{2,1,0:T(8,128)}, u32[]{:S(2)}, u32[]{:S(2)}) collective-permute-start(f32[1,128,512]{2,1,0:T(8,128)} %bitcast_add_fusion.4), channel_id=1, source_target_pairs={{0,224},{32,0},{64,32},{96,64},{128,96},{160,128},{192,160},{224,1... | collective-permute-start | bytes 786440 | tf_op jit(solution)/shard_map/ppermute | solution.py:105
  169.0 7.9 %collective-permute-start.7 = (f32[1,128,512]{2,1,0:T(8,128)}, f32[1,128,512]{2,1,0:T(8,128)}, u32[]{:S(2)}, u32[]{:S(2)}) collective-permute-start(f32[1,128,512]{2,1,0:T(8,128)} %bitcast_add_fusion.11), channel_id=1, source_target_pairs={{0,32},{32,64},{64,96},{96,128},{128,160},{160,192},{192,224},{224... | collective-permute-start | bytes 786440 | tf_op jit(solution)/shard_map/ppermute | solution.py:104
  172.0 7.7 %collective-permute-start.15 = (f32[1,128,512]{2,1,0:T(8,128)S(1)}, f32[1,128,512]{2,1,0:T(8,128)}, u32[]{:S(2)}, u32[]{:S(2)}) collective-permute-start(f32[1,128,512]{2,1,0:T(8,128)S(1)} %bitcast_add_fusion.3), channel_id=1, source_target_pairs={{0,224},{32,0},{64,32},{96,64},{128,96},{160,128},{192,160},{224,1... | collective-permute-start | bytes 786440 | tf_op jit(solution)/shard_map/ppermute | solution.py:105
  178.7 7.9 %collective-permute-start.8 = (f32[1,128,512]{2,1,0:T(8,128)}, f32[1,128,512]{2,1,0:T(8,128)}, u32[]{:S(2)}, u32[]{:S(2)}) collective-permute-start(f32[1,128,512]{2,1,0:T(8,128)} %bitcast_add_fusion.10), channel_id=1, source_target_pairs={{0,32},{32,64},{64,96},{96,128},{128,160},{160,192},{192,224},{224... | collective-permute-start | bytes 786440 | tf_op jit(solution)/shard_map/ppermute | solution.py:104
  (18 other events, 68.4 us)

commit v5 on v4

--- a/solution.py
+++ b/solution.py
@@ -108,9 +108,18 @@
 
 def reduce_scatter_rows(first, second):
     peers = lax.axis_size("round")
-    x = ring_stage(first, second, "dp", lax.axis_size("dp"), 1, 1)
-    split = x.reshape(x.shape[0], peers, x.shape[1] // peers, x.shape[2])
-    return lax.all_to_all(split, "round", 1, 1, tiled=True).sum(axis=1)
+    groups = lax.axis_size("dp")
+    rows, width = first.shape[1], first.shape[2]
+    half = width // 2
+    early = second.reshape(1, groups, peers, rows // (groups * peers), width)
+    early = lax.all_to_all(early, "round", 2, 2, tiled=True).sum(axis=2)
+    early = early.reshape(1, rows // peers, width)
+    early = ring_stage(early[..., :half], early[..., half:], "dp", groups, 1, 1)
+    late = ring_stage(first[..., :half], first[..., half:], "dp", groups, 1, 1)
+    late = jnp.concatenate([late[0:1], late[1:2]], axis=2)
+    late = late.reshape(1, peers, late.shape[1] // peers, width)
+    late = lax.all_to_all(late, "round", 1, 1, tiled=True).sum(axis=1)
+    return jnp.concatenate([late, jnp.concatenate([early[0:1], early[1:2]], axis=2)], 0)
 
 
 def passed_along(value, axis, steps):

time: 205 us -> 242 us (1.18)
  waiting for transfers between devices: 43 us -> 81.9 us
  starting transfers between devices: 56 us -> 85.9 us
  other arithmetic: 42.9 us -> 25.1 us
  blocking collectives: 15 us -> 0 us
    all_to_all x0 -> x2, waiting for transfers between devices: none -> 21 us  [the longest x1 17 us: reduce_scatter_rows(): early = lax.all_to_all(early, 'round', 2, 2, tiled=True).sum(axis=2)]
    ppermute x7 -> x14, starting transfers between devices: 28.1 us -> 46.3 us  [ring_stage(): lax.ppermute(acc_second, axis, behind) + take(second, (pos + step + 2) % n)]
    ppermute x7 -> x14, waiting for transfers between devices: 6.61 us -> 24.2 us  [ring_stage(): lax.ppermute(acc_second, axis, behind) + take(second, (pos + step + 2) % n)]
    all_to_all x1 -> x0, blocking collectives: 15 us -> none  [reduce_scatter_rows(): return lax.all_to_all(split, 'round', 1, 1, tiled=True).sum(axis=1)]
    all_to_all x0 -> x2, starting transfers between devices: none -> 10.5 us  [the longest x1 5.3 us: reduce_scatter_rows(): late = lax.all_to_all(late, 'round', 1, 1, tiled=True).sum(axis=1)]
    add x7 -> x14, other arithmetic: 10.4 us -> 0.19 us  [ring_stage(): lax.ppermute(acc_second, axis, behind) + take(second, (pos + step + 2) % n)]
    add x7 -> x14, other arithmetic: 8.87 us -> 0.19 us  [ring_stage(): lax.ppermute(acc_first, axis, ahead) + take(first, (pos - step - 2) % n)]
    ppermute x7 -> x14, waiting for transfers between devices: 19.5 us -> 11.7 us  [ring_stage(): lax.ppermute(acc_first, axis, ahead) + take(first, (pos - step - 2) % n)]
  transfers between devices with their start and end apart: 20 -> 36, of which waited for: 19 -> 36; matrix products, arithmetic and copies ran while one was open for 17% -> 5% of each run, Pallas kernels for 0% -> 0%
where the time goes in v5:
time: 242 us; the launch traced here: 239 us
  starting transfers between devices  85.9 us (35%)
  waiting for transfers between devices  81.9 us (34%)
  other arithmetic  25.1 us (10%)
  local copies, waits for them, and re-layouts  16.1 us (7%)
  matrix products  14.9 us (6%)
  Pallas kernels  13 us (5%)
    ppermute x14, starting transfers between devices, ring_stage(): lax.ppermute(acc_second, axis, behind) + take(second, (pos + step + 2) % n)  46.3 us
    ppermute x14, waiting for transfers between devices, ring_stage(): lax.ppermute(acc_second, axis, behind) + take(second, (pos + step + 2) % n)  24.2 us
    all_to_all x4, starting transfers between devices, entering(): everything = lax.all_to_all(copies, axis, 0, 0, tiled=True)  23.2 us
    all_to_all x4, waiting for transfers between devices, entering(): everything = lax.all_to_all(copies, axis, 0, 0, tiled=True)  22.1 us
    all_to_all x1, waiting for transfers between devices, reduce_scatter_rows(): early = lax.all_to_all(early, 'round', 2, 2, tiled=True).sum(axis=2)  17 us
    pallas_call x4, Pallas kernels, recurrence(): pl.pallas_call(functools.partial(_recurrence_kernel, reverse=reverse), ou...  13 us
    ppermute x14, waiting for transfers between devices, ring_stage(): lax.ppermute(acc_first, axis, ahead) + take(first, (pos - step - 2) % n)  11.7 us
    select_n x54, other arithmetic, entering(): state = tuple((jnp.where(reached, a, b) for a, b in zip(new, state)))  7.69 us
  transfers between devices with their start and end apart: 36, of which 36 were waited for; matrix products, arithmetic and copies ran while one was open for 5% of the time, Pallas kernels for 0%

profile of v5, /device:TPU:8, one launch (start us, length us, event | category | flops | bytes accessed | tf_op | source)
XLA Modules:
  0.0 238.9 jit_solution(500043087748111218)
XLA Ops:
  12.9 7.4 %all-to-all-start = ((f32[16,4,2,512]{3,2,1,0:T(2,128)}), f32[16,4,2,512]{3,2,1,0:T(2,128)S(1)}, u32[]{:S(2)}, u32[]{:S(2)}) async-start(f32[16,4,2,512]{3,2,1,0:T(2,128)} %broadcast_in_dim.10), calls=%async_computation | async-start | bytes 524288 | tf_op jit(solution)/shard_map/all_to_all | solution.py:73
  20.3 7.1 %all-to-all-done = f32[16,4,2,512]{3,2,1,0:T(2,128)S(1)} async-done(((f32[16,4,2,512]{3,2,1,0:T(2,128)}), f32[16,4,2,512]{3,2,1,0:T(2,128)S(1)}, u32[]{:S(2)}, u32[]{:S(2)}) %all-to-all-start) | async-done | bytes 262176 | tf_op jit(solution)/shard_map/all_to_all | solution.py:73
  38.6 5.5 %all-to-all-start.1 = ((f32[16,4,2,512]{3,2,1,0:T(2,128)}), f32[16,4,2,512]{3,2,1,0:T(2,128)}, u32[]{:S(2)}, u32[]{:S(2)}) async-start(f32[16,4,2,512]{3,2,1,0:T(2,128)} %broadcast_in_dim.11), calls=%async_computation.1 | async-start | bytes 524288 | tf_op jit(solution)/shard_map/all_to_all | solution.py:73
  44.1 8.0 %all-to-all-done.1 = f32[16,4,2,512]{3,2,1,0:T(2,128)} async-done(((f32[16,4,2,512]{3,2,1,0:T(2,128)}), f32[16,4,2,512]{3,2,1,0:T(2,128)}, u32[]{:S(2)}, u32[]{:S(2)}) %all-to-all-start.1) | async-done | bytes 262176 | tf_op jit(solution)/shard_map/all_to_all | solution.py:73
  70.5 5.2 %all-to-all-start.2 = ((f32[16,4,2,512]{3,2,1,0:T(2,128)}), f32[16,4,2,512]{3,2,1,0:T(2,128)S(1)}, u32[]{:S(2)}, u32[]{:S(2)}) async-start(f32[16,4,2,512]{3,2,1,0:T(2,128)} %broadcast_in_dim.12), calls=%async_computation.2 | async-start | bytes 524288 | tf_op jit(solution)/shard_map/all_to_all | solution.py:73
  79.0 3.6 %all-to-all-done.2 = f32[16,4,2,512]{3,2,1,0:T(2,128)S(1)} async-done(((f32[16,4,2,512]{3,2,1,0:T(2,128)}), f32[16,4,2,512]{3,2,1,0:T(2,128)S(1)}, u32[]{:S(2)}, u32[]{:S(2)}) %all-to-all-start.2) | async-done | bytes 262176 | tf_op jit(solution)/shard_map/all_to_all | solution.py:73
  98.1 5.2 %all-to-all-start.3 = ((f32[16,4,2,512]{3,2,1,0:T(2,128)}), f32[16,4,2,512]{3,2,1,0:T(2,128)S(1)}, u32[]{:S(2)}, u32[]{:S(2)}) async-start(f32[16,4,2,512]{3,2,1,0:T(2,128)} %broadcast_in_dim.13), calls=%async_computation.3 | async-start | bytes 524288 | tf_op jit(solution)/shard_map/all_to_all | solution.py:73
  115.3 6.1 %collective-permute-start.9 = (f32[1,128,256]{1,2,0:T(8,128)S(1)}, f32[1,128,256]{1,2,0:T(8,128)S(1)}, u32[]{:S(2)}, u32[]{:S(2)}) collective-permute-start(f32[1,128,256]{1,2,0:T(8,128)S(1)} %constant_dynamic-slice_fusion.2), channel_id=1, source_target_pairs={{0,224},{32,0},{64,32},{96,64},{128,96},{160,128},{192,160},{224,1... | collective-permute-start | bytes 393224 | tf_op jit(solution)/shard_map/ppermute | solution.py:105
  123.9 3.7 %collective-permute-start.10 = (f32[1,128,256]{1,2,0:T(8,128)S(1)}, f32[1,128,256]{1,2,0:T(8,128)S(1)}, u32[]{:S(2)}, u32[]{:S(2)}) collective-permute-start(f32[1,128,256]{1,2,0:T(8,128)S(1)} %dynamic-slice_add_fusion.6), channel_id=1, source_target_pairs={{0,224},{32,0},{64,32},{96,64},{128,96},{160,128},{192,160},{224,1... | collective-permute-start | bytes 393224 | tf_op jit(solution)/shard_map/ppermute | solution.py:105
  130.2 3.7 %collective-permute-start.11 = (f32[1,128,256]{1,2,0:T(8,128)S(1)}, f32[1,128,256]{1,2,0:T(8,128)S(1)}, u32[]{:S(2)}, u32[]{:S(2)}) collective-permute-start(f32[1,128,256]{1,2,0:T(8,128)S(1)} %dynamic-slice_add_fusion.5), channel_id=1, source_target_pairs={{0,224},{32,0},{64,32},{96,64},{128,96},{160,128},{192,160},{224,1... | collective-permute-start | bytes 393224 | tf_op jit(solution)/shard_map/ppermute | solution.py:105
  137.1 3.8 %collective-permute-start.12 = (f32[1,128,256]{1,2,0:T(8,128)S(1)}, f32[1,128,256]{1,2,0:T(8,128)S(1)}, u32[]{:S(2)}, u32[]{:S(2)}) collective-permute-start(f32[1,128,256]{1,2,0:T(8,128)S(1)} %dynamic-slice_add_fusion.4), channel_id=1, source_target_pairs={{0,224},{32,0},{64,32},{96,64},{128,96},{160,128},{192,160},{224,1... | collective-permute-start | bytes 393224 | tf_op jit(solution)/shard_map/ppermute | solution.py:105
  144.4 3.8 %collective-permute-start.13 = (f32[1,128,256]{1,2,0:T(8,128)S(1)}, f32[1,128,256]{1,2,0:T(8,128)S(1)}, u32[]{:S(2)}, u32[]{:S(2)}) collective-permute-start(f32[1,128,256]{1,2,0:T(8,128)S(1)} %dynamic-slice_add_fusion.3), channel_id=1, source_target_pairs={{0,224},{32,0},{64,32},{96,64},{128,96},{160,128},{192,160},{224,1... | collective-permute-start | bytes 393224 | tf_op jit(solution)/shard_map/ppermute | solution.py:105
  150.8 3.8 %collective-permute-start.14 = (f32[1,128,256]{1,2,0:T(8,128)S(1)}, f32[1,128,256]{1,2,0:T(8,128)S(1)}, u32[]{:S(2)}, u32[]{:S(2)}) collective-permute-start(f32[1,128,256]{1,2,0:T(8,128)S(1)} %dynamic-slice_add_fusion.2), channel_id=1, source_target_pairs={{0,224},{32,0},{64,32},{96,64},{128,96},{160,128},{192,160},{224,1... | collective-permute-start | bytes 393224 | tf_op jit(solution)/shard_map/ppermute | solution.py:105
  157.1 3.7 %collective-permute-start.15 = (f32[1,128,256]{1,2,0:T(8,128)S(1)}, f32[1,128,256]{1,2,0:T(8,128)S(1)}, u32[]{:S(2)}, u32[]{:S(2)}) collective-permute-start(f32[1,128,256]{1,2,0:T(8,128)S(1)} %dynamic-slice_add_fusion.1), channel_id=1, source_target_pairs={{0,224},{32,0},{64,32},{96,64},{128,96},{160,128},{192,160},{224,1... | collective-permute-start | bytes 393224 | tf_op jit(solution)/shard_map/ppermute | solution.py:105
  163.4 4.2 %collective-permute-done.8 = f32[1,128,256]{1,2,0:T(8,128)S(1)} collective-permute-done((f32[1,128,256]{1,2,0:T(8,128)S(1)}, f32[1,128,256]{1,2,0:T(8,128)S(1)}, u32[]{:S(2)}, u32[]{:S(2)}) %collective-permute-start.8) | collective-permute-done | bytes 131104 | tf_op jit(solution)/shard_map/ppermute | solution.py:104
  168.5 5.3 %all-to-all-start.4 = ((f32[1,16,8,512]{3,2,0,1:T(8,128)}), f32[1,16,8,512]{3,2,0,1:T(8,128)S(1)}, u32[]{:S(2)}, u32[]{:S(2)}) async-start(f32[1,16,8,512]{3,2,0,1:T(8,128)} %bitcast.2640), calls=%async_computation.4 | async-start | bytes 524288 | tf_op jit(solution)/shard_map/all_to_all | solution.py:121
  177.1 3.9 %all-to-all-done.4 = f32[1,16,8,512]{3,2,0,1:T(8,128)S(1)} async-done(((f32[1,16,8,512]{3,2,0,1:T(8,128)}), f32[1,16,8,512]{3,2,0,1:T(8,128)S(1)}, u32[]{:S(2)}, u32[]{:S(2)}) %all-to-all-start.4) | async-done | bytes 262176 | tf_op jit(solution)/shard_map/all_to_all | solution.py:121
  181.0 5.2 %all-to-all-start.5 = ((f32[1,8,16,8,512]{4,3,1,0,2:T(8,128)}), f32[1,8,16,8,512]{4,3,1,0,2:T(8,128)S(1)}, u32[]{:S(2)}, u32[]{:S(2)}) async-start(f32[1,8,16,8,512]{4,3,1,0,2:T(8,128)} %copy.59), calls=%async_computation.5 | async-start | bytes 4194304 | tf_op jit(solution)/shard_map/all_to_all | solution.py:115
  186.8 17.0 %all-to-all-done.5 = f32[1,8,16,8,512]{4,3,1,0,2:T(8,128)S(1)} async-done(((f32[1,8,16,8,512]{4,3,1,0,2:T(8,128)}), f32[1,8,16,8,512]{4,3,1,0,2:T(8,128)S(1)}, u32[]{:S(2)}, u32[]{:S(2)}) %all-to-all-start.5) | async-done | bytes 2097184 | tf_op jit(solution)/shard_map/all_to_all | solution.py:115
  215.2 3.5 %collective-permute-start.26 = (f32[1,8,256]{2,1,0:T(8,128)S(1)}, f32[1,8,256]{2,1,0:T(8,128)S(1)}, u32[]{:S(2)}, u32[]{:S(2)}) collective-permute-start(f32[1,8,256]{2,1,0:T(8,128)S(1)} %dynamic-slice_add_fusion.18), channel_id=1, source_target_pairs={{0,224},{32,0},{64,32},{96,64},{128,96},{160,128},{192,160},{224,1... | collective-permute-start | bytes 24584 | tf_op jit(solution)/shard_map/ppermute | solution.py:105
  220.1 3.5 %collective-permute-start.27 = (f32[1,8,256]{2,1,0:T(8,128)S(1)}, f32[1,8,256]{2,1,0:T(8,128)S(1)}, u32[]{:S(2)}, u32[]{:S(2)}) collective-permute-start(f32[1,8,256]{2,1,0:T(8,128)S(1)} %dynamic-slice_add_fusion.17), channel_id=1, source_target_pairs={{0,224},{32,0},{64,32},{96,64},{128,96},{160,128},{192,160},{224,1... | collective-permute-start | bytes 24584 | tf_op jit(solution)/shard_map/ppermute | solution.py:105
  224.9 3.5 %collective-permute-start.28 = (f32[1,8,256]{2,1,0:T(8,128)S(1)}, f32[1,8,256]{2,1,0:T(8,128)S(1)}, u32[]{:S(2)}, u32[]{:S(2)}) collective-permute-start(f32[1,8,256]{2,1,0:T(8,128)S(1)} %dynamic-slice_add_fusion.16), channel_id=1, source_target_pairs={{0,224},{32,0},{64,32},{96,64},{128,96},{160,128},{192,160},{224,1... | collective-permute-start | bytes 24584 | tf_op jit(solution)/shard_map/ppermute | solution.py:105
  229.8 3.5 %collective-permute-start.29 = (f32[1,8,256]{2,1,0:T(8,128)S(1)}, f32[1,8,256]{2,1,0:T(8,128)S(1)}, u32[]{:S(2)}, u32[]{:S(2)}) collective-permute-start(f32[1,8,256]{2,1,0:T(8,128)S(1)} %dynamic-slice_add_fusion.15), channel_id=1, source_target_pairs={{0,224},{32,0},{64,32},{96,64},{128,96},{160,128},{192,160},{224,1... | collective-permute-start | bytes 24584 | tf_op jit(solution)/shard_map/ppermute | solution.py:105
  234.7 3.6 %collective-permute-done.22 = f32[1,8,256]{2,1,0:T(8,128)S(1)} collective-permute-done((f32[1,8,256]{2,1,0:T(8,128)S(1)}, f32[1,8,256]{2,1,0:T(8,128)S(1)}, u32[]{:S(2)}, u32[]{:S(2)}) %collective-permute-start.22) | collective-permute-done | bytes 8224 | tf_op jit(solution)/shard_map/ppermute | solution.py:104
  (233 shorter events, 113.3 us)
Async XLA Ops:
  12.9 14.5 %all-to-all-start = ((f32[16,4,2,512]{3,2,1,0:T(2,128)}), f32[16,4,2,512]{3,2,1,0:T(2,128)S(1)}, u32[]{:S(2)}, u32[]{:S(2)}) async-start(f32[16,4,2,512]{3,2,1,0:T(2,128)} %broadcast_in_dim.10), calls=%async_computation | async-start | bytes 524288 | tf_op jit(solution)/shard_map/all_to_all | solution.py:73
  38.6 13.4 %all-to-all-start.1 = ((f32[16,4,2,512]{3,2,1,0:T(2,128)}), f32[16,4,2,512]{3,2,1,0:T(2,128)}, u32[]{:S(2)}, u32[]{:S(2)}) async-start(f32[16,4,2,512]{3,2,1,0:T(2,128)} %broadcast_in_dim.11), calls=%async_computation.1 | async-start | bytes 524288 | tf_op jit(solution)/shard_map/all_to_all | solution.py:73
  70.5 12.1 %all-to-all-start.2 = ((f32[16,4,2,512]{3,2,1,0:T(2,128)}), f32[16,4,2,512]{3,2,1,0:T(2,128)S(1)}, u32[]{:S(2)}, u32[]{:S(2)}) async-start(f32[16,4,2,512]{3,2,1,0:T(2,128)} %broadcast_in_dim.12), calls=%async_computation.2 | async-start | bytes 524288 | tf_op jit(solution)/shard_map/all_to_all | solution.py:73
  98.1 12.6 %all-to-all-start.3 = ((f32[16,4,2,512]{3,2,1,0:T(2,128)}), f32[16,4,2,512]{3,2,1,0:T(2,128)S(1)}, u32[]{:S(2)}, u32[]{:S(2)}) async-start(f32[16,4,2,512]{3,2,1,0:T(2,128)} %broadcast_in_dim.13), calls=%async_computation.3 | async-start | bytes 524288 | tf_op jit(solution)/shard_map/all_to_all | solution.py:73
  115.3 8.6 %collective-permute-start.9 = (f32[1,128,256]{1,2,0:T(8,128)S(1)}, f32[1,128,256]{1,2,0:T(8,128)S(1)}, u32[]{:S(2)}, u32[]{:S(2)}) collective-permute-start(f32[1,128,256]{1,2,0:T(8,128)S(1)} %constant_dynamic-slice_fusion.2), channel_id=1, source_target_pairs={{0,224},{32,0},{64,32},{96,64},{128,96},{160,128},{192,160},{224,1... | collective-permute-start | bytes 393224 | tf_op jit(solution)/shard_map/ppermute | solution.py:105
  122.0 6.3 %collective-permute-start.2 = (f32[1,128,256]{1,2,0:T(8,128)S(1)}, f32[1,128,256]{1,2,0:T(8,128)S(1)}, u32[]{:S(2)}, u32[]{:S(2)}) collective-permute-start(f32[1,128,256]{1,2,0:T(8,128)S(1)} %constant_dynamic-slice_fusion.3), channel_id=1, source_target_pairs={{0,32},{32,64},{64,96},{96,128},{128,160},{160,192},{192,224},{224... | collective-permute-start | bytes 393224 | tf_op jit(solution)/shard_map/ppermute | solution.py:104
  123.9 6.3 %collective-permute-start.10 = (f32[1,128,256]{1,2,0:T(8,128)S(1)}, f32[1,128,256]{1,2,0:T(8,128)S(1)}, u32[]{:S(2)}, u32[]{:S(2)}) collective-permute-start(f32[1,128,256]{1,2,0:T(8,128)S(1)} %dynamic-slice_add_fusion.6), channel_id=1, source_target_pairs={{0,224},{32,0},{64,32},{96,64},{128,96},{160,128},{192,160},{224,1... | collective-permute-start | bytes 393224 | tf_op jit(solution)/shard_map/ppermute | solution.py:105
  128.3 6.3 %collective-permute-start.3 = (f32[1,128,256]{1,2,0:T(8,128)S(1)}, f32[1,128,256]{1,2,0:T(8,128)S(1)}, u32[]{:S(2)}, u32[]{:S(2)}) collective-permute-start(f32[1,128,256]{1,2,0:T(8,128)S(1)} %dynamic-slice_add_fusion.13), channel_id=1, source_target_pairs={{0,32},{32,64},{64,96},{96,128},{128,160},{160,192},{192,224},{224... | collective-permute-start | bytes 393224 | tf_op jit(solution)/shard_map/ppermute | solution.py:104
  130.2 6.9 %collective-permute-start.11 = (f32[1,128,256]{1,2,0:T(8,128)S(1)}, f32[1,128,256]{1,2,0:T(8,128)S(1)}, u32[]{:S(2)}, u32[]{:S(2)}) collective-permute-start(f32[1,128,256]{1,2,0:T(8,128)S(1)} %dynamic-slice_add_fusion.5), channel_id=1, source_target_pairs={{0,224},{32,0},{64,32},{96,64},{128,96},{160,128},{192,160},{224,1... | collective-permute-start | bytes 393224 | tf_op jit(solution)/shard_map/ppermute | solution.py:105
  134.5 7.2 %collective-permute-start.4 = (f32[1,128,256]{1,2,0:T(8,128)S(1)}, f32[1,128,256]{1,2,0:T(8,128)S(1)}, u32[]{:S(2)}, u32[]{:S(2)}) collective-permute-start(f32[1,128,256]{1,2,0:T(8,128)S(1)} %dynamic-slice_add_fusion.12), channel_id=1, source_target_pairs={{0,32},{32,64},{64,96},{96,128},{128,160},{160,192},{192,224},{224... | collective-permute-start | bytes 393224 | tf_op jit(solution)/shard_map/ppermute | solution.py:104
  137.1 7.2 %collective-permute-start.12 = (f32[1,128,256]{1,2,0:T(8,128)S(1)}, f32[1,128,256]{1,2,0:T(8,128)S(1)}, u32[]{:S(2)}, u32[]{:S(2)}) collective-permute-start(f32[1,128,256]{1,2,0:T(8,128)S(1)} %dynamic-slice_add_fusion.4), channel_id=1, source_target_pairs={{0,224},{32,0},{64,32},{96,64},{128,96},{160,128},{192,160},{224,1... | collective-permute-start | bytes 393224 | tf_op jit(solution)/shard_map/ppermute | solution.py:105
  141.8 7.0 %collective-permute-start.5 = (f32[1,128,256]{1,2,0:T(8,128)S(1)}, f32[1,128,256]{1,2,0:T(8,128)S(1)}, u32[]{:S(2)}, u32[]{:S(2)}) collective-permute-start(f32[1,128,256]{1,2,0:T(8,128)S(1)} %dynamic-slice_add_fusion.11), channel_id=1, source_target_pairs={{0,32},{32,64},{64,96},{96,128},{128,160},{160,192},{192,224},{224... | collective-permute-start | bytes 393224 | tf_op jit(solution)/shard_map/ppermute | solution.py:104
  144.4 6.4 %collective-permute-start.13 = (f32[1,128,256]{1,2,0:T(8,128)S(1)}, f32[1,128,256]{1,2,0:T(8,128)S(1)}, u32[]{:S(2)}, u32[]{:S(2)}) collective-permute-start(f32[1,128,256]{1,2,0:T(8,128)S(1)} %dynamic-slice_add_fusion.3), channel_id=1, source_target_pairs={{0,224},{32,0},{64,32},{96,64},{128,96},{160,128},{192,160},{224,1... | collective-permute-start | bytes 393224 | tf_op jit(solution)/shard_map/ppermute | solution.py:105
  148.8 6.3 %collective-permute-start.6 = (f32[1,128,256]{1,2,0:T(8,128)S(1)}, f32[1,128,256]{1,2,0:T(8,128)S(1)}, u32[]{:S(2)}, u32[]{:S(2)}) collective-permute-start(f32[1,128,256]{1,2,0:T(8,128)S(1)} %dynamic-slice_add_fusion.10), channel_id=1, source_target_pairs={{0,32},{32,64},{64,96},{96,128},{128,160},{160,192},{192,224},{224... | collective-permute-start | bytes 393224 | tf_op jit(solution)/shard_map/ppermute | solution.py:104
  150.8 6.3 %collective-permute-start.14 = (f32[1,128,256]{1,2,0:T(8,128)S(1)}, f32[1,128,256]{1,2,0:T(8,128)S(1)}, u32[]{:S(2)}, u32[]{:S(2)}) collective-permute-start(f32[1,128,256]{1,2,0:T(8,128)S(1)} %dynamic-slice_add_fusion.2), channel_id=1, source_target_pairs={{0,224},{32,0},{64,32},{96,64},{128,96},{160,128},{192,160},{224,1... | collective-permute-start | bytes 393224 | tf_op jit(solution)/shard_map/ppermute | solution.py:105
  155.1 6.3 %collective-permute-start.7 = (f32[1,128,256]{1,2,0:T(8,128)S(1)}, f32[1,128,256]{1,2,0:T(8,128)S(1)}, u32[]{:S(2)}, u32[]{:S(2)}) collective-permute-start(f32[1,128,256]{1,2,0:T(8,128)S(1)} %dynamic-slice_add_fusion.9), channel_id=1, source_target_pairs={{0,32},{32,64},{64,96},{96,128},{128,160},{160,192},{192,224},{224... | collective-permute-start | bytes 393224 | tf_op jit(solution)/shard_map/ppermute | solution.py:104
  157.1 6.3 %collective-permute-start.15 = (f32[1,128,256]{1,2,0:T(8,128)S(1)}, f32[1,128,256]{1,2,0:T(8,128)S(1)}, u32[]{:S(2)}, u32[]{:S(2)}) collective-permute-start(f32[1,128,256]{1,2,0:T(8,128)S(1)} %dynamic-slice_add_fusion.1), channel_id=1, source_target_pairs={{0,224},{32,0},{64,32},{96,64},{128,96},{160,128},{192,160},{224,1... | collective-permute-start | bytes 393224 | tf_op jit(solution)/shard_map/ppermute | solution.py:105
  161.3 6.3 %collective-permute-start.8 = (f32[1,128,256]{1,2,0:T(8,128)S(1)}, f32[1,128,256]{1,2,0:T(8,128)S(1)}, u32[]{:S(2)}, u32[]{:S(2)}) collective-permute-start(f32[1,128,256]{1,2,0:T(8,128)S(1)} %dynamic-slice_add_fusion.8), channel_id=1, source_target_pairs={{0,32},{32,64},{64,96},{96,128},{128,160},{160,192},{192,224},{224... | collective-permute-start | bytes 393224 | tf_op jit(solution)/shard_map/ppermute | solution.py:104
  168.5 12.5 %all-to-all-start.4 = ((f32[1,16,8,512]{3,2,0,1:T(8,128)}), f32[1,16,8,512]{3,2,0,1:T(8,128)S(1)}, u32[]{:S(2)}, u32[]{:S(2)}) async-start(f32[1,16,8,512]{3,2,0,1:T(8,128)} %bitcast.2640), calls=%async_computation.4 | async-start | bytes 524288 | tf_op jit(solution)/shard_map/all_to_all | solution.py:121
  181.0 22.8 %all-to-all-start.5 = ((f32[1,8,16,8,512]{4,3,1,0,2:T(8,128)}), f32[1,8,16,8,512]{4,3,1,0,2:T(8,128)S(1)}, u32[]{:S(2)}, u32[]{:S(2)}) async-start(f32[1,8,16,8,512]{4,3,1,0,2:T(8,128)} %copy.59), calls=%async_computation.5 | async-start | bytes 4194304 | tf_op jit(solution)/shard_map/all_to_all | solution.py:115
  204.1 4.9 %collective-permute-start.16 = (f32[1,8,256]{2,1,0:T(8,128)S(1)}, f32[1,8,256]{2,1,0:T(8,128)S(1)}, u32[]{:S(2)}, u32[]{:S(2)}) collective-permute-start(f32[1,8,256]{2,1,0:T(8,128)S(1)} %constant_dynamic-slice_fusion.1), channel_id=1, source_target_pairs={{0,32},{32,64},{64,96},{96,128},{128,160},{160,192},{192,224},{224... | collective-permute-start | bytes 24584 | tf_op jit(solution)/shard_map/ppermute | solution.py:104
  209.1 4.9 %collective-permute-start.17 = (f32[1,8,256]{2,1,0:T(8,128)S(1)}, f32[1,8,256]{2,1,0:T(8,128)S(1)}, u32[]{:S(2)}, u32[]{:S(2)}) collective-permute-start(f32[1,8,256]{2,1,0:T(8,128)S(1)} %dynamic-slice_add_fusion.27), channel_id=1, source_target_pairs={{0,32},{32,64},{64,96},{96,128},{128,160},{160,192},{192,224},{224... | collective-permute-start | bytes 24584 | tf_op jit(solution)/shard_map/ppermute | solution.py:104
  213.9 4.9 %collective-permute-start.18 = (f32[1,8,256]{2,1,0:T(8,128)S(1)}, f32[1,8,256]{2,1,0:T(8,128)S(1)}, u32[]{:S(2)}, u32[]{:S(2)}) collective-permute-start(f32[1,8,256]{2,1,0:T(8,128)S(1)} %dynamic-slice_add_fusion.26), channel_id=1, source_target_pairs={{0,32},{32,64},{64,96},{96,128},{128,160},{160,192},{192,224},{224... | collective-permute-start | bytes 24584 | tf_op jit(solution)/shard_map/ppermute | solution.py:104
  215.2 4.9 %collective-permute-start.26 = (f32[1,8,256]{2,1,0:T(8,128)S(1)}, f32[1,8,256]{2,1,0:T(8,128)S(1)}, u32[]{:S(2)}, u32[]{:S(2)}) collective-permute-start(f32[1,8,256]{2,1,0:T(8,128)S(1)} %dynamic-slice_add_fusion.18), channel_id=1, source_target_pairs={{0,224},{32,0},{64,32},{96,64},{128,96},{160,128},{192,160},{224,1... | collective-permute-start | bytes 24584 | tf_op jit(solution)/shard_map/ppermute | solution.py:105
  (31 other events, 206.2 us)

commit v6 on v4

--- a/solution.py
+++ b/solution.py
@@ -39,14 +39,15 @@
     zero = jnp.zeros((1, width), jnp.float32)
     start = (jnp.ones((1, width), jnp.float32), zero, tuple((zero, zero) for _ in range(shots)))
     p_re, p_im, states = lax.fori_loop(0, rounds, step, start, unroll=8)
-    for b in range(shots):
-        end_ref[0, pl.ds(b, 1), :] = p_re
-        end_ref[1, pl.ds(b, 1), :] = p_im
-        end_ref[2, pl.ds(b, 1), :] = states[b][0]
-        end_ref[3, pl.ds(b, 1), :] = states[b][1]
-
-
-def recurrence(a_re, a_im, d_re, d_im, reverse=False):
+    for copy in range(end_ref.shape[0]):
+        for b in range(shots):
+            end_ref[copy, 0, pl.ds(b, 1), :] = p_re
+            end_ref[copy, 1, pl.ds(b, 1), :] = p_im
+            end_ref[copy, 2, pl.ds(b, 1), :] = states[b][0]
+            end_ref[copy, 3, pl.ds(b, 1), :] = states[b][1]
+
+
+def recurrence(a_re, a_im, d_re, d_im, reverse=False, copies=1):
     rounds, width = a_re.shape
     shots = d_re.shape[0]
     vmem = pl.BlockSpec(memory_space=pltpu.VMEM)
@@ -54,7 +55,7 @@
     state = jax.ShapeDtypeStruct((shots, rounds, width), jnp.float32)
     return pl.pallas_call(
         functools.partial(_recurrence_kernel, reverse=reverse),
-        out_shape=(coeff, coeff, state, state, jax.ShapeDtypeStruct((4, shots, width), jnp.float32)),
+        out_shape=(coeff, coeff, state, state, jax.ShapeDtypeStruct((copies, 4, shots, width), jnp.float32)),
         in_specs=[vmem] * 4,
         out_specs=(vmem,) * 5,
         cost_estimate=pl.CostEstimate(
@@ -67,9 +68,9 @@
 
 def entering(shard, axis, combine, identity, reverse):
     peers, position = (lax.axis_size(axis), lax.axis_index(axis))
+    copies = shard
+    shard = tuple(copies[0, i] for i in range(copies.shape[1]))
     common = jnp.broadcast_shapes(*(part.shape for part in shard))
-    stacked = jnp.stack([jnp.broadcast_to(part, common) for part in shard])
-    copies = jnp.broadcast_to(stacked[None], (peers,) + stacked.shape)
     everything = lax.all_to_all(copies, axis, 0, 0, tiled=True)
     state = tuple(
         jnp.broadcast_to(jnp.asarray(zero, part.dtype), common) for part, zero in zip(shard, identity)
@@ -160,11 +161,10 @@
     drive_real = driven[:, :, :feature_count] * input_gain
     drive_imag = driven[:, :, feature_count:] * input_gain
     prod_real, prod_imag, local_real, local_imag, ends = recurrence(
-        trans_real, trans_imag, drive_real, drive_imag
+        trans_real, trans_imag, drive_real, drive_imag, copies=lax.axis_size("round")
     )
     prod_real, prod_imag = (prod_real[None], prod_imag[None])
-    summary = (ends[0], ends[1], ends[2], ends[3])
-    carried = incoming_state(summary, neutral_of(summary))
+    carried = incoming_state(ends, neutral_of(tuple(ends[0, i] for i in range(4))))
     carry_real = carried[2][:, None]
     carry_imag = carried[3][:, None]
     state_real = local_real + prod_real * carry_real - prod_imag * carry_imag
@@ -200,11 +200,10 @@
     pushed_real = back_real * error_real - back_imag * error_imag
     pushed_imag = back_real * error_imag + back_imag * error_real
     suffix_real, suffix_imag, local_real, local_imag, ends = recurrence(
-        back_real[0], back_imag[0], pushed_real, pushed_imag, reverse=True
+        back_real[0], back_imag[0], pushed_real, pushed_imag, reverse=True, copies=lax.axis_size("round")
     )
     suffix_real, suffix_imag = (suffix_real[None], suffix_imag[None])
-    summary = (ends[0], ends[1], ends[2], ends[3])
-    carried = incoming_adjoint(summary, neutral_of(summary))
+    carried = incoming_adjoint(ends, neutral_of(tuple(ends[0, i] for i in range(4))))
     carry_real = carried[2][:, None]
     carry_imag = carried[3][:, None]
     passed_real = local_real + suffix_real * carry_real - suffix_imag * carry_imag

time: 205 us -> 199 us (0.971)
  local copies, waits for them, and re-layouts: 16.4 us -> 10.2 us
    broadcast_in_dim x4 -> x0, local copies, waits for them, and re-layouts: 6.24 us -> none  [entering(): copies = jnp.broadcast_to(stacked[None], (peers,) + stacked.shape)]
where the time goes in v6:
time: 199 us; the launch traced here: 198 us
  starting transfers between devices  56 us (28%)
  waiting for transfers between devices  43 us (22%)
  other arithmetic  42.9 us (22%)
  matrix products  15.4 us (8%)
  blocking collectives  15 us (8%)
  Pallas kernels  13.5 us (7%)
  local copies, waits for them, and re-layouts  10.2 us (5%)
    ppermute x7, starting transfers between devices, ring_stage(): lax.ppermute(acc_second, axis, behind) + take(second, (pos + step + 2) % n)  28.1 us
    all_to_all x4, starting transfers between devices, entering(): everything = lax.all_to_all(copies, axis, 0, 0, tiled=True)  24.7 us
    ppermute x7, waiting for transfers between devices, ring_stage(): lax.ppermute(acc_first, axis, ahead) + take(first, (pos - step - 2) % n)  19.5 us
    all_to_all x4, waiting for transfers between devices, entering(): everything = lax.all_to_all(copies, axis, 0, 0, tiled=True)  15.5 us
    all_to_all x1, blocking collectives, reduce_scatter_rows(): return lax.all_to_all(split, 'round', 1, 1, tiled=True).sum(axis=1)  15 us
    pallas_call x4, Pallas kernels, recurrence(): pl.pallas_call(functools.partial(_recurrence_kernel, reverse=reverse), ou...  13.5 us
    add x7, other arithmetic, ring_stage(): lax.ppermute(acc_second, axis, behind) + take(second, (pos + step + 2) % n)  10.4 us
    add x7, other arithmetic, ring_stage(): lax.ppermute(acc_first, axis, ahead) + take(first, (pos - step - 2) % n)  8.87 us
  transfers between devices with their start and end apart: 20, of which 19 were waited for; matrix products, arithmetic and copies ran while one was open for 17% of the time, Pallas kernels for 0%

profile of v6, /device:TPU:8, one launch (start us, length us, event | category | flops | bytes accessed | tf_op | source)
XLA Modules:
  0.0 197.6 jit_solution(10261995874119654656)
XLA Ops:
  8.1 3.4 %shard_map.104 = (f32[128,512]{1,0:T(8,128)}, f32[128,512]{1,0:T(8,128)}, f32[2,128,512]{2,1,0:T(8,128)}, f32[2,128,512]{2,1,0:T(8,128)}, f32[16,4,2,512]{3,2,1,0:T(2,128)}) custom-call(f32[128,512]{1,0:T(8,128)} %get-tuple-element.215.a_re_ref, f32[128,512]{1,0:T(8,128)} %get-tuple-element.214.a_im_ref, f32[2,128,512]{2,1,0:T(8,128)} %get-tuple-element.198.d_re_ref, ...), custom_call_target="tpu_custom_call" | custom-call | flops 1572864 | bytes 3145728 | tf_op jit(solution)/shard_map/pallas_call | solution.py:56
  11.5 7.4 %all-to-all-start = ((f32[16,4,2,512]{3,2,1,0:T(2,128)}), f32[16,4,2,512]{3,2,1,0:T(2,128)S(1)}, u32[]{:S(2)}, u32[]{:S(2)}) async-start(f32[16,4,2,512]{3,2,1,0:T(2,128)} %get-tuple-element.24), calls=%async_computation | async-start | bytes 524288 | tf_op jit(solution)/shard_map/all_to_all | solution.py:74
  18.9 7.1 %all-to-all-done = f32[16,4,2,512]{3,2,1,0:T(2,128)S(1)} async-done(((f32[16,4,2,512]{3,2,1,0:T(2,128)}), f32[16,4,2,512]{3,2,1,0:T(2,128)S(1)}, u32[]{:S(2)}, u32[]{:S(2)}) %all-to-all-start) | async-done | bytes 262176 | tf_op jit(solution)/shard_map/all_to_all | solution.py:74
  32.6 3.4 %shard_map.105 = (f32[128,512]{1,0:T(8,128)}, f32[128,512]{1,0:T(8,128)}, f32[2,128,512]{2,1,0:T(8,128)}, f32[2,128,512]{2,1,0:T(8,128)}, f32[16,4,2,512]{3,2,1,0:T(2,128)}) custom-call(f32[128,512]{1,0:T(8,128)} %get-tuple-element.215.a_re_ref, f32[128,512]{1,0:T(8,128)} %get-tuple-element.214.a_im_ref, f32[2,128,512]{2,1,0:T(8,128)} %get-tuple-element.196.d_re_ref, ...), custom_call_target="tpu_custom_call" | custom-call | flops 1572864 | bytes 3145728 | tf_op jit(solution)/shard_map/pallas_call | solution.py:56
  35.9 5.4 %all-to-all-start.1 = ((f32[16,4,2,512]{3,2,1,0:T(2,128)}), f32[16,4,2,512]{3,2,1,0:T(2,128)}, u32[]{:S(2)}, u32[]{:S(2)}) async-start(f32[16,4,2,512]{3,2,1,0:T(2,128)} %get-tuple-element.29), calls=%async_computation.1 | async-start | bytes 524288 | tf_op jit(solution)/shard_map/all_to_all | solution.py:74
  41.5 7.9 %all-to-all-done.1 = f32[16,4,2,512]{3,2,1,0:T(2,128)} async-done(((f32[16,4,2,512]{3,2,1,0:T(2,128)}), f32[16,4,2,512]{3,2,1,0:T(2,128)}, u32[]{:S(2)}, u32[]{:S(2)}) %all-to-all-start.1) | async-done | bytes 262176 | tf_op jit(solution)/shard_map/all_to_all | solution.py:74
  56.1 2.4 %subtract_convert_fusion = (bf16[2,128,512]{2,1,0:T(8,128)(2,1)}, bf16[2,128,512]{2,1,0:T(8,128)(2,1)}) fusion(f32[2,128,512]{2,1,0:T(8,128)} %get-tuple-element.27, f32[2,512]{1,0:T(2,128)S(1)} %fusion.64, f32[128,512]{1,0:T(8,128)} %get-tuple-element.30, f32[2,512]{1,0:T(2,128)S(1)} %get-tuple-element.137, f32[128,512]{1,0:T(8,128)} %get-tuple-element.28, ...), kind=kLoop, calls=%fused_computation.76 | loop fusion | flops 1310720 | bytes 2105344 | tf_op jit(solution)/shard_map/convert
  63.0 3.3 %shard_map.106 = (f32[128,512]{1,0:T(8,128)}, f32[128,512]{1,0:T(8,128)}, f32[2,128,512]{2,1,0:T(8,128)}, f32[2,128,512]{2,1,0:T(8,128)}, f32[16,4,2,512]{3,2,1,0:T(2,128)}) custom-call(f32[128,512]{1,0:T(8,128)} %get-tuple-element.215.a_re_ref, f32[128,512]{1,0:T(8,128)} %copy-done.5, f32[2,128,512]{2,1,0:T(8,128)} %get-tuple-element.190.d_re_ref, ...), custom_call_target="tpu_custom_call" | custom-call | flops 1572864 | bytes 3145728 | tf_op jit(solution)/shard_map/pallas_call | solution.py:56
  66.3 5.2 %all-to-all-start.2 = ((f32[16,4,2,512]{3,2,1,0:T(2,128)}), f32[16,4,2,512]{3,2,1,0:T(2,128)S(1)}, u32[]{:S(2)}, u32[]{:S(2)}) async-start(f32[16,4,2,512]{3,2,1,0:T(2,128)} %get-tuple-element.34), calls=%async_computation.2 | async-start | bytes 524288 | tf_op jit(solution)/shard_map/all_to_all | solution.py:74
  74.8 3.1 %fusion.42 = f32[1024,512,1]{1,0,2:T(8,128)} fusion(f32[512]{0:T(512)S(1)} %convert_element_type.76, f32[2,128]{1,0:T(2,128)S(1)} %fusion.429, pred[]{:T(512)S(6)} %eq.21, bf16[2,128,512]{2,1,0:T(8,128)(2,1)} %get-tuple-element.204, bf16[2,128,512]{2,1,0:T(8,128)(2,1)} %get-tuple-element.203, bf16[2,128,512]{2,1,0:T(8,128)(2,1)} %copy-done.15, ...), kind=kOutput, calls=%fused_computation.82 | convolution fusion | flops 271187968 | bytes 3148801 | tf_op jit(solution)/shard_map/brk,brw->kw/dot_general | solution.py:192
  87.2 3.4 %shard_map.107 = (f32[128,512]{1,0:T(8,128)}, f32[128,512]{1,0:T(8,128)}, f32[2,128,512]{2,1,0:T(8,128)}, f32[2,128,512]{2,1,0:T(8,128)}, f32[16,4,2,512]{3,2,1,0:T(2,128)}) custom-call(f32[128,512]{1,0:T(8,128)} %get-tuple-element.215.a_re_ref, f32[128,512]{1,0:T(8,128)} %copy-done.5, f32[2,128,512]{2,1,0:T(8,128)} %get-tuple-element.188.d_re_ref, ...), custom_call_target="tpu_custom_call" | custom-call | flops 1572864 | bytes 3145728 | tf_op jit(solution)/shard_map/pallas_call | solution.py:56
  90.6 6.7 %all-to-all-start.3 = ((f32[16,4,2,512]{3,2,1,0:T(2,128)}), f32[16,4,2,512]{3,2,1,0:T(2,128)S(1)}, u32[]{:S(2)}, u32[]{:S(2)}) async-start(f32[16,4,2,512]{3,2,1,0:T(2,128)} %get-tuple-element.39), calls=%async_computation.3 | async-start | bytes 524288 | tf_op jit(solution)/shard_map/all_to_all | solution.py:74
  97.3 2.4 %bitcast_add_fusion = f32[1024,512]{1,0:T(8,128)S(1)} fusion(f32[1024,512,1]{1,0,2:T(8,128)} %fusion.42, bf16[2,128,512]{2,1,0:T(8,128)(2,1)S(1)} %copy-done.12, pred[]{:T(512)S(6)} %eq.21, bf16[2,128,512]{2,1,0:T(8,128)(2,1)} %get-tuple-element.204, bf16[2,128,512]{2,1,0:T(8,128)(2,1)} %get-tuple-element.203, bf16[2,128,512]{2,1,0:T(8,128)(2,1)} %copy-done.15, ...), kind=kOutput, calls=%fused_computation | convolution fusion | flops 271712256 | bytes 5505025 | tf_op jit(solution)/shard_map/brk,brw->kw/dot_general | solution.py:192
  101.9 5.9 %collective-permute-start.9 = (f32[1,128,512]{2,1,0:T(8,128)}, f32[1,128,512]{2,1,0:T(8,128)}, u32[]{:S(2)}, u32[]{:S(2)}) collective-permute-start(f32[1,128,512]{2,1,0:T(8,128)} %dynamic-slice_bitcast_fusion), channel_id=1, source_target_pairs={{0,224},{32,0},{64,32},{96,64},{128,96},{160,128},{192,160},{224,1... | collective-permute-start | bytes 786440 | tf_op jit(solution)/shard_map/ppermute | solution.py:106
  116.2 3.7 %collective-permute-start.10 = (f32[1,128,512]{2,1,0:T(8,128)}, f32[1,128,512]{2,1,0:T(8,128)}, u32[]{:S(2)}, u32[]{:S(2)}) collective-permute-start(f32[1,128,512]{2,1,0:T(8,128)} %bitcast_add_fusion.8), channel_id=1, source_target_pairs={{0,224},{32,0},{64,32},{96,64},{128,96},{160,128},{192,160},{224,1... | collective-permute-start | bytes 786440 | tf_op jit(solution)/shard_map/ppermute | solution.py:106
  119.9 4.4 %collective-permute-done.2 = f32[1,128,512]{2,1,0:T(8,128)} collective-permute-done((f32[1,128,512]{2,1,0:T(8,128)S(1)}, f32[1,128,512]{2,1,0:T(8,128)}, u32[]{:S(2)}, u32[]{:S(2)}) %collective-permute-start.2) | collective-permute-done | bytes 262176 | tf_op jit(solution)/shard_map/ppermute | solution.py:105
  127.4 3.7 %collective-permute-start.11 = (f32[1,128,512]{2,1,0:T(8,128)}, f32[1,128,512]{2,1,0:T(8,128)}, u32[]{:S(2)}, u32[]{:S(2)}) collective-permute-start(f32[1,128,512]{2,1,0:T(8,128)} %bitcast_add_fusion.7), channel_id=1, source_target_pairs={{0,224},{32,0},{64,32},{96,64},{128,96},{160,128},{192,160},{224,1... | collective-permute-start | bytes 786440 | tf_op jit(solution)/shard_map/ppermute | solution.py:106
  131.1 3.4 %collective-permute-done.3 = f32[1,128,512]{2,1,0:T(8,128)} collective-permute-done((f32[1,128,512]{2,1,0:T(8,128)S(1)}, f32[1,128,512]{2,1,0:T(8,128)}, u32[]{:S(2)}, u32[]{:S(2)}) %collective-permute-start.3) | collective-permute-done | bytes 262176 | tf_op jit(solution)/shard_map/ppermute | solution.py:105
  137.8 3.7 %collective-permute-start.12 = (f32[1,128,512]{2,1,0:T(8,128)}, f32[1,128,512]{2,1,0:T(8,128)}, u32[]{:S(2)}, u32[]{:S(2)}) collective-permute-start(f32[1,128,512]{2,1,0:T(8,128)} %bitcast_add_fusion.6), channel_id=1, source_target_pairs={{0,224},{32,0},{64,32},{96,64},{128,96},{160,128},{192,160},{224,1... | collective-permute-start | bytes 786440 | tf_op jit(solution)/shard_map/ppermute | solution.py:106
  147.4 3.7 %collective-permute-start.13 = (f32[1,128,512]{2,1,0:T(8,128)}, f32[1,128,512]{2,1,0:T(8,128)}, u32[]{:S(2)}, u32[]{:S(2)}) collective-permute-start(f32[1,128,512]{2,1,0:T(8,128)} %bitcast_add_fusion.5), channel_id=1, source_target_pairs={{0,224},{32,0},{64,32},{96,64},{128,96},{160,128},{192,160},{224,1... | collective-permute-start | bytes 786440 | tf_op jit(solution)/shard_map/ppermute | solution.py:106
  157.0 3.7 %collective-permute-start.14 = (f32[1,128,512]{2,1,0:T(8,128)}, f32[1,128,512]{2,1,0:T(8,128)}, u32[]{:S(2)}, u32[]{:S(2)}) collective-permute-start(f32[1,128,512]{2,1,0:T(8,128)} %bitcast_add_fusion.4), channel_id=1, source_target_pairs={{0,224},{32,0},{64,32},{96,64},{128,96},{160,128},{192,160},{224,1... | collective-permute-start | bytes 786440 | tf_op jit(solution)/shard_map/ppermute | solution.py:106
  166.2 3.8 %collective-permute-start.15 = (f32[1,128,512]{2,1,0:T(8,128)S(1)}, f32[1,128,512]{2,1,0:T(8,128)}, u32[]{:S(2)}, u32[]{:S(2)}) collective-permute-start(f32[1,128,512]{2,1,0:T(8,128)S(1)} %bitcast_add_fusion.3), channel_id=1, source_target_pairs={{0,224},{32,0},{64,32},{96,64},{128,96},{160,128},{192,160},{224,1... | collective-permute-start | bytes 786440 | tf_op jit(solution)/shard_map/ppermute | solution.py:106
  174.9 5.9 %collective-permute-done.8 = f32[1,128,512]{2,1,0:T(8,128)} collective-permute-done((f32[1,128,512]{2,1,0:T(8,128)}, f32[1,128,512]{2,1,0:T(8,128)}, u32[]{:S(2)}, u32[]{:S(2)}) %collective-permute-start.8) | collective-permute-done | bytes 262176 | tf_op jit(solution)/shard_map/ppermute | solution.py:105
  182.0 15.0 %all_to_all.25 = f32[2,16,8,512]{3,2,0,1:T(8,128)S(1)} all-to-all(f32[2,16,8,512]{3,2,0,1:T(8,128)S(1)} %copy.56), channel_id=1, replica_groups=mesh['dp'=8,'section'=2,'round'=16] {'round'}, dimensions={1} | all-to-all | bytes 1048576 | tf_op jit(solution)/shard_map/all_to_all | solution.py:114
  (184 shorter events, 78.2 us)
Async XLA Ops:
  2.7 59.1 %copy-start.5 = (f32[128,512]{1,0:T(8,128)}, f32[128,512]{1,0:T(8,128)S(1)}, u32[]{:S(2)}) copy-start(f32[128,512]{1,0:T(8,128)S(1)} %get-tuple-element.212.a_im_ref) | copy-start | bytes 786436
  8.1 19.7 %copy-start.7 = (bf16[1,1024,512]{2,1,0:T(8,128)(2,1)S(1)}, bf16[1,1024,512]{2,1,0:T(8,128)(2,1)}, u32[]{:S(2)}) copy-start(bf16[1,1024,512]{2,1,0:T(8,128)(2,1)} %param.14) | copy-start | bytes 3145732
  11.5 14.5 %all-to-all-start = ((f32[16,4,2,512]{3,2,1,0:T(2,128)}), f32[16,4,2,512]{3,2,1,0:T(2,128)S(1)}, u32[]{:S(2)}, u32[]{:S(2)}) async-start(f32[16,4,2,512]{3,2,1,0:T(2,128)} %get-tuple-element.24), calls=%async_computation | async-start | bytes 524288 | tf_op jit(solution)/shard_map/all_to_all | solution.py:74
  28.3 2.4 %collective-permute-start = (bf16[2,128,512]{2,1,0:T(8,128)(2,1)S(1)}, bf16[2,128,512]{2,1,0:T(8,128)(2,1)S(1)}, u32[]{:S(2)}, u32[]{:S(2)}) collective-permute-start(bf16[2,128,512]{2,1,0:T(8,128)(2,1)S(1)} %fusion), channel_id=1, source_target_pairs={{0,16},{1,17},{2,18},{3,19},{4,20},{5,21},{6,22},{7,23},{8,24},{9,... | collective-permute-start | bytes 786440 | tf_op jit(solution)/shard_map/ppermute | solution.py:120
  30.9 52.2 %copy-start.9 = (bf16[2,128,512]{2,1,0:T(8,128)(2,1)}, bf16[2,128,512]{2,1,0:T(8,128)(2,1)S(1)}, u32[]{:S(2)}) copy-start(bf16[2,128,512]{2,1,0:T(8,128)(2,1)S(1)} %get-tuple-element.162) | copy-start | bytes 786436
  35.9 13.4 %all-to-all-start.1 = ((f32[16,4,2,512]{3,2,1,0:T(2,128)}), f32[16,4,2,512]{3,2,1,0:T(2,128)}, u32[]{:S(2)}, u32[]{:S(2)}) async-start(f32[16,4,2,512]{3,2,1,0:T(2,128)} %get-tuple-element.29), calls=%async_computation.1 | async-start | bytes 524288 | tf_op jit(solution)/shard_map/all_to_all | solution.py:74
  66.3 12.1 %all-to-all-start.2 = ((f32[16,4,2,512]{3,2,1,0:T(2,128)}), f32[16,4,2,512]{3,2,1,0:T(2,128)S(1)}, u32[]{:S(2)}, u32[]{:S(2)}) async-start(f32[16,4,2,512]{3,2,1,0:T(2,128)} %get-tuple-element.34), calls=%async_computation.2 | async-start | bytes 524288 | tf_op jit(solution)/shard_map/all_to_all | solution.py:74
  81.7 3.6 %collective-permute-start.1 = (bf16[2,128,512]{2,1,0:T(8,128)(2,1)S(1)}, bf16[2,128,512]{2,1,0:T(8,128)(2,1)S(1)}, u32[]{:S(2)}, u32[]{:S(2)}) collective-permute-start(bf16[2,128,512]{2,1,0:T(8,128)(2,1)S(1)} %fusion.28), channel_id=1, source_target_pairs={{16,0},{17,1},{18,2},{19,3},{20,4},{21,5},{22,6},{23,7},{24,8},{25... | collective-permute-start | bytes 786440 | tf_op jit(solution)/shard_map/ppermute | solution.py:120
  87.2 10.1 %copy-start.12 = (bf16[2,128,512]{2,1,0:T(8,128)(2,1)S(1)}, bf16[2,128,512]{2,1,0:T(8,128)(2,1)}, u32[]{:S(2)}) copy-start(bf16[2,128,512]{2,1,0:T(8,128)(2,1)} %copy-done.11) | copy-start | bytes 786436
  90.6 17.2 %all-to-all-start.3 = ((f32[16,4,2,512]{3,2,1,0:T(2,128)}), f32[16,4,2,512]{3,2,1,0:T(2,128)S(1)}, u32[]{:S(2)}, u32[]{:S(2)}) async-start(f32[16,4,2,512]{3,2,1,0:T(2,128)} %get-tuple-element.39), calls=%async_computation.3 | async-start | bytes 524288 | tf_op jit(solution)/shard_map/all_to_all | solution.py:74
  101.9 12.6 %collective-permute-start.9 = (f32[1,128,512]{2,1,0:T(8,128)}, f32[1,128,512]{2,1,0:T(8,128)}, u32[]{:S(2)}, u32[]{:S(2)}) collective-permute-start(f32[1,128,512]{2,1,0:T(8,128)} %dynamic-slice_bitcast_fusion), channel_id=1, source_target_pairs={{0,224},{32,0},{64,32},{96,64},{128,96},{160,128},{192,160},{224,1... | collective-permute-start | bytes 786440 | tf_op jit(solution)/shard_map/ppermute | solution.py:106
  113.5 10.8 %collective-permute-start.2 = (f32[1,128,512]{2,1,0:T(8,128)S(1)}, f32[1,128,512]{2,1,0:T(8,128)}, u32[]{:S(2)}, u32[]{:S(2)}) collective-permute-start(f32[1,128,512]{2,1,0:T(8,128)S(1)} %dynamic-slice_bitcast_fusion.1), channel_id=1, source_target_pairs={{0,32},{32,64},{64,96},{96,128},{128,160},{160,192},{192,224},{224... | collective-permute-start | bytes 786440 | tf_op jit(solution)/shard_map/ppermute | solution.py:105
  116.2 9.6 %collective-permute-start.10 = (f32[1,128,512]{2,1,0:T(8,128)}, f32[1,128,512]{2,1,0:T(8,128)}, u32[]{:S(2)}, u32[]{:S(2)}) collective-permute-start(f32[1,128,512]{2,1,0:T(8,128)} %bitcast_add_fusion.8), channel_id=1, source_target_pairs={{0,224},{32,0},{64,32},{96,64},{128,96},{160,128},{192,160},{224,1... | collective-permute-start | bytes 786440 | tf_op jit(solution)/shard_map/ppermute | solution.py:106
  125.4 9.1 %collective-permute-start.3 = (f32[1,128,512]{2,1,0:T(8,128)S(1)}, f32[1,128,512]{2,1,0:T(8,128)}, u32[]{:S(2)}, u32[]{:S(2)}) collective-permute-start(f32[1,128,512]{2,1,0:T(8,128)S(1)} %bitcast_add_fusion.15), channel_id=1, source_target_pairs={{0,32},{32,64},{64,96},{96,128},{128,160},{160,192},{192,224},{224... | collective-permute-start | bytes 786440 | tf_op jit(solution)/shard_map/ppermute | solution.py:105
  127.4 8.7 %collective-permute-start.11 = (f32[1,128,512]{2,1,0:T(8,128)}, f32[1,128,512]{2,1,0:T(8,128)}, u32[]{:S(2)}, u32[]{:S(2)}) collective-permute-start(f32[1,128,512]{2,1,0:T(8,128)} %bitcast_add_fusion.7), channel_id=1, source_target_pairs={{0,224},{32,0},{64,32},{96,64},{128,96},{160,128},{192,160},{224,1... | collective-permute-start | bytes 786440 | tf_op jit(solution)/shard_map/ppermute | solution.py:106
  135.5 8.3 %collective-permute-start.4 = (f32[1,128,512]{2,1,0:T(8,128)S(1)}, f32[1,128,512]{2,1,0:T(8,128)}, u32[]{:S(2)}, u32[]{:S(2)}) collective-permute-start(f32[1,128,512]{2,1,0:T(8,128)S(1)} %bitcast_add_fusion.14), channel_id=1, source_target_pairs={{0,32},{32,64},{64,96},{96,128},{128,160},{160,192},{192,224},{224... | collective-permute-start | bytes 786440 | tf_op jit(solution)/shard_map/ppermute | solution.py:105
  137.8 7.9 %collective-permute-start.12 = (f32[1,128,512]{2,1,0:T(8,128)}, f32[1,128,512]{2,1,0:T(8,128)}, u32[]{:S(2)}, u32[]{:S(2)}) collective-permute-start(f32[1,128,512]{2,1,0:T(8,128)} %bitcast_add_fusion.6), channel_id=1, source_target_pairs={{0,224},{32,0},{64,32},{96,64},{128,96},{160,128},{192,160},{224,1... | collective-permute-start | bytes 786440 | tf_op jit(solution)/shard_map/ppermute | solution.py:106
  144.9 7.8 %collective-permute-start.5 = (f32[1,128,512]{2,1,0:T(8,128)S(1)}, f32[1,128,512]{2,1,0:T(8,128)}, u32[]{:S(2)}, u32[]{:S(2)}) collective-permute-start(f32[1,128,512]{2,1,0:T(8,128)S(1)} %bitcast_add_fusion.13), channel_id=1, source_target_pairs={{0,32},{32,64},{64,96},{96,128},{128,160},{160,192},{192,224},{224... | collective-permute-start | bytes 786440 | tf_op jit(solution)/shard_map/ppermute | solution.py:105
  147.4 7.9 %collective-permute-start.13 = (f32[1,128,512]{2,1,0:T(8,128)}, f32[1,128,512]{2,1,0:T(8,128)}, u32[]{:S(2)}, u32[]{:S(2)}) collective-permute-start(f32[1,128,512]{2,1,0:T(8,128)} %bitcast_add_fusion.5), channel_id=1, source_target_pairs={{0,224},{32,0},{64,32},{96,64},{128,96},{160,128},{192,160},{224,1... | collective-permute-start | bytes 786440 | tf_op jit(solution)/shard_map/ppermute | solution.py:106
  153.7 7.8 %collective-permute-start.6 = (f32[1,128,512]{2,1,0:T(8,128)S(1)}, f32[1,128,512]{2,1,0:T(8,128)}, u32[]{:S(2)}, u32[]{:S(2)}) collective-permute-start(f32[1,128,512]{2,1,0:T(8,128)S(1)} %bitcast_add_fusion.12), channel_id=1, source_target_pairs={{0,32},{32,64},{64,96},{96,128},{128,160},{160,192},{192,224},{224... | collective-permute-start | bytes 786440 | tf_op jit(solution)/shard_map/ppermute | solution.py:105
  157.0 8.3 %collective-permute-start.14 = (f32[1,128,512]{2,1,0:T(8,128)}, f32[1,128,512]{2,1,0:T(8,128)}, u32[]{:S(2)}, u32[]{:S(2)}) collective-permute-start(f32[1,128,512]{2,1,0:T(8,128)} %bitcast_add_fusion.4), channel_id=1, source_target_pairs={{0,224},{32,0},{64,32},{96,64},{128,96},{160,128},{192,160},{224,1... | collective-permute-start | bytes 786440 | tf_op jit(solution)/shard_map/ppermute | solution.py:106
  163.3 7.9 %collective-permute-start.7 = (f32[1,128,512]{2,1,0:T(8,128)}, f32[1,128,512]{2,1,0:T(8,128)}, u32[]{:S(2)}, u32[]{:S(2)}) collective-permute-start(f32[1,128,512]{2,1,0:T(8,128)} %bitcast_add_fusion.11), channel_id=1, source_target_pairs={{0,32},{32,64},{64,96},{96,128},{128,160},{160,192},{192,224},{224... | collective-permute-start | bytes 786440 | tf_op jit(solution)/shard_map/ppermute | solution.py:105
  166.2 7.7 %collective-permute-start.15 = (f32[1,128,512]{2,1,0:T(8,128)S(1)}, f32[1,128,512]{2,1,0:T(8,128)}, u32[]{:S(2)}, u32[]{:S(2)}) collective-permute-start(f32[1,128,512]{2,1,0:T(8,128)S(1)} %bitcast_add_fusion.3), channel_id=1, source_target_pairs={{0,224},{32,0},{64,32},{96,64},{128,96},{160,128},{192,160},{224,1... | collective-permute-start | bytes 786440 | tf_op jit(solution)/shard_map/ppermute | solution.py:106
  172.9 7.9 %collective-permute-start.8 = (f32[1,128,512]{2,1,0:T(8,128)}, f32[1,128,512]{2,1,0:T(8,128)}, u32[]{:S(2)}, u32[]{:S(2)}) collective-permute-start(f32[1,128,512]{2,1,0:T(8,128)} %bitcast_add_fusion.10), channel_id=1, source_target_pairs={{0,32},{32,64},{64,96},{96,128},{128,160},{160,192},{192,224},{224... | collective-permute-start | bytes 786440 | tf_op jit(solution)/shard_map/ppermute | solution.py:105
  (18 other events, 65.5 us)

commit v7 on v6

--- a/solution.py
+++ b/solution.py
@@ -38,7 +38,7 @@
 
     zero = jnp.zeros((1, width), jnp.float32)
     start = (jnp.ones((1, width), jnp.float32), zero, tuple((zero, zero) for _ in range(shots)))
-    p_re, p_im, states = lax.fori_loop(0, rounds, step, start, unroll=8)
+    p_re, p_im, states = lax.fori_loop(0, rounds, step, start, unroll=16)
     for copy in range(end_ref.shape[0]):
         for b in range(shots):
             end_ref[copy, 0, pl.ds(b, 1), :] = p_re

time: 199 us -> 199 us (level)
  no operation moved by 1% of the time
where the time goes in v7:
time: 199 us; the launch traced here: 198 us
  starting transfers between devices  56 us (28%)
  waiting for transfers between devices  43 us (22%)
  other arithmetic  42.9 us (22%)
  matrix products  15.4 us (8%)
  blocking collectives  15 us (8%)
  Pallas kernels  13.5 us (7%)
  local copies, waits for them, and re-layouts  10.1 us (5%)
    ppermute x7, starting transfers between devices, ring_stage(): lax.ppermute(acc_second, axis, behind) + take(second, (pos + step + 2) % n)  28.1 us
    all_to_all x4, starting transfers between devices, entering(): everything = lax.all_to_all(copies, axis, 0, 0, tiled=True)  24.7 us
    ppermute x7, waiting for transfers between devices, ring_stage(): lax.ppermute(acc_first, axis, ahead) + take(first, (pos - step - 2) % n)  19.5 us
    all_to_all x4, waiting for transfers between devices, entering(): everything = lax.all_to_all(copies, axis, 0, 0, tiled=True)  15.5 us
    all_to_all x1, blocking collectives, reduce_scatter_rows(): return lax.all_to_all(split, 'round', 1, 1, tiled=True).sum(axis=1)  15 us
    pallas_call x4, Pallas kernels, recurrence(): pl.pallas_call(functools.partial(_recurrence_kernel, reverse=reverse), ou...  13.5 us
    add x7, other arithmetic, ring_stage(): lax.ppermute(acc_second, axis, behind) + take(second, (pos + step + 2) % n)  10.4 us
    add x7, other arithmetic, ring_stage(): lax.ppermute(acc_first, axis, ahead) + take(first, (pos - step - 2) % n)  8.87 us
  transfers between devices with their start and end apart: 20, of which 19 were waited for; matrix products, arithmetic and copies ran while one was open for 17% of the time, Pallas kernels for 0%

profile of v7, /device:TPU:8, one launch (start us, length us, event | category | flops | bytes accessed | tf_op | source)
XLA Modules:
  0.0 197.6 jit_solution(3603789909812444962)
XLA Ops:
  8.1 3.4 %shard_map.104 = (f32[128,512]{1,0:T(8,128)}, f32[128,512]{1,0:T(8,128)}, f32[2,128,512]{2,1,0:T(8,128)}, f32[2,128,512]{2,1,0:T(8,128)}, f32[16,4,2,512]{3,2,1,0:T(2,128)}) custom-call(f32[128,512]{1,0:T(8,128)} %get-tuple-element.215.a_re_ref, f32[128,512]{1,0:T(8,128)} %get-tuple-element.214.a_im_ref, f32[2,128,512]{2,1,0:T(8,128)} %get-tuple-element.198.d_re_ref, ...), custom_call_target="tpu_custom_call" | custom-call | flops 1572864 | bytes 3145728 | tf_op jit(solution)/shard_map/pallas_call | solution.py:56
  11.5 7.4 %all-to-all-start = ((f32[16,4,2,512]{3,2,1,0:T(2,128)}), f32[16,4,2,512]{3,2,1,0:T(2,128)S(1)}, u32[]{:S(2)}, u32[]{:S(2)}) async-start(f32[16,4,2,512]{3,2,1,0:T(2,128)} %get-tuple-element.24), calls=%async_computation | async-start | bytes 524288 | tf_op jit(solution)/shard_map/all_to_all | solution.py:74
  18.9 7.1 %all-to-all-done = f32[16,4,2,512]{3,2,1,0:T(2,128)S(1)} async-done(((f32[16,4,2,512]{3,2,1,0:T(2,128)}), f32[16,4,2,512]{3,2,1,0:T(2,128)S(1)}, u32[]{:S(2)}, u32[]{:S(2)}) %all-to-all-start) | async-done | bytes 262176 | tf_op jit(solution)/shard_map/all_to_all | solution.py:74
  32.6 3.3 %shard_map.105 = (f32[128,512]{1,0:T(8,128)}, f32[128,512]{1,0:T(8,128)}, f32[2,128,512]{2,1,0:T(8,128)}, f32[2,128,512]{2,1,0:T(8,128)}, f32[16,4,2,512]{3,2,1,0:T(2,128)}) custom-call(f32[128,512]{1,0:T(8,128)} %get-tuple-element.215.a_re_ref, f32[128,512]{1,0:T(8,128)} %get-tuple-element.214.a_im_ref, f32[2,128,512]{2,1,0:T(8,128)} %get-tuple-element.196.d_re_ref, ...), custom_call_target="tpu_custom_call" | custom-call | flops 1572864 | bytes 3145728 | tf_op jit(solution)/shard_map/pallas_call | solution.py:56
  35.9 5.4 %all-to-all-start.1 = ((f32[16,4,2,512]{3,2,1,0:T(2,128)}), f32[16,4,2,512]{3,2,1,0:T(2,128)}, u32[]{:S(2)}, u32[]{:S(2)}) async-start(f32[16,4,2,512]{3,2,1,0:T(2,128)} %get-tuple-element.29), calls=%async_computation.1 | async-start | bytes 524288 | tf_op jit(solution)/shard_map/all_to_all | solution.py:74
  41.5 7.9 %all-to-all-done.1 = f32[16,4,2,512]{3,2,1,0:T(2,128)} async-done(((f32[16,4,2,512]{3,2,1,0:T(2,128)}), f32[16,4,2,512]{3,2,1,0:T(2,128)}, u32[]{:S(2)}, u32[]{:S(2)}) %all-to-all-start.1) | async-done | bytes 262176 | tf_op jit(solution)/shard_map/all_to_all | solution.py:74
  56.0 2.4 %subtract_convert_fusion = (bf16[2,128,512]{2,1,0:T(8,128)(2,1)}, bf16[2,128,512]{2,1,0:T(8,128)(2,1)}) fusion(f32[2,128,512]{2,1,0:T(8,128)} %get-tuple-element.27, f32[2,512]{1,0:T(2,128)S(1)} %fusion.64, f32[128,512]{1,0:T(8,128)} %get-tuple-element.30, f32[2,512]{1,0:T(2,128)S(1)} %get-tuple-element.137, f32[128,512]{1,0:T(8,128)} %get-tuple-element.28, ...), kind=kLoop, calls=%fused_computation.76 | loop fusion | flops 1310720 | bytes 2105344 | tf_op jit(solution)/shard_map/convert
  62.9 3.3 %shard_map.106 = (f32[128,512]{1,0:T(8,128)}, f32[128,512]{1,0:T(8,128)}, f32[2,128,512]{2,1,0:T(8,128)}, f32[2,128,512]{2,1,0:T(8,128)}, f32[16,4,2,512]{3,2,1,0:T(2,128)}) custom-call(f32[128,512]{1,0:T(8,128)} %get-tuple-element.215.a_re_ref, f32[128,512]{1,0:T(8,128)} %copy-done.5, f32[2,128,512]{2,1,0:T(8,128)} %get-tuple-element.190.d_re_ref, ...), custom_call_target="tpu_custom_call" | custom-call | flops 1572864 | bytes 3145728 | tf_op jit(solution)/shard_map/pallas_call | solution.py:56
  66.3 5.2 %all-to-all-start.2 = ((f32[16,4,2,512]{3,2,1,0:T(2,128)}), f32[16,4,2,512]{3,2,1,0:T(2,128)S(1)}, u32[]{:S(2)}, u32[]{:S(2)}) async-start(f32[16,4,2,512]{3,2,1,0:T(2,128)} %get-tuple-element.34), calls=%async_computation.2 | async-start | bytes 524288 | tf_op jit(solution)/shard_map/all_to_all | solution.py:74
  74.8 3.1 %fusion.42 = f32[1024,512,1]{1,0,2:T(8,128)} fusion(f32[512]{0:T(512)S(1)} %convert_element_type.76, f32[2,128]{1,0:T(2,128)S(1)} %fusion.429, pred[]{:T(512)S(6)} %eq.21, bf16[2,128,512]{2,1,0:T(8,128)(2,1)} %get-tuple-element.204, bf16[2,128,512]{2,1,0:T(8,128)(2,1)} %get-tuple-element.203, bf16[2,128,512]{2,1,0:T(8,128)(2,1)} %copy-done.15, ...), kind=kOutput, calls=%fused_computation.82 | convolution fusion | flops 271187968 | bytes 3148801 | tf_op jit(solution)/shard_map/brk,brw->kw/dot_general | solution.py:192
  87.1 3.4 %shard_map.107 = (f32[128,512]{1,0:T(8,128)}, f32[128,512]{1,0:T(8,128)}, f32[2,128,512]{2,1,0:T(8,128)}, f32[2,128,512]{2,1,0:T(8,128)}, f32[16,4,2,512]{3,2,1,0:T(2,128)}) custom-call(f32[128,512]{1,0:T(8,128)} %get-tuple-element.215.a_re_ref, f32[128,512]{1,0:T(8,128)} %copy-done.5, f32[2,128,512]{2,1,0:T(8,128)} %get-tuple-element.188.d_re_ref, ...), custom_call_target="tpu_custom_call" | custom-call | flops 1572864 | bytes 3145728 | tf_op jit(solution)/shard_map/pallas_call | solution.py:56
  90.6 6.7 %all-to-all-start.3 = ((f32[16,4,2,512]{3,2,1,0:T(2,128)}), f32[16,4,2,512]{3,2,1,0:T(2,128)S(1)}, u32[]{:S(2)}, u32[]{:S(2)}) async-start(f32[16,4,2,512]{3,2,1,0:T(2,128)} %get-tuple-element.39), calls=%async_computation.3 | async-start | bytes 524288 | tf_op jit(solution)/shard_map/all_to_all | solution.py:74
  97.3 2.4 %bitcast_add_fusion = f32[1024,512]{1,0:T(8,128)S(1)} fusion(f32[1024,512,1]{1,0,2:T(8,128)} %fusion.42, bf16[2,128,512]{2,1,0:T(8,128)(2,1)S(1)} %copy-done.12, pred[]{:T(512)S(6)} %eq.21, bf16[2,128,512]{2,1,0:T(8,128)(2,1)} %get-tuple-element.204, bf16[2,128,512]{2,1,0:T(8,128)(2,1)} %get-tuple-element.203, bf16[2,128,512]{2,1,0:T(8,128)(2,1)} %copy-done.15, ...), kind=kOutput, calls=%fused_computation | convolution fusion | flops 271712256 | bytes 5505025 | tf_op jit(solution)/shard_map/brk,brw->kw/dot_general | solution.py:192
  101.9 5.9 %collective-permute-start.9 = (f32[1,128,512]{2,1,0:T(8,128)}, f32[1,128,512]{2,1,0:T(8,128)}, u32[]{:S(2)}, u32[]{:S(2)}) collective-permute-start(f32[1,128,512]{2,1,0:T(8,128)} %dynamic-slice_bitcast_fusion), channel_id=1, source_target_pairs={{0,224},{32,0},{64,32},{96,64},{128,96},{160,128},{192,160},{224,1... | collective-permute-start | bytes 786440 | tf_op jit(solution)/shard_map/ppermute | solution.py:106
  116.2 3.7 %collective-permute-start.10 = (f32[1,128,512]{2,1,0:T(8,128)}, f32[1,128,512]{2,1,0:T(8,128)}, u32[]{:S(2)}, u32[]{:S(2)}) collective-permute-start(f32[1,128,512]{2,1,0:T(8,128)} %bitcast_add_fusion.8), channel_id=1, source_target_pairs={{0,224},{32,0},{64,32},{96,64},{128,96},{160,128},{192,160},{224,1... | collective-permute-start | bytes 786440 | tf_op jit(solution)/shard_map/ppermute | solution.py:106
  119.8 4.4 %collective-permute-done.2 = f32[1,128,512]{2,1,0:T(8,128)} collective-permute-done((f32[1,128,512]{2,1,0:T(8,128)S(1)}, f32[1,128,512]{2,1,0:T(8,128)}, u32[]{:S(2)}, u32[]{:S(2)}) %collective-permute-start.2) | collective-permute-done | bytes 262176 | tf_op jit(solution)/shard_map/ppermute | solution.py:105
  127.4 3.7 %collective-permute-start.11 = (f32[1,128,512]{2,1,0:T(8,128)}, f32[1,128,512]{2,1,0:T(8,128)}, u32[]{:S(2)}, u32[]{:S(2)}) collective-permute-start(f32[1,128,512]{2,1,0:T(8,128)} %bitcast_add_fusion.7), channel_id=1, source_target_pairs={{0,224},{32,0},{64,32},{96,64},{128,96},{160,128},{192,160},{224,1... | collective-permute-start | bytes 786440 | tf_op jit(solution)/shard_map/ppermute | solution.py:106
  131.1 3.4 %collective-permute-done.3 = f32[1,128,512]{2,1,0:T(8,128)} collective-permute-done((f32[1,128,512]{2,1,0:T(8,128)S(1)}, f32[1,128,512]{2,1,0:T(8,128)}, u32[]{:S(2)}, u32[]{:S(2)}) %collective-permute-start.3) | collective-permute-done | bytes 262176 | tf_op jit(solution)/shard_map/ppermute | solution.py:105
  137.8 3.7 %collective-permute-start.12 = (f32[1,128,512]{2,1,0:T(8,128)}, f32[1,128,512]{2,1,0:T(8,128)}, u32[]{:S(2)}, u32[]{:S(2)}) collective-permute-start(f32[1,128,512]{2,1,0:T(8,128)} %bitcast_add_fusion.6), channel_id=1, source_target_pairs={{0,224},{32,0},{64,32},{96,64},{128,96},{160,128},{192,160},{224,1... | collective-permute-start | bytes 786440 | tf_op jit(solution)/shard_map/ppermute | solution.py:106
  147.3 3.7 %collective-permute-start.13 = (f32[1,128,512]{2,1,0:T(8,128)}, f32[1,128,512]{2,1,0:T(8,128)}, u32[]{:S(2)}, u32[]{:S(2)}) collective-permute-start(f32[1,128,512]{2,1,0:T(8,128)} %bitcast_add_fusion.5), channel_id=1, source_target_pairs={{0,224},{32,0},{64,32},{96,64},{128,96},{160,128},{192,160},{224,1... | collective-permute-start | bytes 786440 | tf_op jit(solution)/shard_map/ppermute | solution.py:106
  156.9 3.7 %collective-permute-start.14 = (f32[1,128,512]{2,1,0:T(8,128)}, f32[1,128,512]{2,1,0:T(8,128)}, u32[]{:S(2)}, u32[]{:S(2)}) collective-permute-start(f32[1,128,512]{2,1,0:T(8,128)} %bitcast_add_fusion.4), channel_id=1, source_target_pairs={{0,224},{32,0},{64,32},{96,64},{128,96},{160,128},{192,160},{224,1... | collective-permute-start | bytes 786440 | tf_op jit(solution)/shard_map/ppermute | solution.py:106
  166.2 3.8 %collective-permute-start.15 = (f32[1,128,512]{2,1,0:T(8,128)S(1)}, f32[1,128,512]{2,1,0:T(8,128)}, u32[]{:S(2)}, u32[]{:S(2)}) collective-permute-start(f32[1,128,512]{2,1,0:T(8,128)S(1)} %bitcast_add_fusion.3), channel_id=1, source_target_pairs={{0,224},{32,0},{64,32},{96,64},{128,96},{160,128},{192,160},{224,1... | collective-permute-start | bytes 786440 | tf_op jit(solution)/shard_map/ppermute | solution.py:106
  174.8 5.9 %collective-permute-done.8 = f32[1,128,512]{2,1,0:T(8,128)} collective-permute-done((f32[1,128,512]{2,1,0:T(8,128)}, f32[1,128,512]{2,1,0:T(8,128)}, u32[]{:S(2)}, u32[]{:S(2)}) %collective-permute-start.8) | collective-permute-done | bytes 262176 | tf_op jit(solution)/shard_map/ppermute | solution.py:105
  181.9 15.0 %all_to_all.25 = f32[2,16,8,512]{3,2,0,1:T(8,128)S(1)} all-to-all(f32[2,16,8,512]{3,2,0,1:T(8,128)S(1)} %copy.56), channel_id=1, replica_groups=mesh['dp'=8,'section'=2,'round'=16] {'round'}, dimensions={1} | all-to-all | bytes 1048576 | tf_op jit(solution)/shard_map/all_to_all | solution.py:114
  (184 shorter events, 78.2 us)
Async XLA Ops:
  2.7 59.1 %copy-start.5 = (f32[128,512]{1,0:T(8,128)}, f32[128,512]{1,0:T(8,128)S(1)}, u32[]{:S(2)}) copy-start(f32[128,512]{1,0:T(8,128)S(1)} %get-tuple-element.212.a_im_ref) | copy-start | bytes 786436
  8.1 19.7 %copy-start.7 = (bf16[1,1024,512]{2,1,0:T(8,128)(2,1)S(1)}, bf16[1,1024,512]{2,1,0:T(8,128)(2,1)}, u32[]{:S(2)}) copy-start(bf16[1,1024,512]{2,1,0:T(8,128)(2,1)} %param.14) | copy-start | bytes 3145732
  11.5 14.5 %all-to-all-start = ((f32[16,4,2,512]{3,2,1,0:T(2,128)}), f32[16,4,2,512]{3,2,1,0:T(2,128)S(1)}, u32[]{:S(2)}, u32[]{:S(2)}) async-start(f32[16,4,2,512]{3,2,1,0:T(2,128)} %get-tuple-element.24), calls=%async_computation | async-start | bytes 524288 | tf_op jit(solution)/shard_map/all_to_all | solution.py:74
  28.3 2.4 %collective-permute-start = (bf16[2,128,512]{2,1,0:T(8,128)(2,1)S(1)}, bf16[2,128,512]{2,1,0:T(8,128)(2,1)S(1)}, u32[]{:S(2)}, u32[]{:S(2)}) collective-permute-start(bf16[2,128,512]{2,1,0:T(8,128)(2,1)S(1)} %fusion), channel_id=1, source_target_pairs={{0,16},{1,17},{2,18},{3,19},{4,20},{5,21},{6,22},{7,23},{8,24},{9,... | collective-permute-start | bytes 786440 | tf_op jit(solution)/shard_map/ppermute | solution.py:120
  30.9 52.2 %copy-start.9 = (bf16[2,128,512]{2,1,0:T(8,128)(2,1)}, bf16[2,128,512]{2,1,0:T(8,128)(2,1)S(1)}, u32[]{:S(2)}) copy-start(bf16[2,128,512]{2,1,0:T(8,128)(2,1)S(1)} %get-tuple-element.162) | copy-start | bytes 786436
  35.9 13.4 %all-to-all-start.1 = ((f32[16,4,2,512]{3,2,1,0:T(2,128)}), f32[16,4,2,512]{3,2,1,0:T(2,128)}, u32[]{:S(2)}, u32[]{:S(2)}) async-start(f32[16,4,2,512]{3,2,1,0:T(2,128)} %get-tuple-element.29), calls=%async_computation.1 | async-start | bytes 524288 | tf_op jit(solution)/shard_map/all_to_all | solution.py:74
  66.3 12.1 %all-to-all-start.2 = ((f32[16,4,2,512]{3,2,1,0:T(2,128)}), f32[16,4,2,512]{3,2,1,0:T(2,128)S(1)}, u32[]{:S(2)}, u32[]{:S(2)}) async-start(f32[16,4,2,512]{3,2,1,0:T(2,128)} %get-tuple-element.34), calls=%async_computation.2 | async-start | bytes 524288 | tf_op jit(solution)/shard_map/all_to_all | solution.py:74
  81.7 3.6 %collective-permute-start.1 = (bf16[2,128,512]{2,1,0:T(8,128)(2,1)S(1)}, bf16[2,128,512]{2,1,0:T(8,128)(2,1)S(1)}, u32[]{:S(2)}, u32[]{:S(2)}) collective-permute-start(bf16[2,128,512]{2,1,0:T(8,128)(2,1)S(1)} %fusion.28), channel_id=1, source_target_pairs={{16,0},{17,1},{18,2},{19,3},{20,4},{21,5},{22,6},{23,7},{24,8},{25... | collective-permute-start | bytes 786440 | tf_op jit(solution)/shard_map/ppermute | solution.py:120
  87.1 10.1 %copy-start.12 = (bf16[2,128,512]{2,1,0:T(8,128)(2,1)S(1)}, bf16[2,128,512]{2,1,0:T(8,128)(2,1)}, u32[]{:S(2)}) copy-start(bf16[2,128,512]{2,1,0:T(8,128)(2,1)} %copy-done.11) | copy-start | bytes 786436
  90.6 17.2 %all-to-all-start.3 = ((f32[16,4,2,512]{3,2,1,0:T(2,128)}), f32[16,4,2,512]{3,2,1,0:T(2,128)S(1)}, u32[]{:S(2)}, u32[]{:S(2)}) async-start(f32[16,4,2,512]{3,2,1,0:T(2,128)} %get-tuple-element.39), calls=%async_computation.3 | async-start | bytes 524288 | tf_op jit(solution)/shard_map/all_to_all | solution.py:74
  101.9 12.6 %collective-permute-start.9 = (f32[1,128,512]{2,1,0:T(8,128)}, f32[1,128,512]{2,1,0:T(8,128)}, u32[]{:S(2)}, u32[]{:S(2)}) collective-permute-start(f32[1,128,512]{2,1,0:T(8,128)} %dynamic-slice_bitcast_fusion), channel_id=1, source_target_pairs={{0,224},{32,0},{64,32},{96,64},{128,96},{160,128},{192,160},{224,1... | collective-permute-start | bytes 786440 | tf_op jit(solution)/shard_map/ppermute | solution.py:106
  113.5 10.8 %collective-permute-start.2 = (f32[1,128,512]{2,1,0:T(8,128)S(1)}, f32[1,128,512]{2,1,0:T(8,128)}, u32[]{:S(2)}, u32[]{:S(2)}) collective-permute-start(f32[1,128,512]{2,1,0:T(8,128)S(1)} %dynamic-slice_bitcast_fusion.1), channel_id=1, source_target_pairs={{0,32},{32,64},{64,96},{96,128},{128,160},{160,192},{192,224},{224... | collective-permute-start | bytes 786440 | tf_op jit(solution)/shard_map/ppermute | solution.py:105
  116.2 9.6 %collective-permute-start.10 = (f32[1,128,512]{2,1,0:T(8,128)}, f32[1,128,512]{2,1,0:T(8,128)}, u32[]{:S(2)}, u32[]{:S(2)}) collective-permute-start(f32[1,128,512]{2,1,0:T(8,128)} %bitcast_add_fusion.8), channel_id=1, source_target_pairs={{0,224},{32,0},{64,32},{96,64},{128,96},{160,128},{192,160},{224,1... | collective-permute-start | bytes 786440 | tf_op jit(solution)/shard_map/ppermute | solution.py:106
  125.3 9.1 %collective-permute-start.3 = (f32[1,128,512]{2,1,0:T(8,128)S(1)}, f32[1,128,512]{2,1,0:T(8,128)}, u32[]{:S(2)}, u32[]{:S(2)}) collective-permute-start(f32[1,128,512]{2,1,0:T(8,128)S(1)} %bitcast_add_fusion.15), channel_id=1, source_target_pairs={{0,32},{32,64},{64,96},{96,128},{128,160},{160,192},{192,224},{224... | collective-permute-start | bytes 786440 | tf_op jit(solution)/shard_map/ppermute | solution.py:105
  127.4 8.7 %collective-permute-start.11 = (f32[1,128,512]{2,1,0:T(8,128)}, f32[1,128,512]{2,1,0:T(8,128)}, u32[]{:S(2)}, u32[]{:S(2)}) collective-permute-start(f32[1,128,512]{2,1,0:T(8,128)} %bitcast_add_fusion.7), channel_id=1, source_target_pairs={{0,224},{32,0},{64,32},{96,64},{128,96},{160,128},{192,160},{224,1... | collective-permute-start | bytes 786440 | tf_op jit(solution)/shard_map/ppermute | solution.py:106
  135.5 8.3 %collective-permute-start.4 = (f32[1,128,512]{2,1,0:T(8,128)S(1)}, f32[1,128,512]{2,1,0:T(8,128)}, u32[]{:S(2)}, u32[]{:S(2)}) collective-permute-start(f32[1,128,512]{2,1,0:T(8,128)S(1)} %bitcast_add_fusion.14), channel_id=1, source_target_pairs={{0,32},{32,64},{64,96},{96,128},{128,160},{160,192},{192,224},{224... | collective-permute-start | bytes 786440 | tf_op jit(solution)/shard_map/ppermute | solution.py:105
  137.8 7.9 %collective-permute-start.12 = (f32[1,128,512]{2,1,0:T(8,128)}, f32[1,128,512]{2,1,0:T(8,128)}, u32[]{:S(2)}, u32[]{:S(2)}) collective-permute-start(f32[1,128,512]{2,1,0:T(8,128)} %bitcast_add_fusion.6), channel_id=1, source_target_pairs={{0,224},{32,0},{64,32},{96,64},{128,96},{160,128},{192,160},{224,1... | collective-permute-start | bytes 786440 | tf_op jit(solution)/shard_map/ppermute | solution.py:106
  144.8 7.8 %collective-permute-start.5 = (f32[1,128,512]{2,1,0:T(8,128)S(1)}, f32[1,128,512]{2,1,0:T(8,128)}, u32[]{:S(2)}, u32[]{:S(2)}) collective-permute-start(f32[1,128,512]{2,1,0:T(8,128)S(1)} %bitcast_add_fusion.13), channel_id=1, source_target_pairs={{0,32},{32,64},{64,96},{96,128},{128,160},{160,192},{192,224},{224... | collective-permute-start | bytes 786440 | tf_op jit(solution)/shard_map/ppermute | solution.py:105
  147.3 7.9 %collective-permute-start.13 = (f32[1,128,512]{2,1,0:T(8,128)}, f32[1,128,512]{2,1,0:T(8,128)}, u32[]{:S(2)}, u32[]{:S(2)}) collective-permute-start(f32[1,128,512]{2,1,0:T(8,128)} %bitcast_add_fusion.5), channel_id=1, source_target_pairs={{0,224},{32,0},{64,32},{96,64},{128,96},{160,128},{192,160},{224,1... | collective-permute-start | bytes 786440 | tf_op jit(solution)/shard_map/ppermute | solution.py:106
  153.7 7.8 %collective-permute-start.6 = (f32[1,128,512]{2,1,0:T(8,128)S(1)}, f32[1,128,512]{2,1,0:T(8,128)}, u32[]{:S(2)}, u32[]{:S(2)}) collective-permute-start(f32[1,128,512]{2,1,0:T(8,128)S(1)} %bitcast_add_fusion.12), channel_id=1, source_target_pairs={{0,32},{32,64},{64,96},{96,128},{128,160},{160,192},{192,224},{224... | collective-permute-start | bytes 786440 | tf_op jit(solution)/shard_map/ppermute | solution.py:105
  156.9 8.3 %collective-permute-start.14 = (f32[1,128,512]{2,1,0:T(8,128)}, f32[1,128,512]{2,1,0:T(8,128)}, u32[]{:S(2)}, u32[]{:S(2)}) collective-permute-start(f32[1,128,512]{2,1,0:T(8,128)} %bitcast_add_fusion.4), channel_id=1, source_target_pairs={{0,224},{32,0},{64,32},{96,64},{128,96},{160,128},{192,160},{224,1... | collective-permute-start | bytes 786440 | tf_op jit(solution)/shard_map/ppermute | solution.py:106
  163.2 7.9 %collective-permute-start.7 = (f32[1,128,512]{2,1,0:T(8,128)}, f32[1,128,512]{2,1,0:T(8,128)}, u32[]{:S(2)}, u32[]{:S(2)}) collective-permute-start(f32[1,128,512]{2,1,0:T(8,128)} %bitcast_add_fusion.11), channel_id=1, source_target_pairs={{0,32},{32,64},{64,96},{96,128},{128,160},{160,192},{192,224},{224... | collective-permute-start | bytes 786440 | tf_op jit(solution)/shard_map/ppermute | solution.py:105
  166.2 7.7 %collective-permute-start.15 = (f32[1,128,512]{2,1,0:T(8,128)S(1)}, f32[1,128,512]{2,1,0:T(8,128)}, u32[]{:S(2)}, u32[]{:S(2)}) collective-permute-start(f32[1,128,512]{2,1,0:T(8,128)S(1)} %bitcast_add_fusion.3), channel_id=1, source_target_pairs={{0,224},{32,0},{64,32},{96,64},{128,96},{160,128},{192,160},{224,1... | collective-permute-start | bytes 786440 | tf_op jit(solution)/shard_map/ppermute | solution.py:106
  172.9 7.9 %collective-permute-start.8 = (f32[1,128,512]{2,1,0:T(8,128)}, f32[1,128,512]{2,1,0:T(8,128)}, u32[]{:S(2)}, u32[]{:S(2)}) collective-permute-start(f32[1,128,512]{2,1,0:T(8,128)} %bitcast_add_fusion.10), channel_id=1, source_target_pairs={{0,32},{32,64},{64,96},{96,128},{128,160},{160,192},{192,224},{224... | collective-permute-start | bytes 786440 | tf_op jit(solution)/shard_map/ppermute | solution.py:105
  (18 other events, 65.5 us)
